TPU v7x, 256 devices: a whole 4x4x8 slice. The times are simulated.
256 devices in a mesh: shard: 8 (over z), tensor: 4 (over y), section: 8 (over x, core).
Axes of the slice: x: 4, y: 4, z: 8, core: 2. Of those that a mesh axis runs over, the one named last changes fastest.
Arguments:
- emb_grad: float32 [960, 32000], P(('tensor', 'section'), 'shard'), may hold values from -60 to 60
- mlp_grad: float32 [3, 960, 2560], P(None, ('tensor', 'section'), 'shard'), may hold values from -60 to 60
- emb_basis: float32 [960, 256], P(('tensor', 'section')), may hold values from -0.1875 to 0.1875
- mlp_basis: float32 [3, 960, 256], P(None, ('tensor', 'section')), may hold values from -0.1875 to 0.1875
- emb_first: float32 [256, 32000], P(('tensor', 'section'), 'shard'), may hold values from -6 to 6
- emb_second: float32 [256, 32000], P(('tensor', 'section'), 'shard'), may hold values from 0.002 to 0.05
- mlp_first: float32 [256, 3, 2560], P(('tensor', 'section'), None, 'shard'), may hold values from -6 to 6
- mlp_second: float32 [256, 3, 2560], P(('tensor', 'section'), None, 'shard'), may hold values from 0.002 to 0.05
Outputs:
- emb_update: float32 [960, 32000], P(('tensor', 'section'), 'shard')
- mlp_update: float32 [3, 960, 2560], P(None, ('tensor', 'section'), 'shard')
- emb_first_new: float32 [256, 32000], P(('tensor', 'section'), 'shard')
- emb_second_new: float32 [256, 32000], P(('tensor', 'section'), 'shard')
- mlp_first_new: float32 [256, 3, 2560], P(('tensor', 'section'), None, 'shard')
- mlp_second_new: float32 [256, 3, 2560], P(('tensor', 'section'), None, 'shard')
- emb_basis_new: float32 [960, 256], P(('tensor', 'section'))
- mlp_basis_new: float32 [3, 960, 256], P(None, ('tensor', 'section'))
All inputs are finite; a program needn't handle non-finite values.
Results may differ from a plain program's by a relative error of at most 0.0003.
Values sent between devices are 32-bit elements; how exact they have to be, the bound alone decides.
No kernel may reach another device: no remote copies, remote signals or barrier semaphores. Data moves between devices by JAX's collectives and lax.ppermute only.
A program may use at most 64 MiB of HBM per device.

v0:
```python
import jax
import jax.numpy as jnp
from jax import lax
from jax.sharding import PartitionSpec as P

NS_STEPS = 3


coef_a = 3.4445
coef_b = -4.775
coef_c = 2.0315
bias_one = 1.0 - 0.9**10
bias_two = 1.0 - 0.999**10
adam_eps = 1e-08
norm_eps = 1e-07
highest = lax.Precision.HIGHEST


def adam_moments(first, second, projected):
    first_new = 0.9 * first + 0.1 * projected
    second_new = 0.999 * second + 0.001 * projected * projected
    direction = first_new / bias_one / (jnp.sqrt(second_new / bias_two) + adam_eps)
    return (first_new, second_new, direction)


def polish(current, gram_term):
    polynomial = coef_b * gram_term + coef_c * jnp.einsum(
        "...rs,...st->...rt", gram_term, gram_term, precision=highest
    )
    return coef_a * current + jnp.einsum(
        "...dr,...rs->...ds", current, polynomial, precision=highest
    )


def gram_sums(emb_iterate, mlp_iterate):
    emb_gram = jnp.einsum("dr,ds->rs", emb_iterate, emb_iterate, precision=highest)
    mlp_gram = jnp.einsum("kdr,kds->krs", mlp_iterate, mlp_iterate, precision=highest)
    return lax.psum((emb_gram, mlp_gram), ("tensor", "section"))


def local_terms(emb_grad, mlp_grad, emb_basis, mlp_basis):
    emb_term = jnp.einsum("dr,dv->rv", emb_basis, emb_grad, precision=highest)
    mlp_term = jnp.einsum("kdr,kdf->rkf", mlp_basis, mlp_grad, precision=highest)
    return (emb_term, mlp_term)


def project_back(emb_basis, mlp_basis, emb_total, mlp_total, emb_piece, mlp_piece):
    emb_total = jnp.dot(emb_basis, emb_piece, precision=highest)
    mlp_total = jnp.einsum("kdr,rkf->kdf", mlp_basis, mlp_piece, precision=highest)
    return (emb_total, mlp_total)


def local(emb_grad, mlp_grad, emb_basis, mlp_basis, emb_first, emb_second, mlp_first, mlp_second):
    emb_term, mlp_term = local_terms(emb_grad, mlp_grad, emb_basis, mlp_basis)
    emb_zero = jnp.zeros(emb_grad.shape, jnp.float32)
    mlp_zero = jnp.zeros(mlp_grad.shape, jnp.float32)
    emb_share, mlp_share = (
        lax.psum_scatter(emb_term, ("tensor", "section"), scatter_dimension=0, tiled=True),
        lax.psum_scatter(mlp_term, ("tensor", "section"), scatter_dimension=0, tiled=True),
    )
    emb_first_new, emb_second_new, emb_direction = adam_moments(emb_first, emb_second, emb_share)
    mlp_first_new, mlp_second_new, mlp_direction = adam_moments(mlp_first, mlp_second, mlp_share)
    emb_total = emb_zero
    mlp_total = mlp_zero
    emb_piece = lax.all_gather(emb_direction, ("tensor", "section"), axis=0, tiled=True)
    emb_projected = lax.all_gather(emb_share, ("tensor", "section"), axis=0, tiled=True)
    mlp_piece = lax.all_gather(mlp_direction, ("tensor", "section"), axis=0, tiled=True)
    mlp_projected = lax.all_gather(mlp_share, ("tensor", "section"), axis=0, tiled=True)
    emb_total, mlp_total = project_back(
        emb_basis, mlp_basis, emb_total, mlp_total, emb_piece, mlp_piece
    )
    emb_found_block = jnp.einsum("dv,rv->dr", emb_grad, emb_projected, precision=highest)
    mlp_found_block = jnp.einsum("kdf,rkf->kdr", mlp_grad, mlp_projected, precision=highest)
    emb_part, mlp_part = lax.psum((emb_found_block, mlp_found_block), "shard")
    emb_squares, mlp_squares = lax.psum(
        (jnp.sum(emb_part * emb_part), jnp.sum(mlp_part * mlp_part, axis=(1, 2))),
        ("tensor", "section"),
    )
    emb_iterate = emb_part / (jnp.sqrt(emb_squares) + norm_eps)
    mlp_iterate = mlp_part / (jnp.sqrt(mlp_squares) + norm_eps)[:, None, None]
    emb_gram, mlp_gram = gram_sums(emb_iterate, mlp_iterate)
    for sweep_index in range(NS_STEPS):
        if sweep_index > 0:
            emb_gram, mlp_gram = gram_sums(emb_iterate, mlp_iterate)
        emb_iterate = polish(emb_iterate, emb_gram)
        mlp_iterate = polish(mlp_iterate, mlp_gram)
    return (
        emb_total,
        mlp_total,
        emb_first_new,
        emb_second_new,
        mlp_first_new,
        mlp_second_new,
        emb_iterate,
        mlp_iterate,
    )


def solution(mesh):
    placed = (
        P(("tensor", "section"), "shard"),
        P(None, ("tensor", "section"), "shard"),
        P(("tensor", "section"), None),
        P(None, ("tensor", "section"), None),
        P(("tensor", "section"), "shard"),
        P(("tensor", "section"), "shard"),
        P(("tensor", "section"), None, "shard"),
        P(("tensor", "section"), None, "shard"),
    )
    return jax.shard_map(
        local,
        mesh=mesh,
        in_specs=placed,
        out_specs=(
            P(("tensor", "section"), "shard"),
            P(None, ("tensor", "section"), "shard"),
            P(("tensor", "section"), "shard"),
            P(("tensor", "section"), "shard"),
            P(("tensor", "section"), None, "shard"),
            P(("tensor", "section"), None, "shard"),
            P(("tensor", "section"), None),
            P(None, ("tensor", "section"), None),
        ),
        check_vma=False,
    )
```

profile of v0, /device:TPU:1, one launch (start us, length us, event | category | flops | bytes accessed | tf_op | source)
XLA Modules:
  0.0 871.1 jit_solution(18195244616906129334)
XLA Ops:
  7.2 2.0 convolution_bitcast_fusion.1
  9.3 1.5 copy.31
  10.8 0.0 reduce-scatter.2.cloned.1.call-start
  10.9 5.0 fusion.12
  16.0 0.0 all-reduce.11.cloned.1.call-start
  16.0 0.6 copy-done.13
  16.6 0.6 dynamic-slice
  17.9 113.6 %all-reduce.13.cloned.1.call-done = f32[256,3,320]{2,1,0:T(4,128)} async-done(((f32[256,3,320]{2,1,0:T(4,128)}), f32[256,3,320]{2,1,0:T(4,128)}) %all-reduce.13.cloned.1.call-update) | async-done | bytes 983056
  131.5 0.8 constant_dynamic-slice_fusion
  132.3 0.7 add_divide_fusion.1
  133.0 26.2 %all_gather.15 = f32[256,3,320]{2,0,1:T(8,128)S(1)} all-gather(f32[8,3,320]{2,0,1:T(8,128)S(1)} %get-tuple-element.35), channel_id=1, replica_groups=mesh['shard'=8,'tensor'=4,'section'=8] {'tensor','section'}, dimensions={0}, use_global_device_ids=true | all-gather | bytes 1013760 | tf_op jit(solution)/shard_map/all_gather | solution.py:68
  159.2 1.9 convolution_bitcast_fusion.3
  161.1 62.5 %reduce-scatter.2.cloned.1.call-done = f32[8,4000]{1,0:T(8,128)} async-done(((f32[256,4000]{1,0:T(8,128)}), f32[8,4000]{1,0:T(8,128)}) %reduce-scatter.2.cloned.1.call-update) | async-done | bytes 128016 | tf_op jit(solution)/shard_map/reduce_scatter | solution.py:58
  223.7 71.3 %all-reduce.11.cloned.1.call-done = f32[3,30,256]{2,1,0:T(8,128)} async-done(((f32[3,30,256]{2,1,0:T(8,128)}), f32[3,30,256]{2,1,0:T(8,128)}) %all-reduce.11.cloned.1.call-update) | async-done | bytes 92176 | tf_op jit(solution)/shard_map/psum | solution.py:74
  295.0 1.0 multiply_reduce_fusion
  296.0 56.0 %all-gather.5.cloned.1.call-done = f32[256,4000]{1,0:T(8,128)} async-done(((f32[8,4000]{1,0:T(8,128)}), f32[256,4000]{1,0:T(8,128)}) %all-gather.5.cloned.1.call-update) | async-done | bytes 4096016 | tf_op jit(solution)/shard_map/all_gather | solution.py:66
  352.0 5.9 convolution_bitcast_fusion.4
  357.8 23.2 %psum.70 = f32[30,256]{1,0:T(8,128)S(1)} all-reduce(f32[30,256]{1,0:T(8,128)S(1)} %convolution_bitcast_fusion.4), channel_id=1, replica_groups=mesh['shard'=8,'tensor'=4,'section'=8] {'shard'}, use_global_device_ids=true, to_apply=%region_2.0 | all-reduce | flops 7680 | bytes 61440 | tf_op jit(solution)/shard_map/psum | solution.py:74
  381.0 0.6 multiply_reduce_fusion.1
  381.6 70.0 %all-reduce.1 = (f32[]{:T(128)}, f32[3]{0:T(128)S(1)}) all-reduce(f32[]{:T(128)} %multiply_reduce_fusion.1, f32[3]{0:T(128)S(1)} %multiply_reduce_fusion), channel_id=1, replica_groups=mesh['shard'=8,'tensor'=4,'section'=8] {'tensor','section'}, use_global_device_ids=true, to_apply=%region_4.0 | all-reduce | flops 4 | bytes 32 | tf_op jit(solution)/shard_map/psum | solution.py:75
  452.3 1.1 fusion.9
  453.4 1.9 fusion.8
  455.3 0.2 all-reduce.17.cloned.1.call-start
  455.6 109.0 %all-reduce.19.cloned.1.call-done = (f32[256,256]{1,0:T(8,128)}, f32[3,256,256]{2,1,0:T(8,128)}) async-done(((f32[256,256]{1,0:T(8,128)}, f32[3,256,256]{2,1,0:T(8,128)}), (f32[256,256]{1,0:T(8,128)}, f32[3,256,256]{2,1,0:T(8,128)})) %all-reduce.19.cloned.1.call-update) | async-done | bytes 1048592 | tf_op jit(solution)/shard_map/psum | solution.py:38
  564.6 2.7 fusion.2
  567.3 0.6 convolution_add_fusion.2
  567.9 1.8 fusion.15
  569.6 0.4 fusion.5
  570.0 0.2 convolution_add_fusion.5
  570.3 1.1 fusion.13
  571.4 0.0 all-gather.3.cloned.1.call-start
  571.5 0.8 add_divide_fusion
  572.3 26.7 %all_gather.13 = f32[256,3,320]{2,0,1:T(8,128)S(1)} all-gather(f32[8,3,320]{2,0,1:T(8,128)S(1)} %get-tuple-element.32), channel_id=1, replica_groups=mesh['shard'=8,'tensor'=4,'section'=8] {'tensor','section'}, dimensions={0}, use_global_device_ids=true | all-gather | bytes 1013760 | tf_op jit(solution)/shard_map/all_gather | solution.py:67
  599.0 88.5 %all-reduce.17.cloned.1.call-done = (f32[256,256]{1,0:T(8,128)}, f32[3,256,256]{2,1,0:T(8,128)}) async-done(((f32[256,256]{1,0:T(8,128)}, f32[3,256,256]{2,1,0:T(8,128)}), (f32[256,256]{1,0:T(8,128)}, f32[3,256,256]{2,1,0:T(8,128)})) %all-reduce.17.cloned.1.call-update) | async-done | bytes 1048592 | tf_op jit(solution)/shard_map/psum | solution.py:38
  687.6 1.6 fusion.4
  689.1 0.2 convolution_add_fusion.4
  689.4 1.1 fusion.14
  690.5 0.9 fusion.1
  691.5 0.6 convolution_add_fusion.1
  692.0 1.8 fusion.16
  693.8 1.4 convolution_bitcast_fusion.2
  695.3 46.2 %all-gather.3.cloned.1.call-done = f32[256,4000]{1,0:T(8,128)} async-done(((f32[8,4000]{1,0:T(8,128)}), f32[256,4000]{1,0:T(8,128)}) %all-gather.3.cloned.1.call-update) | async-done | bytes 4096016 | tf_op jit(solution)/shard_map/all_gather | solution.py:65
  741.4 5.5 convolution_bitcast_fusion
  747.0 112.2 %all-reduce.15.cloned.1.call-done = (f32[256,256]{1,0:T(8,128)}, f32[3,256,256]{2,1,0:T(8,128)}) async-done(((f32[256,256]{1,0:T(8,128)}, f32[3,256,256]{2,1,0:T(8,128)}), (f32[256,256]{1,0:T(8,128)}, f32[3,256,256]{2,1,0:T(8,128)})) %all-reduce.15.cloned.1.call-update) | async-done | bytes 1048592 | tf_op jit(solution)/shard_map/psum | solution.py:38
  859.2 2.6 fusion
  861.8 1.2 convolution_add_fusion
  863.0 0.4 fusion.3
  863.4 0.9 convolution_add_fusion.3
  (40 shorter events, 0.4 us)
Async XLA Ops:
  7.2 3.7 copy-start
  7.2 124.3 %all-reduce.13.cloned.1.call-start = ((), (), s32[]{:S(2)}) async-start(), calls=%async_computation.5 | async-start | bytes 3145728
  9.2 1.6 copy-start.8
  10.8 212.8 %reduce-scatter.2.cloned.1.call-start = ((), (), s32[]{:S(2)}) async-start(), calls=%async_computation.1 | async-start | bytes 4325376 | tf_op jit(solution)/shard_map/reduce_scatter | solution.py:58
  15.9 0.7 copy-start.13
  15.9 116.3 %copy-start.11 = (f32[8,3,320]{2,0,1:T(8,128)S(1)}, f32[8,3,320]{2,0,1:T(8,128)}, u32[]{:S(2)}) copy-start(f32[8,3,320]{2,0,1:T(8,128)} %param.14) | copy-start | bytes 92164
  15.9 116.4 %copy-start.12 = (f32[8,3,320]{2,0,1:T(8,128)S(1)}, f32[8,3,320]{2,0,1:T(8,128)}, u32[]{:S(2)}) copy-start(f32[8,3,320]{2,0,1:T(8,128)} %param.15) | copy-start | bytes 92164
  16.0 143.2 %copy-start.5 = (f32[3,30,320]{2,1,0:T(8,128)S(1)}, f32[3,30,320]{2,1,0:T(8,128)}, u32[]{:S(2)}) copy-start(f32[3,30,320]{2,1,0:T(8,128)} %param.9) | copy-start | bytes 345604
  16.0 279.0 %all-reduce.11.cloned.1.call-start = ((), (), s32[]{:S(2)}) async-start(), calls=%async_computation.4 | async-start | bytes 196608 | tf_op jit(solution)/shard_map/psum | solution.py:74
  161.1 190.9 %all-gather.5.cloned.1.call-start = ((), (), s32[]{:S(2)}) async-start(), calls=%async_computation.3 | async-start | bytes 4325376 | tf_op jit(solution)/shard_map/all_gather | solution.py:66
  223.6 341.0 %all-reduce.19.cloned.1.call-start = ((), (), s32[]{:S(2)}) async-start(), calls=%async_computation.8 | async-start | bytes 2097152 | tf_op jit(solution)/shard_map/psum | solution.py:38
  296.0 157.4 %copy-start.4 = (f32[3,30,256]{2,1,0:T(8,128)S(1)}, f32[3,30,256]{2,1,0:T(8,128)}, u32[]{:S(2)}) copy-start(f32[3,30,256]{2,1,0:T(8,128)} %all-reduce.11.cloned.1.call-done) | copy-start | bytes 276484
  455.3 232.2 %all-reduce.17.cloned.1.call-start = ((), (), s32[]{:S(2)}) async-start(), calls=%async_computation.7 | async-start | bytes 2097152 | tf_op jit(solution)/shard_map/psum | solution.py:38
  567.3 2.4 copy-start.3
  567.8 3.6 copy-start.6
  567.8 3.6 copy-start.9
  567.9 3.6 copy-start.10
  571.4 170.0 %all-gather.3.cloned.1.call-start = ((), (), s32[]{:S(2)}) async-start(), calls=%async_computation.2 | async-start | bytes 4325376 | tf_op jit(solution)/shard_map/all_gather | solution.py:65
  572.3 286.9 %all-reduce.15.cloned.1.call-start = ((), (), s32[]{:S(2)}) async-start(), calls=%async_computation.6 | async-start | bytes 2097152 | tf_op jit(solution)/shard_map/psum | solution.py:38
  687.6 3.0 copy-start.1
  691.5 2.4 copy-start.7
  859.2 3.8 copy-start.2
Sparse Core Ops, SparseCore 0:
  11.3 120.1 all-reduce.12
  135.4 88.1 reduce-scatter.1
  226.5 68.4 all-reduce.10
  297.4 54.5 all-gather.4
  455.5 109.0 all-reduce.18
  571.5 115.9 all-reduce.16
  690.1 51.2 all-gather.2
  744.7 114.4 all-reduce.14
where the time goes:
time: 872 us; the launch traced here: 871 us
  waiting for transfers between devices  659 us (76%)
  blocking collectives  146 us (17%)
  matrix products  42.7 us (5%)
  between operations  15.7 us (2%)
    psum x3, waiting for transfers between devices, gram_sums(): return lax.psum((emb_gram, mlp_gram), ('tensor', 'section'))  310 us
    unnamed x9, waiting for transfers between devices  114 us
    psum x1, waiting for transfers between devices, local(): emb_part, mlp_part = lax.psum((emb_found_block, mlp_found_block), 'shard')  71.3 us
    psum x1, blocking collectives, local(): lax.psum((jnp.sum(emb_part * emb_part), jnp.sum(mlp_part * mlp_part, axis...  70 us
    reduce_scatter x1, waiting for transfers between devices, local(): lax.psum_scatter(emb_term, ('tensor', 'section'), scatter_dimension=0, ti...  62.5 us
    all_gather x1, waiting for transfers between devices, local(): lax.all_gather(emb_share, ('tensor', 'section'), axis=0, tiled=True)  56 us
    all_gather x1, waiting for transfers between devices, local(): lax.all_gather(emb_direction, ('tensor', 'section'), axis=0, tiled=True)  46.2 us
    all_gather x1, blocking collectives, local(): lax.all_gather(mlp_direction, ('tensor', 'section'), axis=0, tiled=True)  26.7 us
  transfers between devices with their start and end apart: 8, of which 8 were waited for; matrix products, arithmetic and copies ran while one was open for 3% of the time, Pallas kernels for 0%

commit v1 on v0

--- a/solution.py
+++ b/solution.py
@@ -23,12 +23,31 @@
     return (first_new, second_new, direction)
 
 
-def polish(current, gram_term):
-    polynomial = coef_b * gram_term + coef_c * jnp.einsum(
+def newton_schulz(target, gram):
+    squares = jnp.trace(gram, axis1=-2, axis2=-1)
+    scale = 1.0 / (jnp.sqrt(squares) + norm_eps)
+    gram_term = gram * (scale * scale)[..., None, None]
+    eye = jnp.eye(gram.shape[-1], dtype=gram.dtype)
+    total = None
+    for sweep_index in range(NS_STEPS):
+        factor = coef_a * eye + polish_poly(gram_term)
+        if sweep_index + 1 < NS_STEPS:
+            gram_term = jnp.einsum(
+                "...rs,...st->...rt",
+                factor,
+                jnp.einsum("...rs,...st->...rt", gram_term, factor, precision=highest),
+                precision=highest,
+            )
+        total = factor if total is None else jnp.einsum(
+            "...rs,...st->...rt", total, factor, precision=highest
+        )
+    current = target * scale[..., None, None]
+    return jnp.einsum("...dr,...rs->...ds", current, total, precision=highest)
+
+
+def polish_poly(gram_term):
+    return coef_b * gram_term + coef_c * jnp.einsum(
         "...rs,...st->...rt", gram_term, gram_term, precision=highest
-    )
-    return coef_a * current + jnp.einsum(
-        "...dr,...rs->...ds", current, polynomial, precision=highest
     )
 
 
@@ -72,18 +91,9 @@
     emb_found_block = jnp.einsum("dv,rv->dr", emb_grad, emb_projected, precision=highest)
     mlp_found_block = jnp.einsum("kdf,rkf->kdr", mlp_grad, mlp_projected, precision=highest)
     emb_part, mlp_part = lax.psum((emb_found_block, mlp_found_block), "shard")
-    emb_squares, mlp_squares = lax.psum(
-        (jnp.sum(emb_part * emb_part), jnp.sum(mlp_part * mlp_part, axis=(1, 2))),
-        ("tensor", "section"),
-    )
-    emb_iterate = emb_part / (jnp.sqrt(emb_squares) + norm_eps)
-    mlp_iterate = mlp_part / (jnp.sqrt(mlp_squares) + norm_eps)[:, None, None]
-    emb_gram, mlp_gram = gram_sums(emb_iterate, mlp_iterate)
-    for sweep_index in range(NS_STEPS):
-        if sweep_index > 0:
-            emb_gram, mlp_gram = gram_sums(emb_iterate, mlp_iterate)
-        emb_iterate = polish(emb_iterate, emb_gram)
-        mlp_iterate = polish(mlp_iterate, mlp_gram)
+    emb_gram, mlp_gram = gram_sums(emb_part, mlp_part)
+    emb_iterate = newton_schulz(emb_part, emb_gram)
+    mlp_iterate = newton_schulz(mlp_part, mlp_gram)
     return (
         emb_total,
         mlp_total,

time: 872 us -> 549 us (0.63)
  waiting for transfers between devices: 659 us -> 407 us
  blocking collectives: 146 us -> 76.7 us
    psum x3 -> x1, waiting for transfers between devices: 310 us -> 112 us  [gram_sums(): return lax.psum((emb_gram, mlp_gram), ('tensor', 'section'))]
    psum x1 -> x0, blocking collectives: 70 us -> none  [local(): lax.psum((jnp.sum(emb_part * emb_part), jnp.sum(mlp_part * mlp_part, axis...]
    psum x1, waiting for transfers between devices: 71.3 us -> 42.7 us  [local(): emb_part, mlp_part = lax.psum((emb_found_block, mlp_found_block), 'shard')]
    all_gather x1, waiting for transfers between devices: 46.2 us -> 21.4 us  [local(): lax.all_gather(emb_direction, ('tensor', 'section'), axis=0, tiled=True)]
    unnamed x9 -> x7, waiting for transfers between devices: 114 us -> 114 us
  transfers between devices with their start and end apart: 8 -> 6, of which waited for: 8 -> 6; matrix products, arithmetic and copies ran while one was open for 3% -> 5% of each run, Pallas kernels for 0% -> 0%
where the time goes in v1:
time: 549 us
  waiting for transfers between devices  407 us (74%)
  blocking collectives  76.7 us (14%)
  matrix products  41.5 us (8%)
  between operations  15.8 us (3%)
    unnamed x7, waiting for transfers between devices  114 us
    psum x1, waiting for transfers between devices, gram_sums(): return lax.psum((emb_gram, mlp_gram), ('tensor', 'section'))  112 us
    reduce_scatter x1, waiting for transfers between devices, local(): lax.psum_scatter(emb_term, ('tensor', 'section'), scatter_dimension=0, ti...  62.4 us
    all_gather x1, waiting for transfers between devices, local(): lax.all_gather(emb_share, ('tensor', 'section'), axis=0, tiled=True)  54.2 us
    psum x1, waiting for transfers between devices, local(): emb_part, mlp_part = lax.psum((emb_found_block, mlp_found_block), 'shard')  42.7 us
    all_gather x1, blocking collectives, local(): lax.all_gather(mlp_direction, ('tensor', 'section'), axis=0, tiled=True)  26.8 us
    all_gather x1, blocking collectives, local(): lax.all_gather(mlp_share, ('tensor', 'section'), axis=0, tiled=True)  26.2 us
    psum x1, blocking collectives, local(): emb_part, mlp_part = lax.psum((emb_found_block, mlp_found_block), 'shard')  23.7 us
  transfers between devices with their start and end apart: 6, of which 6 were waited for; matrix products, arithmetic and copies ran while one was open for 5% of the time, Pallas kernels for 0%

profile of v1, /device:TPU:1, one launch (start us, length us, event | category | flops | bytes accessed | tf_op | source)
XLA Modules:
  0.0 548.8 jit_solution(6398069834945036047)
XLA Ops:
  7.2 2.0 convolution_bitcast_fusion.1
  9.3 1.5 copy.31
  10.8 0.0 reduce-scatter.2.cloned.1.call-start
  10.9 5.1 fusion.34
  16.0 0.0 all-reduce.6.cloned.1.call-start
  16.1 0.6 copy-done.11
  16.6 0.6 dynamic-slice
  17.9 113.6 %all-reduce.8.cloned.1.call-done = f32[256,3,320]{2,1,0:T(4,128)} async-done(((f32[256,3,320]{2,1,0:T(4,128)}), f32[256,3,320]{2,1,0:T(4,128)}) %all-reduce.8.cloned.1.call-update) | async-done | bytes 983056
  131.5 0.8 constant_dynamic-slice_fusion
  132.3 0.7 add_divide_fusion.1
  133.0 26.2 %all_gather.15 = f32[256,3,320]{2,0,1:T(8,128)S(1)} all-gather(f32[8,3,320]{2,0,1:T(8,128)S(1)} %get-tuple-element.31), channel_id=1, replica_groups=mesh['shard'=8,'tensor'=4,'section'=8] {'tensor','section'}, dimensions={0}, use_global_device_ids=true | all-gather | bytes 1013760 | tf_op jit(solution)/shard_map/all_gather | solution.py:87
  159.2 1.8 convolution_bitcast_fusion.3
  161.2 62.4 %reduce-scatter.2.cloned.1.call-done = f32[8,4000]{1,0:T(8,128)} async-done(((f32[256,4000]{1,0:T(8,128)}), f32[8,4000]{1,0:T(8,128)}) %reduce-scatter.2.cloned.1.call-update) | async-done | bytes 128016 | tf_op jit(solution)/shard_map/reduce_scatter | solution.py:77
  223.7 1.7 add_divide_fusion
  225.4 0.0 all-reduce.10.cloned.1.call-start
  225.5 26.8 %all_gather.13 = f32[256,3,320]{2,0,1:T(8,128)S(1)} all-gather(f32[8,3,320]{2,0,1:T(8,128)S(1)} %get-tuple-element.28), channel_id=1, replica_groups=mesh['shard'=8,'tensor'=4,'section'=8] {'tensor','section'}, dimensions={0}, use_global_device_ids=true | all-gather | bytes 1013760 | tf_op jit(solution)/shard_map/all_gather | solution.py:86
  252.3 42.7 %all-reduce.6.cloned.1.call-done = f32[3,30,256]{2,1,0:T(8,128)} async-done(((f32[3,30,256]{2,1,0:T(8,128)}), f32[3,30,256]{2,1,0:T(8,128)}) %all-reduce.6.cloned.1.call-update) | async-done | bytes 92176 | tf_op jit(solution)/shard_map/psum | solution.py:93
  295.0 2.8 fusion.41
  297.8 54.2 %all-gather.5.cloned.1.call-done = f32[256,4000]{1,0:T(8,128)} async-done(((f32[8,4000]{1,0:T(8,128)}), f32[256,4000]{1,0:T(8,128)}) %all-gather.5.cloned.1.call-update) | async-done | bytes 4096016 | tf_op jit(solution)/shard_map/all_gather | solution.py:85
  352.0 5.9 %convolution_bitcast_fusion.4 = f32[30,256]{1,0:T(8,128)S(1)} fusion(f32[256,4000]{1,0:T(8,128)} %all-gather.5.cloned.1.call-done, f32[30,4000]{1,0:T(8,128)S(1)} %copy-done), kind=kOutput, calls=%fused_computation.22 | convolution fusion | flops 368640000 | bytes 4606720 | tf_op jit(solution)/shard_map/dv,rv->dr/dot_general | solution.py:91
  357.9 23.7 %psum.28 = f32[30,256]{1,0:T(8,128)S(1)} all-reduce(f32[30,256]{1,0:T(8,128)S(1)} %convolution_bitcast_fusion.4), channel_id=1, replica_groups=mesh['shard'=8,'tensor'=4,'section'=8] {'shard'}, use_global_device_ids=true, to_apply=%region_2.0 | all-reduce | flops 7680 | bytes 61440 | tf_op jit(solution)/shard_map/psum | solution.py:93
  381.5 1.1 fusion.35
  382.7 1.4 convolution_bitcast_fusion.2
  384.1 21.4 %all-gather.3.cloned.1.call-done = f32[256,4000]{1,0:T(8,128)} async-done(((f32[8,4000]{1,0:T(8,128)}), f32[256,4000]{1,0:T(8,128)}) %all-gather.3.cloned.1.call-update) | async-done | bytes 4096016 | tf_op jit(solution)/shard_map/all_gather | solution.py:84
  405.5 5.5 %convolution_bitcast_fusion = f32[30,4000]{1,0:T(8,128)} fusion(f32[256,4000]{1,0:T(8,128)} %all-gather.3.cloned.1.call-done, f32[30,256]{1,0:T(8,128)S(1)} %copy-done.6), kind=kOutput, calls=%fused_computation | convolution fusion | flops 368640000 | bytes 4606720 | tf_op jit(solution)/shard_map/dot_general | solution.py:67
  411.0 112.1 %all-reduce.10.cloned.1.call-done = (f32[256,256]{1,0:T(8,128)}, f32[3,256,256]{2,1,0:T(8,128)}) async-done(((f32[256,256]{1,0:T(8,128)}, f32[3,256,256]{2,1,0:T(8,128)}), (f32[256,256]{1,0:T(8,128)}, f32[3,256,256]{2,1,0:T(8,128)})) %all-reduce.10.cloned.1.call-update) | async-done | bytes 1048592 | tf_op jit(solution)/shard_map/psum | solution.py:57
  523.2 1.4 select_reduce_fusion
  524.6 2.8 fusion.5
  527.4 0.9 fusion.13
  528.3 0.9 fusion.42
  529.2 0.9 fusion.3
  530.1 0.9 fusion.44
  531.1 0.9 fusion.43
  532.0 0.6 select_reduce_fusion.1
  533.4 0.4 fusion.9
  533.8 0.4 fusion.19
  534.2 0.4 fusion.36
  534.6 0.4 fusion.10
  534.9 0.4 fusion.38
  535.3 0.4 fusion.37
  535.7 1.1 fusion.45
  536.9 0.9 fusion.1
  537.8 0.4 fusion.39
  538.2 0.4 fusion.11
  538.6 0.4 fusion.40
  539.0 0.9 fusion.28
  539.8 0.9 fusion.46
  540.7 1.2 fusion.24
  (35 shorter events, 0.4 us)
Async XLA Ops:
  7.2 3.7 copy-start
  7.2 124.3 %all-reduce.8.cloned.1.call-start = ((), (), s32[]{:S(2)}) async-start(), calls=%async_computation.5 | async-start | bytes 3145728
  9.2 1.6 copy-start.6
  10.8 212.8 %reduce-scatter.2.cloned.1.call-start = ((), (), s32[]{:S(2)}) async-start(), calls=%async_computation.1 | async-start | bytes 4325376 | tf_op jit(solution)/shard_map/reduce_scatter | solution.py:77
  16.0 0.7 copy-start.11
  16.0 116.3 %copy-start.9 = (f32[8,3,320]{2,0,1:T(8,128)S(1)}, f32[8,3,320]{2,0,1:T(8,128)}, u32[]{:S(2)}) copy-start(f32[8,3,320]{2,0,1:T(8,128)} %param.14) | copy-start | bytes 92164
  16.0 116.3 %copy-start.10 = (f32[8,3,320]{2,0,1:T(8,128)S(1)}, f32[8,3,320]{2,0,1:T(8,128)}, u32[]{:S(2)}) copy-start(f32[8,3,320]{2,0,1:T(8,128)} %param.15) | copy-start | bytes 92164
  16.0 143.2 %copy-start.4 = (f32[3,30,320]{2,1,0:T(8,128)S(1)}, f32[3,30,320]{2,1,0:T(8,128)}, u32[]{:S(2)}) copy-start(f32[3,30,320]{2,1,0:T(8,128)} %param.9) | copy-start | bytes 345604
  16.0 279.0 %all-reduce.6.cloned.1.call-start = ((), (), s32[]{:S(2)}) async-start(), calls=%async_computation.4 | async-start | bytes 196608 | tf_op jit(solution)/shard_map/psum | solution.py:93
  132.3 91.4 %copy-start.7 = (f32[8,4000]{1,0:T(8,128)S(1)}, f32[8,4000]{1,0:T(8,128)}, u32[]{:S(2)}) copy-start(f32[8,4000]{1,0:T(8,128)} %param.12) | copy-start | bytes 384004
  132.3 91.4 %copy-start.8 = (f32[8,4000]{1,0:T(8,128)S(1)}, f32[8,4000]{1,0:T(8,128)}, u32[]{:S(2)}) copy-start(f32[8,4000]{1,0:T(8,128)} %param.13) | copy-start | bytes 384004
  161.1 190.9 %all-gather.5.cloned.1.call-start = ((), (), s32[]{:S(2)}) async-start(), calls=%async_computation.3 | async-start | bytes 4325376 | tf_op jit(solution)/shard_map/all_gather | solution.py:85
  223.6 181.9 %all-gather.3.cloned.1.call-start = ((), (), s32[]{:S(2)}) async-start(), calls=%async_computation.2 | async-start | bytes 4325376 | tf_op jit(solution)/shard_map/all_gather | solution.py:84
  225.4 297.8 %all-reduce.10.cloned.1.call-start = ((), (), s32[]{:S(2)}) async-start(), calls=%async_computation.6 | async-start | bytes 2097152 | tf_op jit(solution)/shard_map/psum | solution.py:57
  297.8 84.9 %copy-start.5 = (f32[3,30,256]{2,1,0:T(8,128)S(1)}, f32[3,30,256]{2,1,0:T(8,128)}, u32[]{:S(2)}) copy-start(f32[3,30,256]{2,1,0:T(8,128)} %param.11) | copy-start | bytes 276484
  523.2 4.2 copy-start.1
  531.1 1.0 copy-start.2
  538.6 2.2 copy-start.3
Sparse Core Ops, SparseCore 0:
  11.3 120.1 all-reduce.7
  135.4 88.1 reduce-scatter.1
  226.5 68.4 all-reduce.5
  297.4 54.5 all-gather.4
  355.0 50.4 all-gather.2
  408.6 114.5 all-reduce.9

commit v2 on v1

v2 whole, which is shorter than its diff:
```python
import jax
import jax.numpy as jnp
from jax import lax
from jax.sharding import PartitionSpec as P

NS_STEPS = 3


coef_a = 3.4445
coef_b = -4.775
coef_c = 2.0315
bias_one = 1.0 - 0.9**10
bias_two = 1.0 - 0.999**10
adam_eps = 1e-08
norm_eps = 1e-07
highest = lax.Precision.HIGHEST
WIDE = ("tensor", "section")


def adam_moments(first, second, projected):
    first_new = 0.9 * first + 0.1 * projected
    second_new = 0.999 * second + 0.001 * projected * projected
    direction = first_new / bias_one / (jnp.sqrt(second_new / bias_two) + adam_eps)
    return (first_new, second_new, direction)


def matmul(x, y):
    return jnp.einsum("...rs,...st->...rt", x, y, precision=highest)


def newton_schulz(target, gram):
    squares = jnp.trace(gram, axis1=-2, axis2=-1)
    scale = 1.0 / (jnp.sqrt(squares) + norm_eps)
    gram_term = gram * (scale * scale)[..., None, None]
    eye = jnp.broadcast_to(jnp.eye(gram.shape[-1], dtype=gram.dtype), gram.shape)

    def sweep(_, carry):
        gram_term, total = carry
        factor = coef_a * eye + coef_b * gram_term + coef_c * matmul(gram_term, gram_term)
        return (matmul(factor, matmul(gram_term, factor)), matmul(total, factor))

    _, total = lax.fori_loop(0, NS_STEPS, sweep, (gram_term, eye))
    current = target * scale[..., None, None]
    return matmul(current, total)


def local(emb_grad, mlp_grad, emb_basis, mlp_basis, emb_first, emb_second, mlp_first, mlp_second):
    mats, rows, cols = mlp_grad.shape
    long_side = emb_grad.shape[1]
    rank = emb_basis.shape[1]
    emb_term = jnp.einsum("dr,dv->rv", emb_basis, emb_grad, precision=highest)
    mlp_term = jnp.einsum("kdr,kdf->rkf", mlp_basis, mlp_grad, precision=highest)
    terms = jnp.concatenate([emb_term, mlp_term.reshape(rank, mats * cols)], axis=1)
    pad = -terms.shape[1] % 512
    terms = jnp.pad(terms, ((0, 0), (0, pad)))
    share = lax.psum_scatter(terms, WIDE, scatter_dimension=0, tiled=True)
    emb_share = share[:, :long_side]
    mlp_share = share[:, long_side : long_side + mats * cols].reshape(-1, mats, cols)
    emb_first_new, emb_second_new, emb_direction = adam_moments(emb_first, emb_second, emb_share)
    mlp_first_new, mlp_second_new, mlp_direction = adam_moments(mlp_first, mlp_second, mlp_share)
    pieces = jnp.concatenate(
        [
            emb_direction,
            mlp_direction.reshape(-1, mats * cols),
            share[:, : long_side + mats * cols],
        ],
        axis=1,
    )
    gathered = lax.all_gather(pieces, WIDE, axis=0, tiled=True)
    width = long_side + mats * cols
    emb_piece = gathered[:, :long_side]
    mlp_piece = gathered[:, long_side:width].reshape(rank, mats, cols)
    emb_projected = gathered[:, width : width + long_side]
    mlp_projected = gathered[:, width + long_side :].reshape(rank, mats, cols)
    emb_total = jnp.dot(emb_basis, emb_piece, precision=highest)
    mlp_total = jnp.einsum("kdr,rkf->kdf", mlp_basis, mlp_piece, precision=highest)
    emb_found = jnp.einsum("dv,rv->dr", emb_grad, emb_projected, precision=highest)
    mlp_found = jnp.einsum("kdf,rkf->dkr", mlp_grad, mlp_projected, precision=highest)
    found = jnp.concatenate([emb_found, mlp_found.reshape(rows, mats * rank)], axis=1)
    found = lax.psum(found, "shard")
    every = lax.all_gather(found, WIDE, axis=0, tiled=True)
    every = every.reshape(-1, mats + 1, rank).transpose(1, 0, 2)
    gram = jnp.einsum("kdr,kds->krs", every, every, precision=highest)
    targets = found.reshape(rows, mats + 1, rank).transpose(1, 0, 2)
    basis_new = newton_schulz(targets, gram)
    return (
        emb_total,
        mlp_total,
        emb_first_new,
        emb_second_new,
        mlp_first_new,
        mlp_second_new,
        basis_new[0],
        basis_new[1:],
    )


def solution(mesh):
    placed = (
        P(WIDE, "shard"),
        P(None, WIDE, "shard"),
        P(WIDE, None),
        P(None, WIDE, None),
        P(WIDE, "shard"),
        P(WIDE, "shard"),
        P(WIDE, None, "shard"),
        P(WIDE, None, "shard"),
    )
    return jax.shard_map(
        local,
        mesh=mesh,
        in_specs=placed,
        out_specs=(
            P(WIDE, "shard"),
            P(None, WIDE, "shard"),
            P(WIDE, "shard"),
            P(WIDE, "shard"),
            P(WIDE, None, "shard"),
            P(WIDE, None, "shard"),
            P(WIDE, None),
            P(None, WIDE, None),
        ),
        check_vma=False,
    )
```

time: 549 us -> 373 us (0.68)
  waiting for transfers between devices: 407 us -> 274 us
  blocking collectives: 76.7 us -> 0 us
  local copies, waits for them, and re-layouts: 3.6 us -> 25.5 us
  matrix products: 41.5 us -> 52 us
    unnamed x7 -> x4, waiting for transfers between devices: 114 us -> 0.07 us
    psum x2 -> x1, waiting for transfers between devices: 155 us -> 66.6 us  [local(): found = lax.psum(found, 'shard')]
    all_gather x2 -> x0, blocking collectives: 53 us -> none  [the longest x1 26.8 us: local(): lax.all_gather(mlp_direction, ('tensor', 'section'), axis=0, tiled=True)]
    all_gather x2, waiting for transfers between devices: 75.5 us -> 113 us  [the longest x1 63.7 us: local(): gathered = lax.all_gather(pieces, WIDE, axis=0, tiled=True)]
    reduce_scatter x1, waiting for transfers between devices: 62.4 us -> 94.5 us  [local(): share = lax.psum_scatter(terms, WIDE, scatter_dimension=0, tiled=True)]
    psum x1 -> x0, blocking collectives: 23.7 us -> none  [local(): emb_part, mlp_part = lax.psum((emb_found_block, mlp_found_block), 'shard')]
    dot_general x27 -> x19, matrix products: 35.6 us -> 46 us  [the longest x13 19.9 us: matmul(): return jnp.einsum('...rs,...st->...rt', x, y, precision=highest)]
    slice x0 -> x6, local copies, waits for them, and re-layouts: none -> 5.99 us  [the longest x2 3.26 us: local(): mlp_projected = gathered[:, width + long_side:].reshape(rank, mats, cols)]
  transfers between devices with their start and end apart: 6 -> 4, of which waited for: 6 -> 4; matrix products, arithmetic and copies ran while one was open for 5% -> 2% of each run, Pallas kernels for 0% -> 0%
where the time goes in v2:
time: 373 us
  waiting for transfers between devices  274 us (73%)
  matrix products  52 us (14%)
  local copies, waits for them, and re-layouts  25.5 us (7%)
  between operations  14 us (4%)
  other arithmetic  6 us (2%)
    reduce_scatter x1, waiting for transfers between devices, local(): share = lax.psum_scatter(terms, WIDE, scatter_dimension=0, tiled=True)  94.5 us
    psum x1, waiting for transfers between devices, local(): found = lax.psum(found, 'shard')  66.6 us
    all_gather x1, waiting for transfers between devices, local(): gathered = lax.all_gather(pieces, WIDE, axis=0, tiled=True)  63.7 us
    all_gather x1, waiting for transfers between devices, local(): every = lax.all_gather(found, WIDE, axis=0, tiled=True)  49.6 us
    dot_general x13, matrix products, matmul(): return jnp.einsum('...rs,...st->...rt', x, y, precision=highest)  19.9 us
    dot_general x1, matrix products, local(): gram = jnp.einsum('kdr,kds->krs', every, every, precision=highest)  10.8 us
  transfers between devices with their start and end apart: 4, of which 4 were waited for; matrix products, arithmetic and copies ran while one was open for 2% of the time, Pallas kernels for 0%

profile of v2, /device:TPU:1, one launch (start us, length us, event | category | flops | bytes accessed | tf_op | source)
XLA Modules:
  0.0 372.7 jit_solution(12584134359558805600)
XLA Ops:
  7.2 2.0 fusion.24
  9.3 4.2 %fusion.23 = f32[256,4000]{0,1:T(8,128)S(1)} fusion(f32[30,256]{1,0:T(8,128)} %param.12, f32[30,4000]{1,0:T(8,128)S(1)} %copy-done), kind=kOutput, calls=%fused_computation.38 | convolution fusion | flops 368640000 | bytes 4606720 | tf_op jit(solution)/shard_map/dr,dv->rv/dot_general | solution.py:51
  13.5 2.6 pad_maximum_fusion
  16.1 5.9 %copy.117 = f32[256,4960]{1,0:T(8,128)} copy(f32[256,4960]{0,1:T(8,128)} %pad_maximum_fusion) | data formatting | bytes 10158080
  22.0 5.4 %pad.4.clone = f32[256,5120]{1,0:T(8,128)} pad(f32[256,4960]{1,0:T(8,128)} %copy.117, f32[]{:T(128)} %constant.22.clone.1), padding=0_0x0_160 | pad | bytes 10321924 | tf_op jit(solution)/shard_map/jit(_pad)/pad | solution.py:55
  27.4 94.5 %reduce-scatter.4.cloned.1.call-done = f32[8,5120]{1,0:T(8,128)} async-done(((f32[256,5120]{1,0:T(8,128)}), f32[8,5120]{1,0:T(8,128)}) %reduce-scatter.4.cloned.1.call-update) | async-done | bytes 163856 | tf_op jit(solution)/shard_map/reduce_scatter | solution.py:56
  121.9 0.8 slice.37
  122.8 0.2 copy.115
  123.0 0.2 copy.97
  123.2 0.7 add_divide_fusion.1
  123.9 0.1 reshape.50
  124.0 0.9 slice.38
  124.9 1.7 add_divide_fusion
  126.6 0.8 concatenate.10
  127.5 63.7 %all-gather.4.cloned.1.call-done = f32[256,9920]{1,0:T(8,128)} async-done(((f32[8,9920]{1,0:T(8,128)}), f32[256,9920]{1,0:T(8,128)}) %all-gather.4.cloned.1.call-update) | async-done | bytes 10158096 | tf_op jit(solution)/shard_map/all_gather | solution.py:69
  191.2 2.0 fusion.20
  193.2 1.3 copy.103
  194.5 1.9 convolution_bitcast_fusion.3
  196.5 6.0 %fusion.9 = f32[30,256]{1,0:T(8,128)S(1)} fusion(f32[30,4000]{1,0:T(8,128)S(1)} %copy-done, f32[256,9920]{1,0:T(8,128)} %all-gather.4.cloned.1.call-done), kind=kOutput, calls=%fused_computation.15 | convolution fusion | flops 368640000 | bytes 4705024 | tf_op jit(solution)/shard_map/dv,rv->dr/dot_general | solution.py:77
  202.5 0.7 pad_maximum_fusion.1
  203.2 0.2 all-gather.6.cloned.1.call-start
  203.5 66.6 %all-reduce.3.cloned.1.call-done = f32[30,1024]{1,0:T(8,128)} async-done(((f32[30,1024]{1,0:T(8,128)}), f32[30,1024]{1,0:T(8,128)}) %all-reduce.3.cloned.1.call-update) | async-done | bytes 122896 | tf_op jit(solution)/shard_map/psum | solution.py:80
  270.1 0.1 copy.106
  270.3 0.3 copy.102
  270.6 1.6 convolution_bitcast_fusion.2
  272.3 5.5 %convolution_bitcast_fusion.1 = f32[30,4000]{1,0:T(8,128)} fusion(f32[30,256]{1,0:T(8,128)S(1)} %copy-done.4, f32[256,9920]{1,0:T(8,128)} %all-gather.4.cloned.1.call-done), kind=kOutput, calls=%fused_computation.6 | convolution fusion | flops 368640000 | bytes 4705024 | tf_op jit(solution)/shard_map/dot_general | solution.py:75
  277.9 49.6 %all-gather.6.cloned.1.call-done = f32[32,30,1024]{2,1,0:T(8,128)} async-done(((f32[1,30,1024]{2,1,0:T(8,128)}), f32[32,30,1024]{2,1,0:T(8,128)}) %all-gather.6.cloned.1.call-update) | async-done | bytes 3932176 | tf_op jit(solution)/shard_map/all_gather | solution.py:81
  327.5 5.6 %reshape.55 = f32[960,4,256]{2,1,0:T(4,128)} reshape(f32[32,30,1024]{2,1,0:T(8,128)} %all-gather.6.cloned.1.call-done) | data formatting | bytes 7864320 | tf_op jit(solution)/shard_map/reshape | solution.py:82
  333.1 10.8 %select_reduce_fusion = (f32[4]{0:T(128)S(1)}, f32[4,256,256]{2,1,0:T(8,128)S(1)}) fusion(pred[256,256]{1,0:T(8,128)(4,1)S(1)} %iota_compare_fusion, f32[960,4,256]{2,1,0:T(4,128)} %reshape.55), kind=kOutput, calls=%fused_computation.16 | convolution fusion | flops 3020423168 | bytes 5046288 | tf_op jit(solution)/shard_map/kdr,kds->krs/dot_general | solution.py:83
  343.9 0.2 broadcast_multiply_fusion.1
  344.2 19.6 %while.13 = (s32[]{:T(128)}, f32[4,256,256]{2,1,0:T(8,128)S(1)}, f32[4,256,256]{1,2,0:T(8,128)S(1)}, f32[256,256]{1,0:T(8,128)S(1)}, s32[]{:T(128)}) while((s32[]{:T(128)}, f32[4,256,256]{2,1,0:T(8,128)S(1)}, f32[4,256,256]{1,2,0:T(8,128)S(1)}, f32[256,256]{1,0:T(8,128)S(1)}, s32[]{:T(128)}) %tuple.36), condition=%wide.region_4.5_spmd.clone, body=%wide.region_3.4_spmd.clone.sunk | while | flops 3222339584 | bytes 14417981 | solution.py:42
  344.4 1.3 fusion.63
  345.7 1.9 fusion.64
  347.7 1.1 fusion.65
  348.8 0.1 copy.140
  348.9 1.9 convolution_bitcast_fusion.5
  350.9 1.3 fusion.63
  352.2 1.9 fusion.64
  354.1 1.1 fusion.65
  355.4 1.9 convolution_bitcast_fusion.5
  357.3 1.3 fusion.63
  358.7 1.9 fusion.64
  360.6 1.1 fusion.65
  361.8 1.9 convolution_bitcast_fusion.5
  363.8 0.1 multiply_bitcast_fusion
  363.9 1.1 fusion.13
  364.9 0.6 slice_bitcast_fusion
  365.5 0.6 slice.44
  (39 shorter events, 0.8 us)
Async XLA Ops:
  7.2 2.1 copy-start
  7.2 114.8 %reduce-scatter.4.cloned.1.call-start = ((), (), s32[]{:S(2)}) async-start(), calls=%async_computation.4 | async-start | bytes 5406720 | tf_op jit(solution)/shard_map/reduce_scatter | solution.py:56
  27.3 95.8 %copy-start.7 = (f32[8,3,320]{2,0,1:T(8,128)S(1)}, f32[8,3,320]{2,0,1:T(8,128)}, u32[]{:S(2)}) copy-start(f32[8,3,320]{2,0,1:T(8,128)} %param.16) | copy-start | bytes 92164
  27.4 95.8 %copy-start.8 = (f32[8,3,320]{2,0,1:T(8,128)S(1)}, f32[8,3,320]{2,0,1:T(8,128)}, u32[]{:S(2)}) copy-start(f32[8,3,320]{2,0,1:T(8,128)} %param.17) | copy-start | bytes 92164
  27.4 97.6 %copy-start.5 = (f32[8,4000]{1,0:T(8,128)S(1)}, f32[8,4000]{1,0:T(8,128)}, u32[]{:S(2)}) copy-start(f32[8,4000]{1,0:T(8,128)} %param.14) | copy-start | bytes 384004
  27.4 97.6 %copy-start.6 = (f32[8,4000]{1,0:T(8,128)S(1)}, f32[8,4000]{1,0:T(8,128)}, u32[]{:S(2)}) copy-start(f32[8,4000]{1,0:T(8,128)} %param.15) | copy-start | bytes 384004
  27.4 163.8 %all-gather.4.cloned.1.call-start = ((), (), s32[]{:S(2)}) async-start(), calls=%async_computation.1 | async-start | bytes 10543104 | tf_op jit(solution)/shard_map/all_gather | solution.py:69
  123.9 70.6 %copy-start.1 = (f32[3,30,320]{2,1,0:T(8,128)S(1)}, f32[3,30,320]{2,1,0:T(8,128)}, u32[]{:S(2)}) copy-start(f32[3,30,320]{2,1,0:T(8,128)} %param.11) | copy-start | bytes 345604
  127.5 142.6 %all-reduce.3.cloned.1.call-start = ((), (), s32[]{:S(2)}) async-start(), calls=%async_computation.2 | async-start | bytes 262144 | tf_op jit(solution)/shard_map/psum | solution.py:80
  196.5 74.2 %copy-start.3 = (f32[3,30,256]{2,1,0:T(8,128)S(1)}, f32[3,30,256]{2,1,0:T(8,128)}, u32[]{:S(2)}) copy-start(f32[3,30,256]{2,1,0:T(8,128)} %param.13) | copy-start | bytes 276484
  196.5 75.7 %copy-start.4 = (f32[30,256]{1,0:T(8,128)S(1)}, f32[30,256]{1,0:T(8,128)}, u32[]{:S(2)}) copy-start(f32[30,256]{1,0:T(8,128)} %param.12) | copy-start | bytes 92164
  203.2 124.3 %all-gather.6.cloned.1.call-start = ((), (), s32[]{:S(2)}) async-start(), calls=%async_computation.3 | async-start | bytes 4325376 | tf_op jit(solution)/shard_map/all_gather | solution.py:81
  270.1 7.7 %copy-start.2 = (f32[30,1024]{1,0:T(8,128)S(1)}, f32[30,1024]{1,0:T(8,128)}, u32[]{:S(2)}) copy-start(f32[30,1024]{1,0:T(8,128)} %all-reduce.3.cloned.1.call-done) | copy-start | bytes 368644
Sparse Core Ops, SparseCore 0:
  27.5 94.3 reduce-scatter.3
  127.6 63.5 all-gather.3
  203.3 66.6 all-reduce.2
  272.5 54.9 all-gather.5

commit v3 on v2

--- a/solution.py
+++ b/solution.py
@@ -1,3 +1,5 @@
+import functools
+
 import jax
 import jax.numpy as jnp
 from jax import lax
@@ -44,7 +46,18 @@
     return matmul(current, total)
 
 
-def local(emb_grad, mlp_grad, emb_basis, mlp_basis, emb_first, emb_second, mlp_first, mlp_second):
+def exchange_sum(value, axis, count):
+    if count & (count - 1):
+        return lax.psum(value, axis)
+    step = 1
+    while step < count:
+        pairs = [(index, index ^ step) for index in range(count)]
+        value = value + lax.ppermute(value, axis, pairs)
+        step *= 2
+    return value
+
+
+def local(shard_count, emb_grad, mlp_grad, emb_basis, mlp_basis, emb_first, emb_second, mlp_first, mlp_second):
     mats, rows, cols = mlp_grad.shape
     long_side = emb_grad.shape[1]
     rank = emb_basis.shape[1]
@@ -77,7 +90,7 @@
     emb_found = jnp.einsum("dv,rv->dr", emb_grad, emb_projected, precision=highest)
     mlp_found = jnp.einsum("kdf,rkf->dkr", mlp_grad, mlp_projected, precision=highest)
     found = jnp.concatenate([emb_found, mlp_found.reshape(rows, mats * rank)], axis=1)
-    found = lax.psum(found, "shard")
+    found = exchange_sum(found, "shard", shard_count)
     every = lax.all_gather(found, WIDE, axis=0, tiled=True)
     every = every.reshape(-1, mats + 1, rank).transpose(1, 0, 2)
     gram = jnp.einsum("kdr,kds->krs", every, every, precision=highest)
@@ -107,7 +120,7 @@
         P(WIDE, None, "shard"),
     )
     return jax.shard_map(
-        local,
+        functools.partial(local, mesh.shape["shard"]),
         mesh=mesh,
         in_specs=placed,
         out_specs=(

time: 373 us -> 324 us (0.87)
  waiting for transfers between devices: 274 us -> 215 us
  starting transfers between devices: 0.34 us -> 10.5 us
    psum x1 -> x0, waiting for transfers between devices: 66.6 us -> none  [local(): found = lax.psum(found, 'shard')]
    ppermute x0 -> x3, waiting for transfers between devices: none -> 12.5 us  [exchange_sum(): value = value + lax.ppermute(value, axis, pairs)]
    ppermute x0 -> x3, starting transfers between devices: none -> 10.3 us  [exchange_sum(): value = value + lax.ppermute(value, axis, pairs)]
    all_gather x1, waiting for transfers between devices: 49.6 us -> 44.1 us  [local(): every = lax.all_gather(found, WIDE, axis=0, tiled=True)]
  transfers between devices with their start and end apart: 4 -> 6, of which waited for: 4 -> 6; matrix products, arithmetic and copies ran while one was open for 2% -> 2% of each run, Pallas kernels for 0% -> 0%
where the time goes in v3:
time: 324 us; the launch traced here: 323 us
  waiting for transfers between devices  215 us (66%)
  matrix products  52 us (16%)
  local copies, waits for them, and re-layouts  25.4 us (8%)
  between operations  14 us (4%)
  starting transfers between devices  10.5 us (3%)
  other arithmetic  6.04 us (2%)
    reduce_scatter x1, waiting for transfers between devices, local(): share = lax.psum_scatter(terms, WIDE, scatter_dimension=0, tiled=True)  94.5 us
    all_gather x1, waiting for transfers between devices, local(): gathered = lax.all_gather(pieces, WIDE, axis=0, tiled=True)  63.7 us
    all_gather x1, waiting for transfers between devices, local(): every = lax.all_gather(found, WIDE, axis=0, tiled=True)  44.1 us
    dot_general x13, matrix products, matmul(): return jnp.einsum('...rs,...st->...rt', x, y, precision=highest)  19.9 us
    ppermute x3, waiting for transfers between devices, exchange_sum(): value = value + lax.ppermute(value, axis, pairs)  12.5 us
    dot_general x1, matrix products, local(): gram = jnp.einsum('kdr,kds->krs', every, every, precision=highest)  10.8 us
    ppermute x3, starting transfers between devices, exchange_sum(): value = value + lax.ppermute(value, axis, pairs)  10.3 us
  transfers between devices with their start and end apart: 6, of which 6 were waited for; matrix products, arithmetic and copies ran while one was open for 2% of the time, Pallas kernels for 0%

profile of v3, /device:TPU:1, one launch (start us, length us, event | category | flops | bytes accessed | tf_op | source)
XLA Modules:
  0.0 323.2 jit_solution(17516760997226267161)
XLA Ops:
  7.2 2.0 fusion.25
  9.3 4.2 %fusion.24 = f32[256,4000]{0,1:T(8,128)S(1)} fusion(f32[30,256]{1,0:T(8,128)} %param.12, f32[30,4000]{1,0:T(8,128)S(1)} %copy-done), kind=kOutput, calls=%fused_computation.39 | convolution fusion | flops 368640000 | bytes 4606720 | tf_op jit(solution)/shard_map/dr,dv->rv/dot_general | solution.py:64
  13.5 2.6 pad_maximum_fusion
  16.0 5.9 %copy.117 = f32[256,4960]{1,0:T(8,128)} copy(f32[256,4960]{0,1:T(8,128)} %pad_maximum_fusion) | data formatting | bytes 10158080
  21.9 5.4 %pad.4.clone = f32[256,5120]{1,0:T(8,128)} pad(f32[256,4960]{1,0:T(8,128)} %copy.117, f32[]{:T(128)} %constant.22.clone.1), padding=0_0x0_160 | pad | bytes 10321924 | tf_op jit(solution)/shard_map/jit(_pad)/pad | solution.py:68
  27.4 94.5 %reduce-scatter.4.cloned.1.call-done = f32[8,5120]{1,0:T(8,128)} async-done(((f32[256,5120]{1,0:T(8,128)}), f32[8,5120]{1,0:T(8,128)}) %reduce-scatter.4.cloned.1.call-update) | async-done | bytes 163856 | tf_op jit(solution)/shard_map/reduce_scatter | solution.py:69
  121.9 0.8 slice.37
  122.8 0.2 copy.115
  123.0 0.2 copy.97
  123.2 0.7 add_divide_fusion.1
  124.0 0.9 slice.38
  124.9 1.7 add_divide_fusion
  126.6 0.8 concatenate.10
  127.5 63.7 %all-gather.4.cloned.1.call-done = f32[256,9920]{1,0:T(8,128)} async-done(((f32[8,9920]{1,0:T(8,128)}), f32[256,9920]{1,0:T(8,128)}) %all-gather.4.cloned.1.call-update) | async-done | bytes 10158096 | tf_op jit(solution)/shard_map/all_gather | solution.py:82
  191.2 1.9 fusion.21
  193.1 1.3 copy.103
  194.4 1.9 convolution_bitcast_fusion.3
  196.5 6.0 %fusion.9 = f32[30,256]{1,0:T(8,128)S(1)} fusion(f32[30,4000]{1,0:T(8,128)S(1)} %copy-done, f32[256,9920]{1,0:T(8,128)} %all-gather.4.cloned.1.call-done), kind=kOutput, calls=%fused_computation.15 | convolution fusion | flops 368640000 | bytes 4705024 | tf_op jit(solution)/shard_map/dv,rv->dr/dot_general | solution.py:90
  202.5 1.4 collective-permute-start
  203.9 3.5 %collective-permute-done = f32[30,1024]{1,0:T(8,128)S(1)} collective-permute-done((f32[30,1024]{1,0:T(8,128)S(1)}, f32[30,1024]{1,0:T(8,128)S(1)}, u32[]{:S(2)}, u32[]{:S(2)}) %collective-permute-start) | collective-permute-done | bytes 122912 | tf_op jit(solution)/shard_map/ppermute | solution.py:55
  207.4 2.4 collective-permute-start.1
  209.8 5.9 %collective-permute-done.1 = f32[30,1024]{1,0:T(8,128)S(1)} collective-permute-done((f32[30,1024]{1,0:T(8,128)S(1)}, f32[30,1024]{1,0:T(8,128)S(1)}, u32[]{:S(2)}, u32[]{:S(2)}) %collective-permute-start.1) | collective-permute-done | bytes 122912 | tf_op jit(solution)/shard_map/ppermute | solution.py:55
  215.7 6.6 %collective-permute-start.2 = (f32[30,1024]{1,0:T(8,128)S(1)}, f32[30,1024]{1,0:T(8,128)S(1)}, u32[]{:S(2)}, u32[]{:S(2)}) collective-permute-start(f32[30,1024]{1,0:T(8,128)S(1)} %add.65), channel_id=1, source_target_pairs={{0,128},{32,160},{64,192},{96,224},{128,0},{160,32},{192,64},{224,... | collective-permute-start | bytes 368648 | tf_op jit(solution)/shard_map/ppermute | solution.py:55
  222.3 3.1 collective-permute-done.2
  225.4 0.7 add.66
  226.3 0.3 copy.102
  226.6 1.6 convolution_bitcast_fusion.2
  228.2 5.5 %convolution_bitcast_fusion.1 = f32[30,4000]{1,0:T(8,128)} fusion(f32[30,256]{1,0:T(8,128)S(1)} %copy-done.4, f32[256,9920]{1,0:T(8,128)} %all-gather.4.cloned.1.call-done), kind=kOutput, calls=%fused_computation.6 | convolution fusion | flops 368640000 | bytes 4705024 | tf_op jit(solution)/shard_map/dot_general | solution.py:88
  233.9 44.1 %all-gather.6.cloned.1.call-done = f32[32,30,1024]{2,1,0:T(8,128)} async-done(((f32[1,30,1024]{2,1,0:T(8,128)}), f32[32,30,1024]{2,1,0:T(8,128)}) %all-gather.6.cloned.1.call-update) | async-done | bytes 3932176 | tf_op jit(solution)/shard_map/all_gather | solution.py:94
  277.9 5.6 %reshape.55 = f32[960,4,256]{2,1,0:T(4,128)} reshape(f32[32,30,1024]{2,1,0:T(8,128)} %all-gather.6.cloned.1.call-done) | data formatting | bytes 7864320 | tf_op jit(solution)/shard_map/reshape | solution.py:95
  283.5 10.8 %select_reduce_fusion = (f32[4]{0:T(128)S(1)}, f32[4,256,256]{2,1,0:T(8,128)S(1)}) fusion(pred[256,256]{1,0:T(8,128)(4,1)S(1)} %iota_compare_fusion, f32[960,4,256]{2,1,0:T(4,128)} %reshape.55), kind=kOutput, calls=%fused_computation.16 | convolution fusion | flops 3020423168 | bytes 5046288 | tf_op jit(solution)/shard_map/kdr,kds->krs/dot_general | solution.py:96
  294.3 0.2 broadcast_multiply_fusion.1
  294.6 19.6 %while.13 = (s32[]{:T(128)}, f32[4,256,256]{2,1,0:T(8,128)S(1)}, f32[4,256,256]{1,2,0:T(8,128)S(1)}, f32[256,256]{1,0:T(8,128)S(1)}, s32[]{:T(128)}) while((s32[]{:T(128)}, f32[4,256,256]{2,1,0:T(8,128)S(1)}, f32[4,256,256]{1,2,0:T(8,128)S(1)}, f32[256,256]{1,0:T(8,128)S(1)}, s32[]{:T(128)}) %tuple.36), condition=%wide.region_3.4_spmd.clone, body=%wide.region_2.3_spmd.clone.sunk | while | flops 3222339584 | bytes 14417981 | solution.py:44
  294.9 1.3 fusion.64
  296.2 1.9 fusion.65
  298.1 1.1 fusion.66
  299.4 1.9 convolution_bitcast_fusion.5
  301.3 1.3 fusion.64
  302.6 1.9 fusion.65
  304.6 1.1 fusion.66
  305.8 1.9 convolution_bitcast_fusion.5
  307.8 1.3 fusion.64
  309.1 1.9 fusion.65
  311.0 1.1 fusion.66
  312.3 1.9 convolution_bitcast_fusion.5
  314.3 1.1 fusion.13
  315.4 0.6 slice_bitcast_fusion
  316.0 0.6 slice.44
  (45 shorter events, 1.2 us)
Async XLA Ops:
  7.2 2.1 copy-start
  7.2 114.8 %reduce-scatter.4.cloned.1.call-start = ((), (), s32[]{:S(2)}) async-start(), calls=%async_computation.3 | async-start | bytes 5406720 | tf_op jit(solution)/shard_map/reduce_scatter | solution.py:69
  27.3 95.8 %copy-start.7 = (f32[8,3,320]{2,0,1:T(8,128)S(1)}, f32[8,3,320]{2,0,1:T(8,128)}, u32[]{:S(2)}) copy-start(f32[8,3,320]{2,0,1:T(8,128)} %param.16) | copy-start | bytes 92164
  27.3 95.8 %copy-start.8 = (f32[8,3,320]{2,0,1:T(8,128)S(1)}, f32[8,3,320]{2,0,1:T(8,128)}, u32[]{:S(2)}) copy-start(f32[8,3,320]{2,0,1:T(8,128)} %param.17) | copy-start | bytes 92164
  27.3 97.6 %copy-start.5 = (f32[8,4000]{1,0:T(8,128)S(1)}, f32[8,4000]{1,0:T(8,128)}, u32[]{:S(2)}) copy-start(f32[8,4000]{1,0:T(8,128)} %param.14) | copy-start | bytes 384004
  27.3 97.6 %copy-start.6 = (f32[8,4000]{1,0:T(8,128)S(1)}, f32[8,4000]{1,0:T(8,128)}, u32[]{:S(2)}) copy-start(f32[8,4000]{1,0:T(8,128)} %param.15) | copy-start | bytes 384004
  27.4 163.8 %all-gather.4.cloned.1.call-start = ((), (), s32[]{:S(2)}) async-start(), calls=%async_computation.1 | async-start | bytes 10543104 | tf_op jit(solution)/shard_map/all_gather | solution.py:82
  123.9 70.6 %copy-start.2 = (f32[3,30,320]{2,1,0:T(8,128)S(1)}, f32[3,30,320]{2,1,0:T(8,128)}, u32[]{:S(2)}) copy-start(f32[3,30,320]{2,1,0:T(8,128)} %param.11) | copy-start | bytes 345604
  127.5 150.5 %all-gather.6.cloned.1.call-start = ((), (), s32[]{:S(2)}) async-start(), calls=%async_computation.2 | async-start | bytes 4325376 | tf_op jit(solution)/shard_map/all_gather | solution.py:94
  196.5 30.2 %copy-start.3 = (f32[3,30,256]{2,1,0:T(8,128)S(1)}, f32[3,30,256]{2,1,0:T(8,128)}, u32[]{:S(2)}) copy-start(f32[3,30,256]{2,1,0:T(8,128)} %param.13) | copy-start | bytes 276484
  196.5 31.8 %copy-start.4 = (f32[30,256]{1,0:T(8,128)S(1)}, f32[30,256]{1,0:T(8,128)}, u32[]{:S(2)}) copy-start(f32[30,256]{1,0:T(8,128)} %param.12) | copy-start | bytes 92164
  202.5 4.9 %collective-permute-start = (f32[30,1024]{1,0:T(8,128)S(1)}, f32[30,1024]{1,0:T(8,128)S(1)}, u32[]{:S(2)}, u32[]{:S(2)}) collective-permute-start(f32[30,1024]{1,0:T(8,128)S(1)} %pad_maximum_fusion.1), channel_id=1, source_target_pairs={{0,32},{32,0},{64,96},{96,64},{128,160},{160,128},{192,224},{224,1... | collective-permute-start | bytes 368648 | tf_op jit(solution)/shard_map/ppermute | solution.py:55
  207.4 8.2 %collective-permute-start.1 = (f32[30,1024]{1,0:T(8,128)S(1)}, f32[30,1024]{1,0:T(8,128)S(1)}, u32[]{:S(2)}, u32[]{:S(2)}) collective-permute-start(f32[30,1024]{1,0:T(8,128)S(1)} %fusion.17), channel_id=1, source_target_pairs={{0,64},{32,96},{64,0},{96,32},{128,192},{160,224},{192,128},{224,1... | collective-permute-start | bytes 368648 | tf_op jit(solution)/shard_map/ppermute | solution.py:55
  215.7 9.7 %collective-permute-start.2 = (f32[30,1024]{1,0:T(8,128)S(1)}, f32[30,1024]{1,0:T(8,128)S(1)}, u32[]{:S(2)}, u32[]{:S(2)}) collective-permute-start(f32[30,1024]{1,0:T(8,128)S(1)} %add.65), channel_id=1, source_target_pairs={{0,128},{32,160},{64,192},{96,224},{128,0},{160,32},{192,64},{224,... | collective-permute-start | bytes 368648 | tf_op jit(solution)/shard_map/ppermute | solution.py:55
  226.1 7.7 %copy-start.1 = (f32[30,1024]{1,0:T(8,128)S(1)}, f32[30,1024]{1,0:T(8,128)}, u32[]{:S(2)}) copy-start(f32[30,1024]{1,0:T(8,128)} %add.66) | copy-start | bytes 368644
Sparse Core Ops, SparseCore 0:
  27.5 94.3 reduce-scatter.3
  127.6 63.5 all-gather.3
  226.2 51.6 all-gather.5

commit v4 on v3

--- a/solution.py
+++ b/solution.py
@@ -57,16 +57,31 @@
     return value
 
 
-def local(shard_count, emb_grad, mlp_grad, emb_basis, mlp_basis, emb_first, emb_second, mlp_first, mlp_second):
+def halving_scatter(value, axis, count):
+    if count & (count - 1):
+        return lax.psum_scatter(value, axis, scatter_dimension=0, tiled=True)
+    bits = count.bit_length() - 1
+    block = value.shape[0] // count
+    index = lax.axis_index(axis)
+    value = value.reshape((2,) * bits + (block,) + value.shape[1:])
+    for bit in range(bits):
+        own = (index >> bit) & 1
+        axis_at = bits - 1 - bit
+        keep = lax.dynamic_index_in_dim(value, own, axis_at, keepdims=False)
+        send = lax.dynamic_index_in_dim(value, 1 - own, axis_at, keepdims=False)
+        pairs = [(place, place ^ (1 << bit)) for place in range(count)]
+        value = keep + lax.ppermute(send, axis, pairs)
+    return value
+
+
+def local(shard_count, wide_count, emb_grad, mlp_grad, emb_basis, mlp_basis, emb_first, emb_second, mlp_first, mlp_second):
     mats, rows, cols = mlp_grad.shape
     long_side = emb_grad.shape[1]
     rank = emb_basis.shape[1]
     emb_term = jnp.einsum("dr,dv->rv", emb_basis, emb_grad, precision=highest)
     mlp_term = jnp.einsum("kdr,kdf->rkf", mlp_basis, mlp_grad, precision=highest)
     terms = jnp.concatenate([emb_term, mlp_term.reshape(rank, mats * cols)], axis=1)
-    pad = -terms.shape[1] % 512
-    terms = jnp.pad(terms, ((0, 0), (0, pad)))
-    share = lax.psum_scatter(terms, WIDE, scatter_dimension=0, tiled=True)
+    share = halving_scatter(terms, WIDE, wide_count)
     emb_share = share[:, :long_side]
     mlp_share = share[:, long_side : long_side + mats * cols].reshape(-1, mats, cols)
     emb_first_new, emb_second_new, emb_direction = adam_moments(emb_first, emb_second, emb_share)
@@ -75,7 +90,7 @@
         [
             emb_direction,
             mlp_direction.reshape(-1, mats * cols),
-            share[:, : long_side + mats * cols],
+            share,
         ],
         axis=1,
     )
@@ -120,7 +135,7 @@
         P(WIDE, None, "shard"),
     )
     return jax.shard_map(
-        functools.partial(local, mesh.shape["shard"]),
+        functools.partial(local, mesh.shape["shard"], mesh.shape["tensor"] * mesh.shape["section"]),
         mesh=mesh,
         in_specs=placed,
         out_specs=(

time: 324 us -> 295 us (0.910)
  waiting for transfers between devices: 215 us -> 184 us
  local copies, waits for them, and re-layouts: 25.4 us -> 19.3 us
  starting transfers between devices: 10.5 us -> 16.4 us
    reduce_scatter x1 -> x0, waiting for transfers between devices: 94.5 us -> none  [local(): share = lax.psum_scatter(terms, WIDE, scatter_dimension=0, tiled=True)]
    ppermute x0 -> x5, waiting for transfers between devices: none -> 60.9 us  [halving_scatter(): value = keep + lax.ppermute(send, axis, pairs)]
    ppermute x0 -> x5, starting transfers between devices: none -> 5.71 us  [halving_scatter(): value = keep + lax.ppermute(send, axis, pairs)]
    add x0 -> x5, other arithmetic: none -> 5.43 us  [halving_scatter(): value = keep + lax.ppermute(send, axis, pairs)]
    pad x1 -> x0, local copies, waits for them, and re-layouts: 5.4 us -> none  [local(): terms = jnp.pad(terms, ((0, 0), (0, pad)))]
    all_gather x1, waiting for transfers between devices: 63.7 us -> 67.5 us  [local(): gathered = lax.all_gather(pieces, WIDE, axis=0, tiled=True)]
  transfers between devices with their start and end apart: 6 -> 10, of which waited for: 6 -> 10; matrix products, arithmetic and copies ran while one was open for 2% -> 3% of each run, Pallas kernels for 0% -> 0%
where the time goes in v4:
time: 295 us
  waiting for transfers between devices  184 us (62%)
  matrix products  51.3 us (17%)
  local copies, waits for them, and re-layouts  19.3 us (7%)
  starting transfers between devices  16.4 us (6%)
  between operations  14.4 us (5%)
  other arithmetic  9.24 us (3%)
    all_gather x1, waiting for transfers between devices, local(): gathered = lax.all_gather(pieces, WIDE, axis=0, tiled=True)  67.5 us
    ppermute x5, waiting for transfers between devices, halving_scatter(): value = keep + lax.ppermute(send, axis, pairs)  60.9 us
    all_gather x1, waiting for transfers between devices, local(): every = lax.all_gather(found, WIDE, axis=0, tiled=True)  42.9 us
    dot_general x13, matrix products, matmul(): return jnp.einsum('...rs,...st->...rt', x, y, precision=highest)  19.9 us
    ppermute x3, waiting for transfers between devices, exchange_sum(): value = value + lax.ppermute(value, axis, pairs)  12.5 us
    dot_general x1, matrix products, local(): gram = jnp.einsum('kdr,kds->krs', every, every, precision=highest)  10.8 us
    ppermute x3, starting transfers between devices, exchange_sum(): value = value + lax.ppermute(value, axis, pairs)  10.4 us
    dot_general x1, matrix products, local(): jnp.einsum('dv,rv->dr', emb_grad, emb_projected, precision=highest)  6.02 us
  transfers between devices with their start and end apart: 10, of which 10 were waited for; matrix products, arithmetic and copies ran while one was open for 3% of the time, Pallas kernels for 0%

profile of v4, /device:TPU:1, one launch (start us, length us, event | category | flops | bytes accessed | tf_op | source)
XLA Modules:
  0.0 294.8 jit_solution(3440013566192693220)
XLA Ops:
  7.2 2.0 convolution_bitcast_fusion.2
  10.0 0.9 concatenate.15
  10.9 3.5 %fusion.31 = f32[256,4000]{1,0:T(8,128)S(1)} fusion(f32[30,256]{1,0:T(8,128)S(1)} %copy-done.7, f32[30,4000]{1,0:T(8,128)S(1)} %copy-done), kind=kOutput, calls=%fused_computation.58 | convolution fusion | flops 368640000 | bytes 4606720 | tf_op jit(solution)/shard_map/dr,dv->rv/dot_general | solution.py:81
  14.4 1.9 copy-done.1
  16.4 1.8 fusion.10
  18.2 3.2 %collective-permute-start = (f32[2,2,2,2,8,4960]{5,4,3,2,1,0:T(8,128)}, f32[2,2,2,2,8,4960]{5,4,3,2,1,0:T(8,128)}, u32[]{:S(2)}, u32[]{:S(2)}) collective-permute-start(f32[2,2,2,2,8,4960]{5,4,3,2,1,0:T(8,128)} %fusion.10), channel_id=1, source_target_pairs={{0,1},{1,0},{2,3},{3,2},{4,5},{5,4},{6,7},{7,6},{8,9},{9,8},{10,11... | collective-permute-start | bytes 7618568 | tf_op jit(solution)/shard_map/ppermute | solution.py:73
  21.4 4.8 %collective-permute-done = f32[2,2,2,2,8,4960]{5,4,3,2,1,0:T(8,128)} collective-permute-done((f32[2,2,2,2,8,4960]{5,4,3,2,1,0:T(8,128)}, f32[2,2,2,2,8,4960]{5,4,3,2,1,0:T(8,128)}, u32[]{:S(2)}, u32[]{:S(2)}) %collective-permute-start) | collective-permute-done | bytes 2539552 | tf_op jit(solution)/shard_map/ppermute | solution.py:73
  26.2 2.8 fusion.13
  29.0 1.2 dynamic-slice_bitcast_fusion
  30.2 29.6 %collective-permute-done.1 = f32[2,2,2,8,4960]{4,3,2,1,0:T(8,128)} collective-permute-done((f32[2,2,2,8,4960]{4,3,2,1,0:T(8,128)}, f32[2,2,2,8,4960]{4,3,2,1,0:T(8,128)}, u32[]{:S(2)}, u32[]{:S(2)}) %collective-permute-start.1) | collective-permute-done | bytes 1269792 | tf_op jit(solution)/shard_map/ppermute | solution.py:73
  59.7 1.4 bitcast_add_fusion
  61.2 1.1 copy-done.3
  62.3 1.1 collective-permute-start.2
  63.4 15.2 %collective-permute-done.2 = f32[2,2,8,4960]{3,2,1,0:T(8,128)S(1)} collective-permute-done((f32[2,2,8,4960]{3,2,1,0:T(8,128)S(1)}, f32[2,2,8,4960]{3,2,1,0:T(8,128)S(1)}, u32[]{:S(2)}, u32[]{:S(2)}) %collective-permute-start.2) | collective-permute-done | bytes 634912 | tf_op jit(solution)/shard_map/ppermute | solution.py:73
  78.6 1.1 bitcast_add_fusion.1
  79.9 7.0 %collective-permute-done.3 = f32[2,8,4960]{2,1,0:T(8,128)S(1)} collective-permute-done((f32[2,8,4960]{2,1,0:T(8,128)S(1)}, f32[2,8,4960]{2,1,0:T(8,128)S(1)}, u32[]{:S(2)}, u32[]{:S(2)}) %collective-permute-start.3) | collective-permute-done | bytes 317472 | tf_op jit(solution)/shard_map/ppermute | solution.py:73
  87.0 1.3 collective-permute-start.4
  88.3 4.4 %collective-permute-done.4 = f32[8,4960]{1,0:T(8,128)S(1)} collective-permute-done((f32[8,4960]{1,0:T(8,128)S(1)}, f32[8,4960]{1,0:T(8,128)S(1)}, u32[]{:S(2)}, u32[]{:S(2)}) %collective-permute-start.4) | collective-permute-done | bytes 158752 | tf_op jit(solution)/shard_map/ppermute | solution.py:73
  95.0 67.5 %all-gather.4.cloned.1.call-done = f32[256,9920]{1,0:T(8,128)} async-done(((f32[8,9920]{1,0:T(8,128)}), f32[256,9920]{1,0:T(8,128)}) %all-gather.4.cloned.1.call-update) | async-done | bytes 10158096 | tf_op jit(solution)/shard_map/all_gather | solution.py:97
  162.5 1.9 fusion.28
  164.4 1.3 copy.61
  165.7 1.9 convolution_bitcast_fusion.4
  167.8 6.0 %fusion.14 = f32[30,256]{1,0:T(8,128)S(1)} fusion(f32[30,4000]{1,0:T(8,128)S(1)} %copy-done, f32[256,9920]{1,0:T(8,128)} %all-gather.4.cloned.1.call-done), kind=kOutput, calls=%fused_computation.26 | convolution fusion | flops 368640000 | bytes 4705024 | tf_op jit(solution)/shard_map/dv,rv->dr/dot_general | solution.py:105
  173.8 1.4 collective-permute-start.5
  175.2 3.5 %collective-permute-done.5 = f32[30,1024]{1,0:T(8,128)S(1)} collective-permute-done((f32[30,1024]{1,0:T(8,128)S(1)}, f32[30,1024]{1,0:T(8,128)S(1)}, u32[]{:S(2)}, u32[]{:S(2)}) %collective-permute-start.5) | collective-permute-done | bytes 122912 | tf_op jit(solution)/shard_map/ppermute | solution.py:55
  178.7 2.4 collective-permute-start.6
  181.1 5.9 %collective-permute-done.6 = f32[30,1024]{1,0:T(8,128)S(1)} collective-permute-done((f32[30,1024]{1,0:T(8,128)S(1)}, f32[30,1024]{1,0:T(8,128)S(1)}, u32[]{:S(2)}, u32[]{:S(2)}) %collective-permute-start.6) | collective-permute-done | bytes 122912 | tf_op jit(solution)/shard_map/ppermute | solution.py:55
  187.0 6.7 %collective-permute-start.7 = (f32[30,1024]{1,0:T(8,128)S(1)}, f32[30,1024]{1,0:T(8,128)S(1)}, u32[]{:S(2)}, u32[]{:S(2)}) collective-permute-start(f32[30,1024]{1,0:T(8,128)S(1)} %add.135), channel_id=1, source_target_pairs={{0,128},{32,160},{64,192},{96,224},{128,0},{160,32},{192,64},{224,... | collective-permute-start | bytes 368648 | tf_op jit(solution)/shard_map/ppermute | solution.py:55
  193.6 3.1 %collective-permute-done.7 = f32[30,1024]{1,0:T(8,128)S(1)} collective-permute-done((f32[30,1024]{1,0:T(8,128)S(1)}, f32[30,1024]{1,0:T(8,128)S(1)}, u32[]{:S(2)}, u32[]{:S(2)}) %collective-permute-start.7) | collective-permute-done | bytes 122912 | tf_op jit(solution)/shard_map/ppermute | solution.py:55
  199.2 1.6 convolution_bitcast_fusion.3
  200.8 5.5 %convolution_bitcast_fusion.1 = f32[30,4000]{1,0:T(8,128)} fusion(f32[30,256]{1,0:T(8,128)S(1)} %copy-done.7, f32[256,9920]{1,0:T(8,128)} %all-gather.4.cloned.1.call-done), kind=kOutput, calls=%fused_computation.9 | convolution fusion | flops 368640000 | bytes 4705024 | tf_op jit(solution)/shard_map/dot_general | solution.py:103
  206.4 42.9 %all-gather.6.cloned.1.call-done = f32[32,30,1024]{2,1,0:T(8,128)} async-done(((f32[1,30,1024]{2,1,0:T(8,128)}), f32[32,30,1024]{2,1,0:T(8,128)}) %all-gather.6.cloned.1.call-update) | async-done | bytes 3932176 | tf_op jit(solution)/shard_map/all_gather | solution.py:109
  249.3 5.6 %reshape.56 = f32[960,4,256]{2,1,0:T(4,128)} reshape(f32[32,30,1024]{2,1,0:T(8,128)} %all-gather.6.cloned.1.call-done) | data formatting | bytes 7864320 | tf_op jit(solution)/shard_map/reshape | solution.py:110
  254.9 10.8 %select_reduce_fusion = (f32[4]{0:T(128)S(1)}, f32[4,256,256]{2,1,0:T(8,128)S(1)}) fusion(pred[256,256]{1,0:T(8,128)(4,1)S(1)} %iota_compare_fusion, f32[960,4,256]{2,1,0:T(4,128)} %reshape.56), kind=kOutput, calls=%fused_computation.27 | convolution fusion | flops 3020423168 | bytes 5046288 | tf_op jit(solution)/shard_map/kdr,kds->krs/dot_general | solution.py:111
  265.9 19.6 %while.13 = (s32[]{:T(128)}, f32[4,256,256]{2,1,0:T(8,128)S(1)}, f32[4,256,256]{1,2,0:T(8,128)S(1)}, f32[256,256]{1,0:T(8,128)S(1)}, s32[]{:T(128)}) while((s32[]{:T(128)}, f32[4,256,256]{2,1,0:T(8,128)S(1)}, f32[4,256,256]{1,2,0:T(8,128)S(1)}, f32[256,256]{1,0:T(8,128)S(1)}, s32[]{:T(128)}) %tuple.35), condition=%wide.region_2.3_spmd.clone, body=%wide.region_1.2_spmd.clone.sunk | while | flops 3222339584 | bytes 14417981 | solution.py:44
  266.3 1.3 fusion.70
  267.6 1.9 fusion.71
  269.5 1.1 fusion.72
  270.7 1.9 convolution_bitcast_fusion.6
  272.7 1.3 fusion.70
  274.0 1.9 fusion.71
  275.9 1.1 fusion.72
  277.2 1.9 convolution_bitcast_fusion.6
  279.2 1.3 fusion.70
  280.5 1.9 fusion.71
  282.4 1.1 fusion.72
  283.6 1.9 convolution_bitcast_fusion.6
  285.7 1.1 fusion.18
  (66 shorter events, 7.9 us)
Async XLA Ops:
  7.2 3.8 %copy-start = (f32[30,4000]{1,0:T(8,128)S(1)}, f32[30,4000]{1,0:T(8,128)}, u32[]{:S(2)}) copy-start(f32[30,4000]{1,0:T(8,128)} %param.10) | copy-start | bytes 1440004
  7.2 3.8 %copy-start.7 = (f32[30,256]{1,0:T(8,128)S(1)}, f32[30,256]{1,0:T(8,128)}, u32[]{:S(2)}) copy-start(f32[30,256]{1,0:T(8,128)} %param.12) | copy-start | bytes 92164
  7.2 155.3 %all-gather.4.cloned.1.call-start = ((), (), s32[]{:S(2)}) async-start(), calls=%async_computation | async-start | bytes 10543104 | tf_op jit(solution)/shard_map/all_gather | solution.py:97
  10.9 7.3 %copy-start.2 = (f32[2,2,2,2,2,8,960]{6,5,4,3,2,1,0:T(8,128)}, f32[2,2,2,2,2,8,960]{6,5,4,3,2,1,0:T(8,128)S(1)}, u32[]{:S(2)}) copy-start(f32[2,2,2,2,2,8,960]{6,5,4,3,2,1,0:T(8,128)S(1)} %concatenate.15) | copy-start | bytes 2949124
  14.4 2.0 copy-start.1
  18.2 8.0 %collective-permute-start = (f32[2,2,2,2,8,4960]{5,4,3,2,1,0:T(8,128)}, f32[2,2,2,2,8,4960]{5,4,3,2,1,0:T(8,128)}, u32[]{:S(2)}, u32[]{:S(2)}) collective-permute-start(f32[2,2,2,2,8,4960]{5,4,3,2,1,0:T(8,128)} %fusion.10), channel_id=1, source_target_pairs={{0,1},{1,0},{2,3},{3,2},{4,5},{5,4},{6,7},{7,6},{8,9},{9,8},{10,11... | collective-permute-start | bytes 7618568 | tf_op jit(solution)/shard_map/ppermute | solution.py:73
  30.2 29.6 %collective-permute-start.1 = (f32[2,2,2,8,4960]{4,3,2,1,0:T(8,128)}, f32[2,2,2,8,4960]{4,3,2,1,0:T(8,128)}, u32[]{:S(2)}, u32[]{:S(2)}) collective-permute-start(f32[2,2,2,8,4960]{4,3,2,1,0:T(8,128)} %dynamic-slice_bitcast_fusion), channel_id=1, source_target_pairs={{0,2},{1,3},{2,0},{3,1},{4,6},{5,7},{6,4},{7,5},{8,10},{9,11},{10,... | collective-permute-start | bytes 3809288 | tf_op jit(solution)/shard_map/ppermute | solution.py:73
  30.2 62.7 %copy-start.10 = (f32[8,3,320]{2,0,1:T(8,128)S(1)}, f32[8,3,320]{2,0,1:T(8,128)}, u32[]{:S(2)}) copy-start(f32[8,3,320]{2,0,1:T(8,128)} %param.16) | copy-start | bytes 92164
  30.2 62.7 %copy-start.11 = (f32[8,3,320]{2,0,1:T(8,128)S(1)}, f32[8,3,320]{2,0,1:T(8,128)}, u32[]{:S(2)}) copy-start(f32[8,3,320]{2,0,1:T(8,128)} %param.17) | copy-start | bytes 92164
  61.2 1.1 copy-start.3
  62.2 30.8 %copy-start.8 = (f32[8,4000]{1,0:T(8,128)S(1)}, f32[8,4000]{1,0:T(8,128)}, u32[]{:S(2)}) copy-start(f32[8,4000]{1,0:T(8,128)} %param.14) | copy-start | bytes 384004
  62.2 30.8 %copy-start.9 = (f32[8,4000]{1,0:T(8,128)S(1)}, f32[8,4000]{1,0:T(8,128)}, u32[]{:S(2)}) copy-start(f32[8,4000]{1,0:T(8,128)} %param.15) | copy-start | bytes 384004
  62.3 16.3 %collective-permute-start.2 = (f32[2,2,8,4960]{3,2,1,0:T(8,128)S(1)}, f32[2,2,8,4960]{3,2,1,0:T(8,128)S(1)}, u32[]{:S(2)}, u32[]{:S(2)}) collective-permute-start(f32[2,2,8,4960]{3,2,1,0:T(8,128)S(1)} %dynamic-slice_bitcast_fusion.1), channel_id=1, source_target_pairs={{0,4},{1,5},{2,6},{3,7},{4,0},{5,1},{6,2},{7,3},{8,12},{9,13},{10,... | collective-permute-start | bytes 1904648 | tf_op jit(solution)/shard_map/ppermute | solution.py:73
  79.8 7.1 %collective-permute-start.3 = (f32[2,8,4960]{2,1,0:T(8,128)S(1)}, f32[2,8,4960]{2,1,0:T(8,128)S(1)}, u32[]{:S(2)}, u32[]{:S(2)}) collective-permute-start(f32[2,8,4960]{2,1,0:T(8,128)S(1)} %dynamic-slice_bitcast_fusion.2), channel_id=1, source_target_pairs={{0,8},{1,9},{2,10},{3,11},{4,12},{5,13},{6,14},{7,15},{8,0},{9,1},... | collective-permute-start | bytes 952328 | tf_op jit(solution)/shard_map/ppermute | solution.py:73
  87.0 5.7 %collective-permute-start.4 = (f32[8,4960]{1,0:T(8,128)S(1)}, f32[8,4960]{1,0:T(8,128)S(1)}, u32[]{:S(2)}, u32[]{:S(2)}) collective-permute-start(f32[8,4960]{1,0:T(8,128)S(1)} %dynamic-slice_bitcast_fusion.3), channel_id=1, source_target_pairs={{0,16},{1,17},{2,18},{3,19},{4,20},{5,21},{6,22},{7,23},{8,24},{9,... | collective-permute-start | bytes 476168 | tf_op jit(solution)/shard_map/ppermute | solution.py:73
  93.1 72.6 %copy-start.5 = (f32[3,30,320]{2,1,0:T(8,128)S(1)}, f32[3,30,320]{2,1,0:T(8,128)}, u32[]{:S(2)}) copy-start(f32[3,30,320]{2,1,0:T(8,128)} %param.11) | copy-start | bytes 345604
  94.7 154.5 %all-gather.6.cloned.1.call-start = ((), (), s32[]{:S(2)}) async-start(), calls=%async_computation.1 | async-start | bytes 4325376 | tf_op jit(solution)/shard_map/all_gather | solution.py:109
  167.8 31.4 %copy-start.6 = (f32[3,30,256]{2,1,0:T(8,128)S(1)}, f32[3,30,256]{2,1,0:T(8,128)}, u32[]{:S(2)}) copy-start(f32[3,30,256]{2,1,0:T(8,128)} %param.13) | copy-start | bytes 276484
  173.8 4.9 %collective-permute-start.5 = (f32[30,1024]{1,0:T(8,128)S(1)}, f32[30,1024]{1,0:T(8,128)S(1)}, u32[]{:S(2)}, u32[]{:S(2)}) collective-permute-start(f32[30,1024]{1,0:T(8,128)S(1)} %pad_maximum_fusion), channel_id=1, source_target_pairs={{0,32},{32,0},{64,96},{96,64},{128,160},{160,128},{192,224},{224,1... | collective-permute-start | bytes 368648 | tf_op jit(solution)/shard_map/ppermute | solution.py:55
  178.7 8.2 %collective-permute-start.6 = (f32[30,1024]{1,0:T(8,128)S(1)}, f32[30,1024]{1,0:T(8,128)S(1)}, u32[]{:S(2)}, u32[]{:S(2)}) collective-permute-start(f32[30,1024]{1,0:T(8,128)S(1)} %fusion.23), channel_id=1, source_target_pairs={{0,64},{32,96},{64,0},{96,32},{128,192},{160,224},{192,128},{224,1... | collective-permute-start | bytes 368648 | tf_op jit(solution)/shard_map/ppermute | solution.py:55
  187.0 9.8 %collective-permute-start.7 = (f32[30,1024]{1,0:T(8,128)S(1)}, f32[30,1024]{1,0:T(8,128)S(1)}, u32[]{:S(2)}, u32[]{:S(2)}) collective-permute-start(f32[30,1024]{1,0:T(8,128)S(1)} %add.135), channel_id=1, source_target_pairs={{0,128},{32,160},{64,192},{96,224},{128,0},{160,32},{192,64},{224,... | collective-permute-start | bytes 368648 | tf_op jit(solution)/shard_map/ppermute | solution.py:55
  198.8 7.5 %copy-start.4 = (f32[30,1024]{1,0:T(8,128)S(1)}, f32[30,1024]{1,0:T(8,128)}, u32[]{:S(2)}) copy-start(f32[30,1024]{1,0:T(8,128)} %add.136) | copy-start | bytes 368644
Sparse Core Ops, SparseCore 0:
  94.8 67.5 all-gather.3
  197.5 51.6 all-gather.5

commit v5 on v4

--- a/solution.py
+++ b/solution.py
@@ -15,7 +15,7 @@
 bias_two = 1.0 - 0.999**10
 adam_eps = 1e-08
 norm_eps = 1e-07
-highest = lax.Precision.HIGHEST
+matmul_precision = lax.Precision.HIGH
 WIDE = ("tensor", "section")
 
 
@@ -27,7 +27,7 @@
 
 
 def matmul(x, y):
-    return jnp.einsum("...rs,...st->...rt", x, y, precision=highest)
+    return jnp.einsum("...rs,...st->...rt", x, y, precision=matmul_precision)
 
 
 def newton_schulz(target, gram):
@@ -78,8 +78,8 @@
     mats, rows, cols = mlp_grad.shape
     long_side = emb_grad.shape[1]
     rank = emb_basis.shape[1]
-    emb_term = jnp.einsum("dr,dv->rv", emb_basis, emb_grad, precision=highest)
-    mlp_term = jnp.einsum("kdr,kdf->rkf", mlp_basis, mlp_grad, precision=highest)
+    emb_term = jnp.einsum("dr,dv->rv", emb_basis, emb_grad, precision=matmul_precision)
+    mlp_term = jnp.einsum("kdr,kdf->rkf", mlp_basis, mlp_grad, precision=matmul_precision)
     terms = jnp.concatenate([emb_term, mlp_term.reshape(rank, mats * cols)], axis=1)
     share = halving_scatter(terms, WIDE, wide_count)
     emb_share = share[:, :long_side]
@@ -100,15 +100,15 @@
     mlp_piece = gathered[:, long_side:width].reshape(rank, mats, cols)
     emb_projected = gathered[:, width : width + long_side]
     mlp_projected = gathered[:, width + long_side :].reshape(rank, mats, cols)
-    emb_total = jnp.dot(emb_basis, emb_piece, precision=highest)
-    mlp_total = jnp.einsum("kdr,rkf->kdf", mlp_basis, mlp_piece, precision=highest)
-    emb_found = jnp.einsum("dv,rv->dr", emb_grad, emb_projected, precision=highest)
-    mlp_found = jnp.einsum("kdf,rkf->dkr", mlp_grad, mlp_projected, precision=highest)
+    emb_total = jnp.dot(emb_basis, emb_piece, precision=matmul_precision)
+    mlp_total = jnp.einsum("kdr,rkf->kdf", mlp_basis, mlp_piece, precision=matmul_precision)
+    emb_found = jnp.einsum("dv,rv->dr", emb_grad, emb_projected, precision=matmul_precision)
+    mlp_found = jnp.einsum("kdf,rkf->dkr", mlp_grad, mlp_projected, precision=matmul_precision)
     found = jnp.concatenate([emb_found, mlp_found.reshape(rows, mats * rank)], axis=1)
     found = exchange_sum(found, "shard", shard_count)
     every = lax.all_gather(found, WIDE, axis=0, tiled=True)
     every = every.reshape(-1, mats + 1, rank).transpose(1, 0, 2)
-    gram = jnp.einsum("kdr,kds->krs", every, every, precision=highest)
+    gram = jnp.einsum("kdr,kds->krs", every, every, precision=matmul_precision)
     targets = found.reshape(rows, mats + 1, rank).transpose(1, 0, 2)
     basis_new = newton_schulz(targets, gram)
     return (

time: 295 us -> 279 us (0.946)
  matrix products: 51.3 us -> 33.8 us
    dot_general x20, matrix products: 51.3 us -> 33.8 us  [the longest x13 11.4 us: matmul(): return jnp.einsum('...rs,...st->...rt', x, y, precision=matmul_precision)]
where the time goes in v5:
time: 279 us
  waiting for transfers between devices  186 us (67%)
  matrix products  33.8 us (12%)
  local copies, waits for them, and re-layouts  19.3 us (7%)
  starting transfers between devices  16.1 us (6%)
  between operations  14.4 us (5%)
  other arithmetic  9.24 us (3%)
    all_gather x1, waiting for transfers between devices, local(): gathered = lax.all_gather(pieces, WIDE, axis=0, tiled=True)  67.7 us
    ppermute x5, waiting for transfers between devices, halving_scatter(): value = keep + lax.ppermute(send, axis, pairs)  61 us
    all_gather x1, waiting for transfers between devices, local(): every = lax.all_gather(found, WIDE, axis=0, tiled=True)  44.6 us
    ppermute x3, waiting for transfers between devices, exchange_sum(): value = value + lax.ppermute(value, axis, pairs)  12.5 us
    dot_general x13, matrix products, matmul(): return jnp.einsum('...rs,...st->...rt', x, y, precision=matmul_precision)  11.4 us
    ppermute x3, starting transfers between devices, exchange_sum(): value = value + lax.ppermute(value, axis, pairs)  10.3 us
    dot_general x1, matrix products, local(): gram = jnp.einsum('kdr,kds->krs', every, every, precision=matmul_precision)  7.36 us
    ppermute x5, starting transfers between devices, halving_scatter(): value = keep + lax.ppermute(send, axis, pairs)  5.71 us
  transfers between devices with their start and end apart: 10, of which 10 were waited for; matrix products, arithmetic and copies ran while one was open for 3% of the time, Pallas kernels for 0%

profile of v5, /device:TPU:1, one launch (start us, length us, event | category | flops | bytes accessed | tf_op | source)
XLA Modules:
  0.0 278.8 jit_solution(16312789523717316262)
XLA Ops:
  7.2 1.6 convolution_bitcast_fusion.2
  8.9 0.8 copy.57
  9.6 0.9 concatenate.15
  10.6 1.8 fusion.31
  12.4 1.9 copy-done.1
  14.4 1.8 fusion.10
  16.2 3.2 %collective-permute-start = (f32[2,2,2,2,8,4960]{5,4,3,2,1,0:T(8,128)}, f32[2,2,2,2,8,4960]{5,4,3,2,1,0:T(8,128)}, u32[]{:S(2)}, u32[]{:S(2)}) collective-permute-start(f32[2,2,2,2,8,4960]{5,4,3,2,1,0:T(8,128)} %fusion.10), channel_id=1, source_target_pairs={{0,1},{1,0},{2,3},{3,2},{4,5},{5,4},{6,7},{7,6},{8,9},{9,8},{10,11... | collective-permute-start | bytes 7618568 | tf_op jit(solution)/shard_map/ppermute | solution.py:73
  19.4 4.8 %collective-permute-done = f32[2,2,2,2,8,4960]{5,4,3,2,1,0:T(8,128)} collective-permute-done((f32[2,2,2,2,8,4960]{5,4,3,2,1,0:T(8,128)}, f32[2,2,2,2,8,4960]{5,4,3,2,1,0:T(8,128)}, u32[]{:S(2)}, u32[]{:S(2)}) %collective-permute-start) | collective-permute-done | bytes 2539552 | tf_op jit(solution)/shard_map/ppermute | solution.py:73
  24.2 2.8 %fusion.13 = f32[2,2,2,2,8,4960]{5,4,3,2,1,0:T(8,128)S(1)} fusion(f32[2,2,2,2,8,4960]{5,4,3,2,1,0:T(8,128)} %collective-permute-done, s32[]{:T(128)S(6)} %select_n.40, f32[2,2,2,2,2,8,4000]{6,5,4,3,2,1,0:T(8,128)} %bitcast.88, f32[2,2,2,2,2,8,960]{6,5,4,3,2,1,0:T(8,128)} %copy-done.2), kind=kLoop, calls=%fused_computation.20 | loop fusion | flops 1269760 | bytes 10158084 | tf_op jit(solution)/shard_map/add | solution.py:73
  27.0 1.2 dynamic-slice_bitcast_fusion
  28.2 29.6 %collective-permute-done.1 = f32[2,2,2,8,4960]{4,3,2,1,0:T(8,128)} collective-permute-done((f32[2,2,2,8,4960]{4,3,2,1,0:T(8,128)}, f32[2,2,2,8,4960]{4,3,2,1,0:T(8,128)}, u32[]{:S(2)}, u32[]{:S(2)}) %collective-permute-start.1) | collective-permute-done | bytes 1269792 | tf_op jit(solution)/shard_map/ppermute | solution.py:73
  57.7 1.4 bitcast_add_fusion
  59.2 1.1 copy-done.3
  60.3 1.1 collective-permute-start.2
  61.4 15.2 %collective-permute-done.2 = f32[2,2,8,4960]{3,2,1,0:T(8,128)S(1)} collective-permute-done((f32[2,2,8,4960]{3,2,1,0:T(8,128)S(1)}, f32[2,2,8,4960]{3,2,1,0:T(8,128)S(1)}, u32[]{:S(2)}, u32[]{:S(2)}) %collective-permute-start.2) | collective-permute-done | bytes 634912 | tf_op jit(solution)/shard_map/ppermute | solution.py:73
  76.6 1.1 bitcast_add_fusion.1
  77.9 7.0 %collective-permute-done.3 = f32[2,8,4960]{2,1,0:T(8,128)S(1)} collective-permute-done((f32[2,8,4960]{2,1,0:T(8,128)S(1)}, f32[2,8,4960]{2,1,0:T(8,128)S(1)}, u32[]{:S(2)}, u32[]{:S(2)}) %collective-permute-start.3) | collective-permute-done | bytes 317472 | tf_op jit(solution)/shard_map/ppermute | solution.py:73
  84.9 1.3 collective-permute-start.4
  86.2 4.4 %collective-permute-done.4 = f32[8,4960]{1,0:T(8,128)S(1)} collective-permute-done((f32[8,4960]{1,0:T(8,128)S(1)}, f32[8,4960]{1,0:T(8,128)S(1)}, u32[]{:S(2)}, u32[]{:S(2)}) %collective-permute-start.4) | collective-permute-done | bytes 158752 | tf_op jit(solution)/shard_map/ppermute | solution.py:73
  91.1 0.8 add_divide_fusion
  91.8 0.8 concatenate.17
  92.8 67.7 %all-gather.4.cloned.1.call-done = f32[256,9920]{1,0:T(8,128)} async-done(((f32[8,9920]{1,0:T(8,128)}), f32[256,9920]{1,0:T(8,128)}) %all-gather.4.cloned.1.call-update) | async-done | bytes 10158096 | tf_op jit(solution)/shard_map/all_gather | solution.py:97
  160.4 1.9 fusion.28
  162.4 1.3 copy.61
  163.7 1.6 convolution_bitcast_fusion.4
  165.4 4.6 %fusion.14 = f32[30,256]{1,0:T(8,128)S(1)} fusion(f32[30,4000]{1,0:T(8,128)S(1)} %copy-done, f32[256,9920]{1,0:T(8,128)} %all-gather.4.cloned.1.call-done), kind=kOutput, calls=%fused_computation.26 | convolution fusion | flops 184320000 | bytes 4705024 | tf_op jit(solution)/shard_map/dv,rv->dr/dot_general | solution.py:105
  170.0 1.4 collective-permute-start.5
  171.4 3.5 %collective-permute-done.5 = f32[30,1024]{1,0:T(8,128)S(1)} collective-permute-done((f32[30,1024]{1,0:T(8,128)S(1)}, f32[30,1024]{1,0:T(8,128)S(1)}, u32[]{:S(2)}, u32[]{:S(2)}) %collective-permute-start.5) | collective-permute-done | bytes 122912 | tf_op jit(solution)/shard_map/ppermute | solution.py:55
  174.9 2.4 collective-permute-start.6
  177.3 5.9 %collective-permute-done.6 = f32[30,1024]{1,0:T(8,128)S(1)} collective-permute-done((f32[30,1024]{1,0:T(8,128)S(1)}, f32[30,1024]{1,0:T(8,128)S(1)}, u32[]{:S(2)}, u32[]{:S(2)}) %collective-permute-start.6) | collective-permute-done | bytes 122912 | tf_op jit(solution)/shard_map/ppermute | solution.py:55
  183.2 6.6 %collective-permute-start.7 = (f32[30,1024]{1,0:T(8,128)S(1)}, f32[30,1024]{1,0:T(8,128)S(1)}, u32[]{:S(2)}, u32[]{:S(2)}) collective-permute-start(f32[30,1024]{1,0:T(8,128)S(1)} %add.135), channel_id=1, source_target_pairs={{0,128},{32,160},{64,192},{96,224},{128,0},{160,32},{192,64},{224,... | collective-permute-start | bytes 368648 | tf_op jit(solution)/shard_map/ppermute | solution.py:55
  189.8 3.1 %collective-permute-done.7 = f32[30,1024]{1,0:T(8,128)S(1)} collective-permute-done((f32[30,1024]{1,0:T(8,128)S(1)}, f32[30,1024]{1,0:T(8,128)S(1)}, u32[]{:S(2)}, u32[]{:S(2)}) %collective-permute-start.7) | collective-permute-done | bytes 122912 | tf_op jit(solution)/shard_map/ppermute | solution.py:55
  192.9 0.7 add.136
  195.4 1.2 convolution_bitcast_fusion.3
  196.5 4.2 %convolution_bitcast_fusion.1 = f32[30,4000]{1,0:T(8,128)} fusion(f32[30,256]{1,0:T(8,128)S(1)} %copy-done.7, f32[256,9920]{1,0:T(8,128)} %all-gather.4.cloned.1.call-done), kind=kOutput, calls=%fused_computation.9 | convolution fusion | flops 184320000 | bytes 4705024 | tf_op jit(solution)/shard_map/dot_general | solution.py:103
  200.8 44.6 %all-gather.6.cloned.1.call-done = f32[32,30,1024]{2,1,0:T(8,128)} async-done(((f32[1,30,1024]{2,1,0:T(8,128)}), f32[32,30,1024]{2,1,0:T(8,128)}) %all-gather.6.cloned.1.call-update) | async-done | bytes 3932176 | tf_op jit(solution)/shard_map/all_gather | solution.py:109
  245.4 5.6 %reshape.56 = f32[960,4,256]{2,1,0:T(4,128)} reshape(f32[32,30,1024]{2,1,0:T(8,128)} %all-gather.6.cloned.1.call-done) | data formatting | bytes 7864320 | tf_op jit(solution)/shard_map/reshape | solution.py:110
  251.0 7.4 %select_reduce_fusion = (f32[4]{0:T(128)S(1)}, f32[4,256,256]{2,1,0:T(8,128)S(1)}) fusion(pred[256,256]{1,0:T(8,128)(4,1)S(1)} %iota_compare_fusion, f32[960,4,256]{2,1,0:T(4,128)} %reshape.56), kind=kOutput, calls=%fused_computation.27 | convolution fusion | flops 1510473728 | bytes 5046288 | tf_op jit(solution)/shard_map/kdr,kds->krs/dot_general | solution.py:111
  258.7 11.3 %while.13 = (s32[]{:T(128)}, f32[4,256,256]{2,1,0:T(8,128)S(1)}, f32[4,256,256]{1,2,0:T(8,128)S(1)}, f32[256,256]{1,0:T(8,128)S(1)}, s32[]{:T(128)}) while((s32[]{:T(128)}, f32[4,256,256]{2,1,0:T(8,128)S(1)}, f32[4,256,256]{1,2,0:T(8,128)S(1)}, f32[256,256]{1,0:T(8,128)S(1)}, s32[]{:T(128)}) %tuple.35), condition=%wide.region_2.3_spmd.clone, body=%wide.region_1.2_spmd.clone.sunk | while | flops 1611726848 | bytes 14417981 | solution.py:44
  258.7 0.8 fusion.70
  259.5 1.1 fusion.71
  261.3 1.1 convolution_bitcast_fusion.6
  262.5 0.8 fusion.70
  263.3 1.1 fusion.71
  265.1 1.1 convolution_bitcast_fusion.6
  266.3 0.8 fusion.70
  267.0 1.1 fusion.71
  268.9 1.1 convolution_bitcast_fusion.6
  (66 shorter events, 7.2 us)
Async XLA Ops:
  7.2 3.4 %copy-start = (f32[30,4000]{1,0:T(8,128)S(1)}, f32[30,4000]{1,0:T(8,128)}, u32[]{:S(2)}) copy-start(f32[30,4000]{1,0:T(8,128)} %param.10) | copy-start | bytes 1440004
  7.2 3.4 %copy-start.7 = (f32[30,256]{1,0:T(8,128)S(1)}, f32[30,256]{1,0:T(8,128)}, u32[]{:S(2)}) copy-start(f32[30,256]{1,0:T(8,128)} %param.12) | copy-start | bytes 92164
  7.2 153.3 %all-gather.4.cloned.1.call-start = ((), (), s32[]{:S(2)}) async-start(), calls=%async_computation | async-start | bytes 10543104 | tf_op jit(solution)/shard_map/all_gather | solution.py:97
  10.5 5.7 %copy-start.2 = (f32[2,2,2,2,2,8,960]{6,5,4,3,2,1,0:T(8,128)}, f32[2,2,2,2,2,8,960]{6,5,4,3,2,1,0:T(8,128)S(1)}, u32[]{:S(2)}) copy-start(f32[2,2,2,2,2,8,960]{6,5,4,3,2,1,0:T(8,128)S(1)} %concatenate.15) | copy-start | bytes 2949124
  12.4 2.0 copy-start.1
  16.2 8.0 %collective-permute-start = (f32[2,2,2,2,8,4960]{5,4,3,2,1,0:T(8,128)}, f32[2,2,2,2,8,4960]{5,4,3,2,1,0:T(8,128)}, u32[]{:S(2)}, u32[]{:S(2)}) collective-permute-start(f32[2,2,2,2,8,4960]{5,4,3,2,1,0:T(8,128)} %fusion.10), channel_id=1, source_target_pairs={{0,1},{1,0},{2,3},{3,2},{4,5},{5,4},{6,7},{7,6},{8,9},{9,8},{10,11... | collective-permute-start | bytes 7618568 | tf_op jit(solution)/shard_map/ppermute | solution.py:73
  28.1 29.6 %collective-permute-start.1 = (f32[2,2,2,8,4960]{4,3,2,1,0:T(8,128)}, f32[2,2,2,8,4960]{4,3,2,1,0:T(8,128)}, u32[]{:S(2)}, u32[]{:S(2)}) collective-permute-start(f32[2,2,2,8,4960]{4,3,2,1,0:T(8,128)} %dynamic-slice_bitcast_fusion), channel_id=1, source_target_pairs={{0,2},{1,3},{2,0},{3,1},{4,6},{5,7},{6,4},{7,5},{8,10},{9,11},{10,... | collective-permute-start | bytes 3809288 | tf_op jit(solution)/shard_map/ppermute | solution.py:73
  28.2 62.7 %copy-start.10 = (f32[8,3,320]{2,0,1:T(8,128)S(1)}, f32[8,3,320]{2,0,1:T(8,128)}, u32[]{:S(2)}) copy-start(f32[8,3,320]{2,0,1:T(8,128)} %param.16) | copy-start | bytes 92164
  28.2 62.7 %copy-start.11 = (f32[8,3,320]{2,0,1:T(8,128)S(1)}, f32[8,3,320]{2,0,1:T(8,128)}, u32[]{:S(2)}) copy-start(f32[8,3,320]{2,0,1:T(8,128)} %param.17) | copy-start | bytes 92164
  59.2 1.1 copy-start.3
  60.2 30.8 %copy-start.8 = (f32[8,4000]{1,0:T(8,128)S(1)}, f32[8,4000]{1,0:T(8,128)}, u32[]{:S(2)}) copy-start(f32[8,4000]{1,0:T(8,128)} %param.14) | copy-start | bytes 384004
  60.2 30.8 %copy-start.9 = (f32[8,4000]{1,0:T(8,128)S(1)}, f32[8,4000]{1,0:T(8,128)}, u32[]{:S(2)}) copy-start(f32[8,4000]{1,0:T(8,128)} %param.15) | copy-start | bytes 384004
  60.3 16.3 %collective-permute-start.2 = (f32[2,2,8,4960]{3,2,1,0:T(8,128)S(1)}, f32[2,2,8,4960]{3,2,1,0:T(8,128)S(1)}, u32[]{:S(2)}, u32[]{:S(2)}) collective-permute-start(f32[2,2,8,4960]{3,2,1,0:T(8,128)S(1)} %dynamic-slice_bitcast_fusion.1), channel_id=1, source_target_pairs={{0,4},{1,5},{2,6},{3,7},{4,0},{5,1},{6,2},{7,3},{8,12},{9,13},{10,... | collective-permute-start | bytes 1904648 | tf_op jit(solution)/shard_map/ppermute | solution.py:73
  77.8 7.1 %collective-permute-start.3 = (f32[2,8,4960]{2,1,0:T(8,128)S(1)}, f32[2,8,4960]{2,1,0:T(8,128)S(1)}, u32[]{:S(2)}, u32[]{:S(2)}) collective-permute-start(f32[2,8,4960]{2,1,0:T(8,128)S(1)} %dynamic-slice_bitcast_fusion.2), channel_id=1, source_target_pairs={{0,8},{1,9},{2,10},{3,11},{4,12},{5,13},{6,14},{7,15},{8,0},{9,1},... | collective-permute-start | bytes 952328 | tf_op jit(solution)/shard_map/ppermute | solution.py:73
  84.9 5.7 %collective-permute-start.4 = (f32[8,4960]{1,0:T(8,128)S(1)}, f32[8,4960]{1,0:T(8,128)S(1)}, u32[]{:S(2)}, u32[]{:S(2)}) collective-permute-start(f32[8,4960]{1,0:T(8,128)S(1)} %dynamic-slice_bitcast_fusion.3), channel_id=1, source_target_pairs={{0,16},{1,17},{2,18},{3,19},{4,20},{5,21},{6,22},{7,23},{8,24},{9,... | collective-permute-start | bytes 476168 | tf_op jit(solution)/shard_map/ppermute | solution.py:73
  91.1 72.6 %copy-start.5 = (f32[3,30,320]{2,1,0:T(8,128)S(1)}, f32[3,30,320]{2,1,0:T(8,128)}, u32[]{:S(2)}) copy-start(f32[3,30,320]{2,1,0:T(8,128)} %param.11) | copy-start | bytes 345604
  92.7 152.7 %all-gather.6.cloned.1.call-start = ((), (), s32[]{:S(2)}) async-start(), calls=%async_computation.1 | async-start | bytes 4325376 | tf_op jit(solution)/shard_map/all_gather | solution.py:109
  165.4 30.0 %copy-start.6 = (f32[3,30,256]{2,1,0:T(8,128)S(1)}, f32[3,30,256]{2,1,0:T(8,128)}, u32[]{:S(2)}) copy-start(f32[3,30,256]{2,1,0:T(8,128)} %param.13) | copy-start | bytes 276484
  170.0 4.9 %collective-permute-start.5 = (f32[30,1024]{1,0:T(8,128)S(1)}, f32[30,1024]{1,0:T(8,128)S(1)}, u32[]{:S(2)}, u32[]{:S(2)}) collective-permute-start(f32[30,1024]{1,0:T(8,128)S(1)} %pad_maximum_fusion), channel_id=1, source_target_pairs={{0,32},{32,0},{64,96},{96,64},{128,160},{160,128},{192,224},{224,1... | collective-permute-start | bytes 368648 | tf_op jit(solution)/shard_map/ppermute | solution.py:55
  174.9 8.2 %collective-permute-start.6 = (f32[30,1024]{1,0:T(8,128)S(1)}, f32[30,1024]{1,0:T(8,128)S(1)}, u32[]{:S(2)}, u32[]{:S(2)}) collective-permute-start(f32[30,1024]{1,0:T(8,128)S(1)} %fusion.23), channel_id=1, source_target_pairs={{0,64},{32,96},{64,0},{96,32},{128,192},{160,224},{192,128},{224,1... | collective-permute-start | bytes 368648 | tf_op jit(solution)/shard_map/ppermute | solution.py:55
  183.2 9.7 %collective-permute-start.7 = (f32[30,1024]{1,0:T(8,128)S(1)}, f32[30,1024]{1,0:T(8,128)S(1)}, u32[]{:S(2)}, u32[]{:S(2)}) collective-permute-start(f32[30,1024]{1,0:T(8,128)S(1)} %add.135), channel_id=1, source_target_pairs={{0,128},{32,160},{64,192},{96,224},{128,0},{160,32},{192,64},{224,... | collective-permute-start | bytes 368648 | tf_op jit(solution)/shard_map/ppermute | solution.py:55
  195.0 5.7 %copy-start.4 = (f32[30,1024]{1,0:T(8,128)S(1)}, f32[30,1024]{1,0:T(8,128)}, u32[]{:S(2)}) copy-start(f32[30,1024]{1,0:T(8,128)} %add.136) | copy-start | bytes 368644
Sparse Core Ops, SparseCore 0:
  92.8 67.5 all-gather.3
  193.7 51.6 all-gather.5

commit v6 on v5

--- a/solution.py
+++ b/solution.py
@@ -57,31 +57,45 @@
     return value
 
 
-def halving_scatter(value, axis, count):
+def halving_scatter(value, axis, count, split_at):
     if count & (count - 1):
         return lax.psum_scatter(value, axis, scatter_dimension=0, tiled=True)
     bits = count.bit_length() - 1
     block = value.shape[0] // count
     index = lax.axis_index(axis)
     value = value.reshape((2,) * bits + (block,) + value.shape[1:])
-    for bit in range(bits):
-        own = (index >> bit) & 1
-        axis_at = bits - 1 - bit
-        keep = lax.dynamic_index_in_dim(value, own, axis_at, keepdims=False)
-        send = lax.dynamic_index_in_dim(value, 1 - own, axis_at, keepdims=False)
-        pairs = [(place, place ^ (1 << bit)) for place in range(count)]
-        value = keep + lax.ppermute(send, axis, pairs)
-    return value
+    value, remaining = halving_step(value, list(range(bits - 1, -1, -1)), 0, axis, count, index)
+    if bits < 2:
+        return value
+    cut = value.shape[-1] // 2
+    low = list(range(1, split_at))
+    high = list(range(split_at, bits))
+    first, first_left = value[..., :cut], remaining
+    second, second_left = value[..., cut:], remaining
+    for bit_a, bit_b in zip(low + high, high + low):
+        first, first_left = halving_step(first, first_left, bit_a, axis, count, index)
+        second, second_left = halving_step(second, second_left, bit_b, axis, count, index)
+    return jnp.concatenate([first, second], axis=-1)
 
 
-def local(shard_count, wide_count, emb_grad, mlp_grad, emb_basis, mlp_basis, emb_first, emb_second, mlp_first, mlp_second):
+def halving_step(value, remaining, bit, axis, count, index):
+    own = (index >> bit) & 1
+    axis_at = remaining.index(bit)
+    keep = lax.dynamic_index_in_dim(value, own, axis_at, keepdims=False)
+    send = lax.dynamic_index_in_dim(value, 1 - own, axis_at, keepdims=False)
+    pairs = [(place, place ^ (1 << bit)) for place in range(count)]
+    left = [other for other in remaining if other != bit]
+    return keep + lax.ppermute(send, axis, pairs), left
+
+
+def local(shard_count, wide_count, split_at, emb_grad, mlp_grad, emb_basis, mlp_basis, emb_first, emb_second, mlp_first, mlp_second):
     mats, rows, cols = mlp_grad.shape
     long_side = emb_grad.shape[1]
     rank = emb_basis.shape[1]
     emb_term = jnp.einsum("dr,dv->rv", emb_basis, emb_grad, precision=matmul_precision)
     mlp_term = jnp.einsum("kdr,kdf->rkf", mlp_basis, mlp_grad, precision=matmul_precision)
     terms = jnp.concatenate([emb_term, mlp_term.reshape(rank, mats * cols)], axis=1)
-    share = halving_scatter(terms, WIDE, wide_count)
+    share = halving_scatter(terms, WIDE, wide_count, split_at)
     emb_share = share[:, :long_side]
     mlp_share = share[:, long_side : long_side + mats * cols].reshape(-1, mats, cols)
     emb_first_new, emb_second_new, emb_direction = adam_moments(emb_first, emb_second, emb_share)
@@ -135,7 +149,12 @@
         P(WIDE, None, "shard"),
     )
     return jax.shard_map(
-        functools.partial(local, mesh.shape["shard"], mesh.shape["tensor"] * mesh.shape["section"]),
+        functools.partial(
+            local,
+            mesh.shape["shard"],
+            mesh.shape["tensor"] * mesh.shape["section"],
+            (mesh.shape["section"]).bit_length() - 1,
+        ),
         mesh=mesh,
         in_specs=placed,
         out_specs=(

time: 279 us -> 256 us (0.918)
  waiting for transfers between devices: 186 us -> 157 us
  starting transfers between devices: 16.1 us -> 23 us
    ppermute x5 -> x9, waiting for transfers between devices: 61 us -> 32.4 us  [halving_step(): return (keep + lax.ppermute(send, axis, pairs), left)]
    ppermute x5 -> x9, starting transfers between devices: 5.71 us -> 12.6 us  [halving_step(): return (keep + lax.ppermute(send, axis, pairs), left)]
  transfers between devices with their start and end apart: 10 -> 14, of which waited for: 10 -> 12; matrix products, arithmetic and copies ran while one was open for 3% -> 4% of each run, Pallas kernels for 0% -> 0%
where the time goes in v6:
time: 256 us; the launch traced here: 255 us
  waiting for transfers between devices  157 us (61%)
  matrix products  33.7 us (13%)
  starting transfers between devices  23 us (9%)
  local copies, waits for them, and re-layouts  18.6 us (7%)
  between operations  14.4 us (6%)
  other arithmetic  7.91 us (3%)
    all_gather x1, waiting for transfers between devices, local(): gathered = lax.all_gather(pieces, WIDE, axis=0, tiled=True)  67.8 us
    all_gather x1, waiting for transfers between devices, local(): every = lax.all_gather(found, WIDE, axis=0, tiled=True)  44.6 us
    ppermute x9, waiting for transfers between devices, halving_step(): return (keep + lax.ppermute(send, axis, pairs), left)  32.4 us
    ppermute x9, starting transfers between devices, halving_step(): return (keep + lax.ppermute(send, axis, pairs), left)  12.6 us
    ppermute x3, waiting for transfers between devices, exchange_sum(): value = value + lax.ppermute(value, axis, pairs)  12.5 us
    dot_general x13, matrix products, matmul(): return jnp.einsum('...rs,...st->...rt', x, y, precision=matmul_precision)  11.4 us
    ppermute x3, starting transfers between devices, exchange_sum(): value = value + lax.ppermute(value, axis, pairs)  10.2 us
    dot_general x1, matrix products, local(): gram = jnp.einsum('kdr,kds->krs', every, every, precision=matmul_precision)  7.36 us
  transfers between devices with their start and end apart: 14, of which 12 were waited for; matrix products, arithmetic and copies ran while one was open for 4% of the time, Pallas kernels for 0%

profile of v6, /device:TPU:1, one launch (start us, length us, event | category | flops | bytes accessed | tf_op | source)
XLA Modules:
  0.0 255.2 jit_solution(8757263816328494285)
XLA Ops:
  7.2 1.6 convolution_bitcast_fusion.2
  8.9 0.8 copy.59
  9.6 0.9 concatenate.19
  10.6 1.8 fusion.32
  12.4 2.0 copy-done.1
  14.4 1.8 fusion.10
  16.2 3.2 %collective-permute-start = (f32[2,2,2,2,8,4960]{5,4,3,2,1,0:T(8,128)}, f32[2,2,2,2,8,4960]{5,4,3,2,1,0:T(8,128)}, u32[]{:S(2)}, u32[]{:S(2)}) collective-permute-start(f32[2,2,2,2,8,4960]{5,4,3,2,1,0:T(8,128)} %fusion.10), channel_id=1, source_target_pairs={{0,1},{1,0},{2,3},{3,2},{4,5},{5,4},{6,7},{7,6},{8,9},{9,8},{10,11... | collective-permute-start | bytes 7618568 | tf_op jit(solution)/shard_map/ppermute | solution.py:88
  19.4 4.8 %collective-permute-done = f32[2,2,2,2,8,4960]{5,4,3,2,1,0:T(8,128)} collective-permute-done((f32[2,2,2,2,8,4960]{5,4,3,2,1,0:T(8,128)}, f32[2,2,2,2,8,4960]{5,4,3,2,1,0:T(8,128)}, u32[]{:S(2)}, u32[]{:S(2)}) %collective-permute-start) | collective-permute-done | bytes 2539552 | tf_op jit(solution)/shard_map/ppermute | solution.py:88
  24.2 2.7 %fusion.13 = f32[2,2,2,2,8,4960]{5,4,3,2,1,0:T(8,128)S(1)} fusion(f32[2,2,2,2,8,4960]{5,4,3,2,1,0:T(8,128)} %collective-permute-done, s32[]{:T(128)S(6)} %select_n.50, f32[2,2,2,2,2,8,4000]{6,5,4,3,2,1,0:T(8,128)} %bitcast.104, f32[2,2,2,2,2,8,960]{6,5,4,3,2,1,0:T(8,128)S(1)} %concatenate.19), kind=kLoop, calls=%fused_computation.20 | loop fusion | flops 1269760 | bytes 10158084 | tf_op jit(solution)/shard_map/add | solution.py:88
  27.4 0.9 dynamic-slice_bitcast_fusion
  28.3 0.9 collective-permute-start.1
  29.2 15.3 %collective-permute-done.5 = f32[2,2,2,8,2480]{4,3,2,1,0:T(8,128)} collective-permute-done((f32[2,2,2,8,2480]{4,3,2,1,0:T(8,128)}, f32[2,2,2,8,2480]{4,3,2,1,0:T(8,128)}, u32[]{:S(2)}, u32[]{:S(2)}) %collective-permute-start.5) | collective-permute-done | bytes 634912 | tf_op jit(solution)/shard_map/ppermute | solution.py:88
  44.5 1.2 bitcast_add_fusion
  45.7 1.3 collective-permute-start.6
  47.1 2.8 %collective-permute-start.2 = (f32[2,2,8,2480]{3,2,1,0:T(8,128)S(1)}, f32[2,2,8,2480]{3,2,1,0:T(8,128)S(1)}, u32[]{:S(2)}, u32[]{:S(2)}) collective-permute-start(f32[2,2,8,2480]{3,2,1,0:T(8,128)S(1)} %dynamic-slice_bitcast_fusion.3), channel_id=1, source_target_pairs={{0,4},{1,5},{2,6},{3,7},{4,0},{5,1},{6,2},{7,3},{8,12},{9,13},{10,... | collective-permute-start | bytes 952328 | tf_op jit(solution)/shard_map/ppermute | solution.py:88
  50.0 5.4 %collective-permute-done.6 = f32[2,2,8,2480]{3,2,1,0:T(8,128)S(1)} collective-permute-done((f32[2,2,8,2480]{3,2,1,0:T(8,128)S(1)}, f32[2,2,8,2480]{3,2,1,0:T(8,128)S(1)}, u32[]{:S(2)}, u32[]{:S(2)}) %collective-permute-start.6) | collective-permute-done | bytes 317472 | tf_op jit(solution)/shard_map/ppermute | solution.py:88
  55.5 1.0 collective-permute-done.2
  57.1 3.0 %collective-permute-done.7 = f32[2,8,2480]{2,1,0:T(8,128)S(1)} collective-permute-done((f32[2,8,2480]{2,1,0:T(8,128)S(1)}, f32[2,8,2480]{2,1,0:T(8,128)S(1)}, u32[]{:S(2)}, u32[]{:S(2)}) %collective-permute-start.7) | collective-permute-done | bytes 158752 | tf_op jit(solution)/shard_map/ppermute | solution.py:88
  60.1 2.3 collective-permute-start.8
  62.5 1.5 collective-permute-start.4
  63.9 1.0 collective-permute-done.8
  65.3 2.0 collective-permute-done.4
  67.4 0.8 add_divide_fusion
  68.2 0.8 concatenate.22
  69.3 67.8 %all-gather.4.cloned.1.call-done = f32[256,9920]{1,0:T(8,128)} async-done(((f32[8,9920]{1,0:T(8,128)}), f32[256,9920]{1,0:T(8,128)}) %all-gather.4.cloned.1.call-update) | async-done | bytes 10158096 | tf_op jit(solution)/shard_map/all_gather | solution.py:111
  137.1 1.9 fusion.28
  139.0 1.3 copy.63
  140.3 1.6 convolution_bitcast_fusion.4
  142.0 4.6 %fusion.14 = f32[30,256]{1,0:T(8,128)S(1)} fusion(f32[30,4000]{1,0:T(8,128)S(1)} %copy-done, f32[256,9920]{1,0:T(8,128)} %all-gather.4.cloned.1.call-done), kind=kOutput, calls=%fused_computation.24 | convolution fusion | flops 184320000 | bytes 4705024 | tf_op jit(solution)/shard_map/dv,rv->dr/dot_general | solution.py:119
  146.7 1.4 collective-permute-start.9
  148.0 3.5 %collective-permute-done.9 = f32[30,1024]{1,0:T(8,128)S(1)} collective-permute-done((f32[30,1024]{1,0:T(8,128)S(1)}, f32[30,1024]{1,0:T(8,128)S(1)}, u32[]{:S(2)}, u32[]{:S(2)}) %collective-permute-start.9) | collective-permute-done | bytes 122912 | tf_op jit(solution)/shard_map/ppermute | solution.py:55
  151.6 2.4 collective-permute-start.10
  153.9 5.9 %collective-permute-done.10 = f32[30,1024]{1,0:T(8,128)S(1)} collective-permute-done((f32[30,1024]{1,0:T(8,128)S(1)}, f32[30,1024]{1,0:T(8,128)S(1)}, u32[]{:S(2)}, u32[]{:S(2)}) %collective-permute-start.10) | collective-permute-done | bytes 122912 | tf_op jit(solution)/shard_map/ppermute | solution.py:55
  159.8 6.4 %collective-permute-start.11 = (f32[30,1024]{1,0:T(8,128)S(1)}, f32[30,1024]{1,0:T(8,128)S(1)}, u32[]{:S(2)}, u32[]{:S(2)}) collective-permute-start(f32[30,1024]{1,0:T(8,128)S(1)} %add.161), channel_id=1, source_target_pairs={{0,128},{32,160},{64,192},{96,224},{128,0},{160,32},{192,64},{224,... | collective-permute-start | bytes 368648 | tf_op jit(solution)/shard_map/ppermute | solution.py:55
  166.2 3.1 %collective-permute-done.11 = f32[30,1024]{1,0:T(8,128)S(1)} collective-permute-done((f32[30,1024]{1,0:T(8,128)S(1)}, f32[30,1024]{1,0:T(8,128)S(1)}, u32[]{:S(2)}, u32[]{:S(2)}) %collective-permute-start.11) | collective-permute-done | bytes 122912 | tf_op jit(solution)/shard_map/ppermute | solution.py:55
  171.8 1.2 convolution_bitcast_fusion.3
  173.0 4.2 %convolution_bitcast_fusion.1 = f32[30,4000]{1,0:T(8,128)} fusion(f32[30,256]{1,0:T(8,128)S(1)} %copy-done.5, f32[256,9920]{1,0:T(8,128)} %all-gather.4.cloned.1.call-done), kind=kOutput, calls=%fused_computation.9 | convolution fusion | flops 184320000 | bytes 4705024 | tf_op jit(solution)/shard_map/dot_general | solution.py:117
  177.3 44.6 %all-gather.6.cloned.1.call-done = f32[32,30,1024]{2,1,0:T(8,128)} async-done(((f32[1,30,1024]{2,1,0:T(8,128)}), f32[32,30,1024]{2,1,0:T(8,128)}) %all-gather.6.cloned.1.call-update) | async-done | bytes 3932176 | tf_op jit(solution)/shard_map/all_gather | solution.py:123
  221.9 5.6 %reshape.56 = f32[960,4,256]{2,1,0:T(4,128)} reshape(f32[32,30,1024]{2,1,0:T(8,128)} %all-gather.6.cloned.1.call-done) | data formatting | bytes 7864320 | tf_op jit(solution)/shard_map/reshape | solution.py:124
  227.5 7.4 %select_reduce_fusion = (f32[4]{0:T(128)S(1)}, f32[4,256,256]{2,1,0:T(8,128)S(1)}) fusion(pred[256,256]{1,0:T(8,128)(4,1)S(1)} %iota_compare_fusion, f32[960,4,256]{2,1,0:T(4,128)} %reshape.56), kind=kOutput, calls=%fused_computation.25 | convolution fusion | flops 1510473728 | bytes 5046288 | tf_op jit(solution)/shard_map/kdr,kds->krs/dot_general | solution.py:125
  235.2 11.3 %while.13 = (s32[]{:T(128)}, f32[4,256,256]{2,1,0:T(8,128)S(1)}, f32[4,256,256]{1,2,0:T(8,128)S(1)}, f32[256,256]{1,0:T(8,128)S(1)}, s32[]{:T(128)}) while((s32[]{:T(128)}, f32[4,256,256]{2,1,0:T(8,128)S(1)}, f32[4,256,256]{1,2,0:T(8,128)S(1)}, f32[256,256]{1,0:T(8,128)S(1)}, s32[]{:T(128)}) %tuple.36), condition=%wide.region_2.3_spmd.clone, body=%wide.region_1.2_spmd.clone.sunk | while | flops 1611726848 | bytes 14417981 | solution.py:44
  235.2 0.8 fusion.71
  236.0 1.1 fusion.72
  237.8 1.1 convolution_bitcast_fusion.6
  239.7 1.1 fusion.72
  241.6 1.1 convolution_bitcast_fusion.6
  243.5 1.1 fusion.72
  245.3 1.1 convolution_bitcast_fusion.6
  (79 shorter events, 10.7 us)
Async XLA Ops:
  7.2 3.4 %copy-start = (f32[30,4000]{1,0:T(8,128)S(1)}, f32[30,4000]{1,0:T(8,128)}, u32[]{:S(2)}) copy-start(f32[30,4000]{1,0:T(8,128)} %param.10) | copy-start | bytes 1440004
  7.2 3.4 %copy-start.5 = (f32[30,256]{1,0:T(8,128)S(1)}, f32[30,256]{1,0:T(8,128)}, u32[]{:S(2)}) copy-start(f32[30,256]{1,0:T(8,128)} %param.12) | copy-start | bytes 92164
  7.2 129.9 %all-gather.4.cloned.1.call-start = ((), (), s32[]{:S(2)}) async-start(), calls=%async_computation | async-start | bytes 10543104 | tf_op jit(solution)/shard_map/all_gather | solution.py:111
  12.4 2.0 copy-start.1
  16.2 8.0 %collective-permute-start = (f32[2,2,2,2,8,4960]{5,4,3,2,1,0:T(8,128)}, f32[2,2,2,2,8,4960]{5,4,3,2,1,0:T(8,128)}, u32[]{:S(2)}, u32[]{:S(2)}) collective-permute-start(f32[2,2,2,2,8,4960]{5,4,3,2,1,0:T(8,128)} %fusion.10), channel_id=1, source_target_pairs={{0,1},{1,0},{2,3},{3,2},{4,5},{5,4},{6,7},{7,6},{8,9},{9,8},{10,11... | collective-permute-start | bytes 7618568 | tf_op jit(solution)/shard_map/ppermute | solution.py:88
  28.2 16.2 %collective-permute-start.5 = (f32[2,2,2,8,2480]{4,3,2,1,0:T(8,128)}, f32[2,2,2,8,2480]{4,3,2,1,0:T(8,128)}, u32[]{:S(2)}, u32[]{:S(2)}) collective-permute-start(f32[2,2,2,8,2480]{4,3,2,1,0:T(8,128)} %dynamic-slice_bitcast_fusion), channel_id=1, source_target_pairs={{0,8},{1,9},{2,10},{3,11},{4,12},{5,13},{6,14},{7,15},{8,0},{9,1},... | collective-permute-start | bytes 1904648 | tf_op jit(solution)/shard_map/ppermute | solution.py:88
  28.3 18.7 %collective-permute-start.1 = (f32[2,2,2,8,2480]{4,3,2,1,0:T(8,128)S(1)}, f32[2,2,2,8,2480]{4,3,2,1,0:T(8,128)S(1)}, u32[]{:S(2)}, u32[]{:S(2)}) collective-permute-start(f32[2,2,2,8,2480]{4,3,2,1,0:T(8,128)S(1)} %dynamic-slice_bitcast_fusion.1), channel_id=1, source_target_pairs={{0,2},{1,3},{2,0},{3,1},{4,6},{5,7},{6,4},{7,5},{8,10},{9,11},{10,... | collective-permute-start | bytes 1904648 | tf_op jit(solution)/shard_map/ppermute | solution.py:88
  45.6 19.5 %copy-start.8 = (f32[8,3,320]{2,0,1:T(8,128)S(1)}, f32[8,3,320]{2,0,1:T(8,128)}, u32[]{:S(2)}) copy-start(f32[8,3,320]{2,0,1:T(8,128)} %param.16) | copy-start | bytes 92164
  45.7 19.5 %copy-start.9 = (f32[8,3,320]{2,0,1:T(8,128)S(1)}, f32[8,3,320]{2,0,1:T(8,128)}, u32[]{:S(2)}) copy-start(f32[8,3,320]{2,0,1:T(8,128)} %param.17) | copy-start | bytes 92164
  45.7 21.6 %copy-start.6 = (f32[8,4000]{1,0:T(8,128)S(1)}, f32[8,4000]{1,0:T(8,128)}, u32[]{:S(2)}) copy-start(f32[8,4000]{1,0:T(8,128)} %param.14) | copy-start | bytes 384004
  45.7 21.6 %copy-start.7 = (f32[8,4000]{1,0:T(8,128)S(1)}, f32[8,4000]{1,0:T(8,128)}, u32[]{:S(2)}) copy-start(f32[8,4000]{1,0:T(8,128)} %param.15) | copy-start | bytes 384004
  45.7 9.6 %collective-permute-start.6 = (f32[2,2,8,2480]{3,2,1,0:T(8,128)S(1)}, f32[2,2,8,2480]{3,2,1,0:T(8,128)S(1)}, u32[]{:S(2)}, u32[]{:S(2)}) collective-permute-start(f32[2,2,8,2480]{3,2,1,0:T(8,128)S(1)} %dynamic-slice_bitcast_fusion.2), channel_id=1, source_target_pairs={{0,16},{1,17},{2,18},{3,19},{4,20},{5,21},{6,22},{7,23},{8,24},{9,... | collective-permute-start | bytes 952328 | tf_op jit(solution)/shard_map/ppermute | solution.py:88
  47.1 9.4 %collective-permute-start.2 = (f32[2,2,8,2480]{3,2,1,0:T(8,128)S(1)}, f32[2,2,8,2480]{3,2,1,0:T(8,128)S(1)}, u32[]{:S(2)}, u32[]{:S(2)}) collective-permute-start(f32[2,2,8,2480]{3,2,1,0:T(8,128)S(1)} %dynamic-slice_bitcast_fusion.3), channel_id=1, source_target_pairs={{0,4},{1,5},{2,6},{3,7},{4,0},{5,1},{6,2},{7,3},{8,12},{9,13},{10,... | collective-permute-start | bytes 952328 | tf_op jit(solution)/shard_map/ppermute | solution.py:88
  55.4 4.6 %collective-permute-start.7 = (f32[2,8,2480]{2,1,0:T(8,128)S(1)}, f32[2,8,2480]{2,1,0:T(8,128)S(1)}, u32[]{:S(2)}, u32[]{:S(2)}) collective-permute-start(f32[2,8,2480]{2,1,0:T(8,128)S(1)} %dynamic-slice_bitcast_fusion.4), channel_id=1, source_target_pairs={{0,2},{1,3},{2,0},{3,1},{4,6},{5,7},{6,4},{7,5},{8,10},{9,11},{10,... | collective-permute-start | bytes 476168 | tf_op jit(solution)/shard_map/ppermute | solution.py:88
  56.6 5.8 %collective-permute-start.3 = (f32[2,8,2480]{2,1,0:T(8,128)S(1)}, f32[2,8,2480]{2,1,0:T(8,128)S(1)}, u32[]{:S(2)}, u32[]{:S(2)}) collective-permute-start(f32[2,8,2480]{2,1,0:T(8,128)S(1)} %dynamic-slice_bitcast_fusion.5), channel_id=1, source_target_pairs={{0,8},{1,9},{2,10},{3,11},{4,12},{5,13},{6,14},{7,15},{8,0},{9,1},... | collective-permute-start | bytes 476168 | tf_op jit(solution)/shard_map/ppermute | solution.py:88
  60.1 4.9 %collective-permute-start.8 = (f32[8,2480]{1,0:T(8,128)S(1)}, f32[8,2480]{1,0:T(8,128)S(1)}, u32[]{:S(2)}, u32[]{:S(2)}) collective-permute-start(f32[8,2480]{1,0:T(8,128)S(1)} %dynamic-slice_bitcast_fusion.6), channel_id=1, source_target_pairs={{0,4},{1,5},{2,6},{3,7},{4,0},{5,1},{6,2},{7,3},{8,12},{9,13},{10,... | collective-permute-start | bytes 238088 | tf_op jit(solution)/shard_map/ppermute | solution.py:88
  62.5 4.9 %collective-permute-start.4 = (f32[8,2480]{1,0:T(8,128)S(1)}, f32[8,2480]{1,0:T(8,128)S(1)}, u32[]{:S(2)}, u32[]{:S(2)}) collective-permute-start(f32[8,2480]{1,0:T(8,128)S(1)} %dynamic-slice_bitcast_fusion.7), channel_id=1, source_target_pairs={{0,16},{1,17},{2,18},{3,19},{4,20},{5,21},{6,22},{7,23},{8,24},{9,... | collective-permute-start | bytes 238088 | tf_op jit(solution)/shard_map/ppermute | solution.py:88
  67.4 72.9 %copy-start.3 = (f32[3,30,320]{2,1,0:T(8,128)S(1)}, f32[3,30,320]{2,1,0:T(8,128)}, u32[]{:S(2)}) copy-start(f32[3,30,320]{2,1,0:T(8,128)} %param.11) | copy-start | bytes 345604
  69.0 152.8 %all-gather.6.cloned.1.call-start = ((), (), s32[]{:S(2)}) async-start(), calls=%async_computation.1 | async-start | bytes 4325376 | tf_op jit(solution)/shard_map/all_gather | solution.py:123
  142.0 29.8 %copy-start.4 = (f32[3,30,256]{2,1,0:T(8,128)S(1)}, f32[3,30,256]{2,1,0:T(8,128)}, u32[]{:S(2)}) copy-start(f32[3,30,256]{2,1,0:T(8,128)} %param.13) | copy-start | bytes 276484
  146.7 4.9 %collective-permute-start.9 = (f32[30,1024]{1,0:T(8,128)S(1)}, f32[30,1024]{1,0:T(8,128)S(1)}, u32[]{:S(2)}, u32[]{:S(2)}) collective-permute-start(f32[30,1024]{1,0:T(8,128)S(1)} %pad_maximum_fusion.1), channel_id=1, source_target_pairs={{0,32},{32,0},{64,96},{96,64},{128,160},{160,128},{192,224},{224,1... | collective-permute-start | bytes 368648 | tf_op jit(solution)/shard_map/ppermute | solution.py:55
  151.6 8.2 %collective-permute-start.10 = (f32[30,1024]{1,0:T(8,128)S(1)}, f32[30,1024]{1,0:T(8,128)S(1)}, u32[]{:S(2)}, u32[]{:S(2)}) collective-permute-start(f32[30,1024]{1,0:T(8,128)S(1)} %fusion.23), channel_id=1, source_target_pairs={{0,64},{32,96},{64,0},{96,32},{128,192},{160,224},{192,128},{224,1... | collective-permute-start | bytes 368648 | tf_op jit(solution)/shard_map/ppermute | solution.py:55
  159.8 9.5 %collective-permute-start.11 = (f32[30,1024]{1,0:T(8,128)S(1)}, f32[30,1024]{1,0:T(8,128)S(1)}, u32[]{:S(2)}, u32[]{:S(2)}) collective-permute-start(f32[30,1024]{1,0:T(8,128)S(1)} %add.161), channel_id=1, source_target_pairs={{0,128},{32,160},{64,192},{96,224},{128,0},{160,32},{192,64},{224,... | collective-permute-start | bytes 368648 | tf_op jit(solution)/shard_map/ppermute | solution.py:55
  171.5 5.7 %copy-start.2 = (f32[30,1024]{1,0:T(8,128)S(1)}, f32[30,1024]{1,0:T(8,128)}, u32[]{:S(2)}) copy-start(f32[30,1024]{1,0:T(8,128)} %add.162) | copy-start | bytes 368644
Sparse Core Ops, SparseCore 0:
  69.2 67.8 all-gather.3
  170.2 51.6 all-gather.5

commit v7 on v6

--- a/solution.py
+++ b/solution.py
@@ -88,37 +88,74 @@
     return keep + lax.ppermute(send, axis, pairs), left
 
 
+def swap(value, axis):
+    return lax.all_to_all(value, axis, 0, 0, tiled=True)
+
+
 def local(shard_count, wide_count, split_at, emb_grad, mlp_grad, emb_basis, mlp_basis, emb_first, emb_second, mlp_first, mlp_second):
     mats, rows, cols = mlp_grad.shape
     long_side = emb_grad.shape[1]
     rank = emb_basis.shape[1]
-    emb_term = jnp.einsum("dr,dv->rv", emb_basis, emb_grad, precision=matmul_precision)
-    mlp_term = jnp.einsum("kdr,kdf->rkf", mlp_basis, mlp_grad, precision=matmul_precision)
-    terms = jnp.concatenate([emb_term, mlp_term.reshape(rank, mats * cols)], axis=1)
-    share = halving_scatter(terms, WIDE, wide_count, split_at)
-    emb_share = share[:, :long_side]
-    mlp_share = share[:, long_side : long_side + mats * cols].reshape(-1, mats, cols)
-    emb_first_new, emb_second_new, emb_direction = adam_moments(emb_first, emb_second, emb_share)
-    mlp_first_new, mlp_second_new, mlp_direction = adam_moments(mlp_first, mlp_second, mlp_share)
-    pieces = jnp.concatenate(
-        [
-            emb_direction,
-            mlp_direction.reshape(-1, mats * cols),
-            share,
-        ],
-        axis=1,
-    )
-    gathered = lax.all_gather(pieces, WIDE, axis=0, tiled=True)
-    width = long_side + mats * cols
-    emb_piece = gathered[:, :long_side]
-    mlp_piece = gathered[:, long_side:width].reshape(rank, mats, cols)
-    emb_projected = gathered[:, width : width + long_side]
-    mlp_projected = gathered[:, width + long_side :].reshape(rank, mats, cols)
-    emb_total = jnp.dot(emb_basis, emb_piece, precision=matmul_precision)
-    mlp_total = jnp.einsum("kdr,rkf->kdf", mlp_basis, mlp_piece, precision=matmul_precision)
-    emb_found = jnp.einsum("dv,rv->dr", emb_grad, emb_projected, precision=matmul_precision)
-    mlp_found = jnp.einsum("kdf,rkf->dkr", mlp_grad, mlp_projected, precision=matmul_precision)
-    found = jnp.concatenate([emb_found, mlp_found.reshape(rows, mats * rank)], axis=1)
+    part = rank // wide_count
+    emb_cut = long_side // wide_count
+    mlp_cut = cols // wide_count
+    group = emb_cut + mats * mlp_cut
+
+    def to_groups(emb_value, mlp_value):
+        lead = emb_value.shape[0]
+        emb_value = emb_value.reshape(lead, wide_count, emb_cut)
+        mlp_value = mlp_value.reshape(mats, lead, wide_count, mlp_cut).transpose(1, 2, 0, 3)
+        mlp_value = mlp_value.reshape(lead, wide_count, mats * mlp_cut)
+        return jnp.concatenate([emb_value, mlp_value], axis=2).transpose(1, 0, 2)
+
+    def from_groups(value):
+        lead = value.shape[1]
+        value = value.transpose(1, 0, 2)
+        emb_value = value[:, :, :emb_cut].reshape(lead, long_side)
+        mlp_value = value[:, :, emb_cut:].reshape(lead, wide_count, mats, mlp_cut)
+        mlp_value = mlp_value.transpose(2, 0, 1, 3).reshape(mats, lead, cols)
+        return emb_value, mlp_value
+
+    bases = jnp.concatenate([emb_basis[:, None], mlp_basis.transpose(1, 0, 2)], axis=1)
+    bases = lax.all_gather(bases, WIDE, axis=0, tiled=True)
+    grads = swap(to_groups(emb_grad, mlp_grad), WIDE).reshape(rows * wide_count, group)
+    mlp_first_by_mat = mlp_first.transpose(1, 0, 2)
+    mlp_second_by_mat = mlp_second.transpose(1, 0, 2)
+    moments = jnp.concatenate(
+        [to_groups(emb_first, mlp_first_by_mat), to_groups(emb_second, mlp_second_by_mat)], axis=2
+    )
+    moments = swap(moments, WIDE).reshape(rank, 2 * group)
+    first = moments[:, :group]
+    second = moments[:, group:]
+
+    emb_cols = grads[:, :emb_cut]
+    mlp_cols = grads[:, emb_cut:].reshape(-1, mats, mlp_cut)
+    emb_small = jnp.einsum("dr,dc->rc", bases[:, 0], emb_cols, precision=matmul_precision)
+    mlp_small = jnp.einsum("dkr,dkc->rkc", bases[:, 1:], mlp_cols, precision=matmul_precision)
+    small = jnp.concatenate([emb_small, mlp_small.reshape(rank, mats * mlp_cut)], axis=1)
+    first_new, second_new, direction = adam_moments(first, second, small)
+    emb_update = jnp.einsum(
+        "dr,rc->dc", bases[:, 0], direction[:, :emb_cut], precision=matmul_precision
+    )
+    mlp_update = jnp.einsum(
+        "dkr,rkc->dkc",
+        bases[:, 1:],
+        direction[:, emb_cut:].reshape(rank, mats, mlp_cut),
+        precision=matmul_precision,
+    )
+    updates = jnp.concatenate([emb_update, mlp_update.reshape(-1, mats * mlp_cut)], axis=1)
+    back_moments = swap(
+        jnp.concatenate([first_new, second_new], axis=1).reshape(wide_count, part, 2 * group), WIDE
+    )
+    emb_first_new, mlp_first_new = from_groups(back_moments[:, :, :group])
+    emb_second_new, mlp_second_new = from_groups(back_moments[:, :, group:])
+    back_updates = swap(updates.reshape(wide_count, rows, group), WIDE)
+    emb_total, mlp_total = from_groups(back_updates)
+
+    emb_found = jnp.einsum("dc,rc->dr", emb_cols, emb_small, precision=matmul_precision)
+    mlp_found = jnp.einsum("dkc,rkc->dkr", mlp_cols, mlp_small, precision=matmul_precision)
+    found = jnp.concatenate([emb_found[:, None], mlp_found], axis=1).reshape(-1, (mats + 1) * rank)
+    found = halving_scatter(found, WIDE, wide_count, split_at)
     found = exchange_sum(found, "shard", shard_count)
     every = lax.all_gather(found, WIDE, axis=0, tiled=True)
     every = every.reshape(-1, mats + 1, rank).transpose(1, 0, 2)
@@ -130,8 +167,8 @@
         mlp_total,
         emb_first_new,
         emb_second_new,
-        mlp_first_new,
-        mlp_second_new,
+        mlp_first_new.transpose(1, 0, 2),
+        mlp_second_new.transpose(1, 0, 2),
         basis_new[0],
         basis_new[1:],
     )

time: 256 us -> 276 us (1.078); the launches traced: 255 us -> 272 us
  waiting for transfers between devices: 157 us -> 98.6 us
  local copies, waits for them, and re-layouts: 18.6 us -> 52.5 us
  blocking collectives: 0 us -> 26.9 us
  starting transfers between devices: 23 us -> 38.3 us
  matrix products: 33.7 us -> 27.6 us
  other arithmetic: 7.91 us -> 12.6 us
    all_gather x1, waiting for transfers between devices: 44.6 us -> 0.02 us  [local(): every = lax.all_gather(found, WIDE, axis=0, tiled=True)]
    all_gather x1, waiting for transfers between devices: 67.8 us -> 29 us  [local(): bases = lax.all_gather(bases, WIDE, axis=0, tiled=True)]
    all_to_all x0 -> x3, waiting for transfers between devices: none -> 37.8 us  [swap(): return lax.all_to_all(value, axis, 0, 0, tiled=True)]
    all_to_all x0 -> x1, blocking collectives: none -> 26.9 us  [swap(): return lax.all_to_all(value, axis, 0, 0, tiled=True)]
    all_to_all x0 -> x3, starting transfers between devices: none -> 17.2 us  [swap(): return lax.all_to_all(value, axis, 0, 0, tiled=True)]
    ppermute x9, waiting for transfers between devices: 32.4 us -> 22.7 us  [halving_step(): return (keep + lax.ppermute(send, axis, pairs), left)]
    dynamic_slice x0 -> x12, local copies, waits for them, and re-layouts: none -> 8.64 us  [the longest x7 5.31 us: halving_step(): keep = lax.dynamic_index_in_dim(value, own, axis_at, keepdims=False)]
    reshape x2 -> x22, local copies, waits for them, and re-layouts: 0.18 us -> 8.33 us  [the longest x3 2.72 us: from_groups(): emb_value = value[:, :, :emb_cut].reshape(lead, long_side)]
  transfers between devices with their start and end apart: 14 -> 17, of which waited for: 12 -> 14; matrix products, arithmetic and copies ran while one was open for 4% -> 12% of each run, Pallas kernels for 0% -> 0%
where the time goes in v7:
time: 276 us; the launch traced here: 272 us
  waiting for transfers between devices  98.6 us (36%)
  local copies, waits for them, and re-layouts  52.5 us (19%)
  starting transfers between devices  38.3 us (14%)
  matrix products  27.6 us (10%)
  blocking collectives  26.9 us (10%)
  between operations  15.2 us (6%)
  other arithmetic  12.6 us (5%)
    all_to_all x3, waiting for transfers between devices, swap(): return lax.all_to_all(value, axis, 0, 0, tiled=True)  37.8 us
    all_gather x1, waiting for transfers between devices, local(): bases = lax.all_gather(bases, WIDE, axis=0, tiled=True)  29 us
    all_to_all x1, blocking collectives, swap(): return lax.all_to_all(value, axis, 0, 0, tiled=True)  26.9 us
    ppermute x9, waiting for transfers between devices, halving_step(): return (keep + lax.ppermute(send, axis, pairs), left)  22.7 us
    all_to_all x3, starting transfers between devices, swap(): return lax.all_to_all(value, axis, 0, 0, tiled=True)  17.2 us
    dot_general x13, matrix products, matmul(): return jnp.einsum('...rs,...st->...rt', x, y, precision=matmul_precision)  11.4 us
    ppermute x9, starting transfers between devices, halving_step(): return (keep + lax.ppermute(send, axis, pairs), left)  10.9 us
    ppermute x3, starting transfers between devices, exchange_sum(): value = value + lax.ppermute(value, axis, pairs)  9.68 us
  transfers between devices with their start and end apart: 17, of which 14 were waited for; matrix products, arithmetic and copies ran while one was open for 12% of the time, Pallas kernels for 0%

profile of v7, /device:TPU:1, one launch (start us, length us, event | category | flops | bytes accessed | tf_op | source)
XLA Modules:
  0.0 271.9 jit_solution(4663308173650850826)
XLA Ops:
  9.8 1.1 copy.187
  13.2 1.4 maximum_bitcast_fusion
  14.5 8.6 %all-to-all-start.1 = ((f32[32,30,155]{2,1,0:T(8,128)}), f32[32,30,155]{2,1,0:T(8,128)S(1)}, u32[]{:S(2)}, u32[]{:S(2)}) async-start(f32[32,30,155]{2,1,0:T(8,128)} %maximum_bitcast_fusion), calls=%async_computation.1 | async-start | bytes 2097152 | tf_op jit(solution)/shard_map/all_to_all | solution.py:92
  23.6 18.0 %all-to-all-done.1 = f32[32,30,155]{2,1,0:T(8,128)S(1)} async-done(((f32[32,30,155]{2,1,0:T(8,128)}), f32[32,30,155]{2,1,0:T(8,128)S(1)}, u32[]{:S(2)}, u32[]{:S(2)}) %all-to-all-start.1) | async-done | bytes 595232 | tf_op jit(solution)/shard_map/all_to_all | solution.py:92
  42.2 29.0 %all-gather.4.cloned.1.call-done = f32[960,4,256]{2,1,0:T(4,128)} async-done(((f32[30,4,256]{2,1,0:T(4,128)}), f32[960,4,256]{2,1,0:T(4,128)}) %all-gather.4.cloned.1.call-update) | async-done | bytes 3932176 | tf_op jit(solution)/shard_map/all_gather | solution.py:120
  71.2 5.1 %slice_reduce_fusion = (f32[960,256]{1,0:T(8,128)S(1)}, f32[960,1,256]{2,1,0:T(1,128)S(1)}) fusion(f32[960,4,256]{2,1,0:T(4,128)} %all-gather.4.cloned.1.call-done), kind=kLoop, calls=%fused_computation.82 | loop fusion | bytes 2949120 | tf_op jit(solution)/shard_map/slice | solution.py:138
  77.9 1.1 fusion.13
  79.0 1.4 convolution_bitcast_fusion.1
  81.3 4.4 %copy.206 = f32[960,4,256]{2,1,0:T(4,128)} copy(f32[960,4,256]{2,0,1:T(8,128)S(1)} %pad_maximum_fusion) | data formatting | bytes 7864320 | tf_op jit(solution)/shard_map/concatenate | solution.py:157
  85.7 5.9 %reshape_reshape.3 = f32[2,2,2,2,2,30,1024]{6,5,4,3,2,1,0:T(8,128)} reshape(f32[960,4,256]{2,1,0:T(4,128)} %copy.206) | data formatting | bytes 7864320 | tf_op jit(solution)/shard_map/reshape;reshape | solution.py:66
  91.6 2.5 constant_dynamic-slice_fusion.13
  94.1 2.8 %copy.272 = f32[2,2,2,2,1,30,1024]{6,3,5,2,1,0,4:T(2,128)} copy(f32[2,2,2,2,1,30,1024]{6,5,4,3,2,1,0:T(8,128)S(1)} %get-tuple-element.96) | data formatting | bytes 3932160 | tf_op jit(solution)/shard_map/jit(dynamic_index_in_dim)/dynamic_slice | solution.py:85
  97.2 4.0 %collective-permute-done = f32[2,2,2,2,30,1024]{5,3,4,2,1,0:T(2,128)} collective-permute-done((f32[2,2,2,2,30,1024]{5,3,4,2,1,0:T(2,128)}, f32[2,2,2,2,30,1024]{5,3,4,2,1,0:T(2,128)}, u32[]{:S(2)}, u32[]{:S(2)}) %collective-permute-start) | collective-permute-done | bytes 1966112 | tf_op jit(solution)/shard_map/ppermute | solution.py:88
  101.2 3.5 %bitcast_add_fusion = f32[2,2,2,2,30,1024]{5,3,4,2,1,0:T(2,128)S(1)} fusion(f32[2,2,2,2,30,1024]{5,3,4,2,1,0:T(2,128)} %collective-permute-done, f32[2,2,2,2,1,30,1024]{6,5,4,3,2,1,0:T(8,128)S(1)} %get-tuple-element.95), kind=kLoop, calls=%fused_computation.13 | loop fusion | flops 491520 | bytes 5898240 | tf_op jit(solution)/shard_map/add | solution.py:88
  107.2 1.7 constant_dynamic-slice_fusion.11
  109.3 9.9 %collective-permute-done.5 = f32[2,2,2,30,512]{4,2,3,1,0:T(2,128)} collective-permute-done((f32[2,2,2,30,512]{4,2,3,1,0:T(2,128)}, f32[2,2,2,30,512]{4,2,3,1,0:T(2,128)}, u32[]{:S(2)}, u32[]{:S(2)}) %collective-permute-start.5) | collective-permute-done | bytes 491552 | tf_op jit(solution)/shard_map/ppermute | solution.py:88
  119.2 1.3 bitcast_add_fusion.1
  120.5 1.9 collective-permute-start.6
  122.4 1.3 bitcast_add_fusion.2
  124.4 1.8 collective-permute-start.2
  126.2 2.2 collective-permute-done.6
  128.9 1.2 collective-permute-start.7
  130.1 2.0 collective-permute-done.2
  134.4 2.0 collective-permute-start.8
  136.6 1.9 collective-permute-start.4
  139.2 3.1 %collective-permute-done.4 = f32[30,512]{1,0:T(8,128)S(1)} collective-permute-done((f32[30,512]{1,0:T(8,128)S(1)}, f32[30,512]{1,0:T(8,128)S(1)}, u32[]{:S(2)}, u32[]{:S(2)}) %collective-permute-start.4) | collective-permute-done | bytes 61472 | tf_op jit(solution)/shard_map/ppermute | solution.py:88
  142.3 1.4 collective-permute-start.9
  143.6 2.5 collective-permute-done.9
  146.2 2.3 collective-permute-start.10
  148.5 3.4 %collective-permute-done.10 = f32[30,1024]{1,0:T(8,128)S(1)} collective-permute-done((f32[30,1024]{1,0:T(8,128)S(1)}, f32[30,1024]{1,0:T(8,128)S(1)}, u32[]{:S(2)}, u32[]{:S(2)}) %collective-permute-start.10) | collective-permute-done | bytes 122912 | tf_op jit(solution)/shard_map/ppermute | solution.py:55
  152.0 6.0 %collective-permute-start.11 = (f32[30,1024]{1,0:T(8,128)S(1)}, f32[30,1024]{1,0:T(8,128)S(1)}, u32[]{:S(2)}, u32[]{:S(2)}) collective-permute-start(f32[30,1024]{1,0:T(8,128)S(1)} %add.145), channel_id=1, source_target_pairs={{0,128},{32,160},{64,192},{96,224},{128,0},{160,32},{192,64},{224,... | collective-permute-start | bytes 368648 | tf_op jit(solution)/shard_map/ppermute | solution.py:55
  158.0 3.1 %collective-permute-done.11 = f32[30,1024]{1,0:T(8,128)S(1)} collective-permute-done((f32[30,1024]{1,0:T(8,128)S(1)}, f32[30,1024]{1,0:T(8,128)S(1)}, u32[]{:S(2)}, u32[]{:S(2)}) %collective-permute-start.11) | collective-permute-done | bytes 122912 | tf_op jit(solution)/shard_map/ppermute | solution.py:55
  164.5 26.9 %all_to_all.20 = f32[32,8,310]{2,1,0:T(8,128)S(1)} all-to-all(f32[32,8,310]{2,1,0:T(8,128)S(1)} %pad_maximum_fusion.2), channel_id=1, replica_groups=mesh['shard'=8,'tensor'=4,'section'=8] {'tensor','section'}, dimensions={0} | all-to-all | bytes 634880 | tf_op jit(solution)/shard_map/all_to_all | solution.py:92
  192.5 3.7 %fusion.10 = f32[960,3,10]{0,2,1:T(8,128)S(1)} fusion(f32[256,3,10]{0,2,1:T(8,128)S(1)} %reshape.122, f32[960,3,256]{2,1,0:T(4,128)} %copy-done), kind=kOutput, calls=%fused_computation.17 | convolution fusion | flops 44236800 | bytes 3095040 | tf_op jit(solution)/shard_map/dkr,rkc->dkc/dot_general | solution.py:140
  198.4 3.7 %all-to-all-start.3 = ((f32[32,8,310]{2,1,0:T(8,128)}), f32[32,8,310]{2,1,0:T(8,128)S(1)}, u32[]{:S(2)}, u32[]{:S(2)}) async-start(f32[32,8,310]{2,1,0:T(8,128)} %bitcast.19), calls=%async_computation.3 | async-start | bytes 786432 | tf_op jit(solution)/shard_map/all_to_all | solution.py:92
  202.1 1.5 fusion.22
  203.6 1.3 pad_maximum_fusion.1
  204.9 7.5 %all-to-all-done.3 = f32[32,8,310]{2,1,0:T(8,128)S(1)} async-done(((f32[32,8,310]{2,1,0:T(8,128)}), f32[32,8,310]{2,1,0:T(8,128)S(1)}, u32[]{:S(2)}, u32[]{:S(2)}) %all-to-all-start.3) | async-done | bytes 317472 | tf_op jit(solution)/shard_map/all_to_all | solution.py:92
  212.4 4.9 %all-to-all-start.2 = ((f32[32,30,155]{2,1,0:T(8,128)}), f32[32,30,155]{2,1,0:T(8,128)S(1)}, u32[]{:S(2)}, u32[]{:S(2)}) async-start(f32[32,30,155]{2,1,0:T(8,128)} %pad_maximum_fusion.1), calls=%async_computation.2 | async-start | bytes 2097152 | tf_op jit(solution)/shard_map/all_to_all | solution.py:92
  221.9 12.3 %all-to-all-done.2 = f32[32,30,155]{2,1,0:T(8,128)S(1)} async-done(((f32[32,30,155]{2,1,0:T(8,128)}), f32[32,30,155]{2,1,0:T(8,128)S(1)}, u32[]{:S(2)}, u32[]{:S(2)}) %all-to-all-start.2) | async-done | bytes 595232 | tf_op jit(solution)/shard_map/all_to_all | solution.py:92
  234.8 1.1 reshape.123
  238.0 5.7 %reshape.134 = f32[960,4,256]{2,1,0:T(4,128)} reshape(f32[32,30,1024]{2,1,0:T(8,128)} %all-gather.6.cloned.1.call-done) | data formatting | bytes 7864320 | tf_op jit(solution)/shard_map/reshape | solution.py:161
  243.7 7.4 %select_reduce_fusion = (f32[4]{0:T(128)S(1)}, f32[4,256,256]{2,1,0:T(8,128)S(1)}) fusion(pred[256,256]{1,0:T(8,128)(4,1)S(1)} %iota_compare_fusion, f32[960,4,256]{2,1,0:T(4,128)} %reshape.134), kind=kOutput, calls=%fused_computation.21 | convolution fusion | flops 1510473728 | bytes 5046288 | tf_op jit(solution)/shard_map/kdr,kds->krs/dot_general | solution.py:162
  251.4 11.3 %while.13 = (s32[]{:T(128)}, f32[4,256,256]{2,1,0:T(8,128)S(1)}, f32[4,256,256]{1,2,0:T(8,128)S(1)}, f32[256,256]{1,0:T(8,128)S(1)}, s32[]{:T(128)}) while((s32[]{:T(128)}, f32[4,256,256]{2,1,0:T(8,128)S(1)}, f32[4,256,256]{1,2,0:T(8,128)S(1)}, f32[256,256]{1,0:T(8,128)S(1)}, s32[]{:T(128)}) %tuple.46), condition=%wide.region_2.3_spmd.clone, body=%wide.region_1.2_spmd.clone.sunk | while | flops 1611726848 | bytes 14417981 | solution.py:44
  254.0 1.1 convolution_bitcast_fusion.4
  256.0 1.1 fusion.68
  257.8 1.1 convolution_bitcast_fusion.4
  261.6 1.1 convolution_bitcast_fusion.4
  (144 shorter events, 38.1 us)
Async XLA Ops:
  7.2 4.7 %copy-start.5 = (f32[30,4000]{1,0:T(8,128)S(1)}, f32[30,4000]{1,0:T(8,128)}, u32[]{:S(2)}) copy-start(f32[30,4000]{1,0:T(8,128)} %param.10) | copy-start | bytes 1440004
  7.2 64.0 %all-gather.4.cloned.1.call-start = ((), (), s32[]{:S(2)}) async-start(), calls=%async_computation.4 | async-start | bytes 4055040 | tf_op jit(solution)/shard_map/all_gather | solution.py:120
  14.5 27.1 %all-to-all-start.1 = ((f32[32,30,155]{2,1,0:T(8,128)}), f32[32,30,155]{2,1,0:T(8,128)S(1)}, u32[]{:S(2)}, u32[]{:S(2)}) async-start(f32[32,30,155]{2,1,0:T(8,128)} %maximum_bitcast_fusion), calls=%async_computation.1 | async-start | bytes 2097152 | tf_op jit(solution)/shard_map/all_to_all | solution.py:92
  23.1 214.9 %all-gather.6.cloned.1.call-start = ((), (), s32[]{:S(2)}) async-start(), calls=%async_computation.5 | async-start | bytes 4325376 | tf_op jit(solution)/shard_map/all_gather | solution.py:160
  71.1 5.7 %copy-start.1 = (f32[960,4,256]{2,1,0:T(4,128)S(1)}, f32[960,4,256]{2,1,0:T(4,128)}, u32[]{:S(2)}) copy-start(f32[960,4,256]{2,1,0:T(4,128)} %all-gather.4.cloned.1.call-done) | copy-start | bytes 11796484
  77.9 3.1 %copy-start = (f32[960,3,256]{2,1,0:T(4,128)}, f32[960,3,256]{2,1,0:T(4,128)S(1)}, u32[]{:S(2)}) copy-start(f32[960,3,256]{2,1,0:T(4,128)S(1)} %slice.86) | copy-start | bytes 8847364
  96.9 4.3 %collective-permute-start = (f32[2,2,2,2,30,1024]{5,3,4,2,1,0:T(2,128)}, f32[2,2,2,2,30,1024]{5,3,4,2,1,0:T(2,128)}, u32[]{:S(2)}, u32[]{:S(2)}) collective-permute-start(f32[2,2,2,2,30,1024]{5,3,4,2,1,0:T(2,128)} %bitcast.127), channel_id=1, source_target_pairs={{0,1},{1,0},{2,3},{3,2},{4,5},{5,4},{6,7},{7,6},{8,9},{9,8},{10,11... | collective-permute-start | bytes 5898248 | tf_op jit(solution)/shard_map/ppermute | solution.py:88
  106.3 12.8 %collective-permute-start.5 = (f32[2,2,2,30,512]{4,2,3,1,0:T(2,128)}, f32[2,2,2,30,512]{4,2,3,1,0:T(2,128)}, u32[]{:S(2)}, u32[]{:S(2)}) collective-permute-start(f32[2,2,2,30,512]{4,2,3,1,0:T(2,128)} %dynamic-slice_bitcast_fusion), channel_id=1, source_target_pairs={{0,8},{1,9},{2,10},{3,11},{4,12},{5,13},{6,14},{7,15},{8,0},{9,1},... | collective-permute-start | bytes 1474568 | tf_op jit(solution)/shard_map/ppermute | solution.py:88
  109.2 13.2 %collective-permute-start.1 = (f32[2,2,2,30,512]{4,2,3,1,0:T(2,128)S(1)}, f32[2,2,2,30,512]{4,2,3,1,0:T(2,128)S(1)}, u32[]{:S(2)}, u32[]{:S(2)}) collective-permute-start(f32[2,2,2,30,512]{4,2,3,1,0:T(2,128)S(1)} %bitcast.163), channel_id=1, source_target_pairs={{0,2},{1,3},{2,0},{3,1},{4,6},{5,7},{6,4},{7,5},{8,10},{9,11},{10,... | collective-permute-start | bytes 1474568 | tf_op jit(solution)/shard_map/ppermute | solution.py:88
  120.5 8.0 %collective-permute-start.6 = (f32[2,2,30,512]{3,1,2,0:T(2,128)S(1)}, f32[2,2,30,512]{3,1,2,0:T(2,128)S(1)}, u32[]{:S(2)}, u32[]{:S(2)}) collective-permute-start(f32[2,2,30,512]{3,1,2,0:T(2,128)S(1)} %dynamic-slice_bitcast_fusion.1), channel_id=1, source_target_pairs={{0,16},{1,17},{2,18},{3,19},{4,20},{5,21},{6,22},{7,23},{8,24},{9,... | collective-permute-start | bytes 737288 | tf_op jit(solution)/shard_map/ppermute | solution.py:88
  123.8 38.0 %copy-start.8 = (f32[8,3,320]{2,0,1:T(8,128)S(1)}, f32[8,3,320]{2,0,1:T(8,128)}, u32[]{:S(2)}) copy-start(f32[8,3,320]{2,0,1:T(8,128)} %param.16) | copy-start | bytes 92164
  124.4 38.2 %copy-start.6 = (f32[8,4000]{1,0:T(8,128)S(1)}, f32[8,4000]{1,0:T(8,128)}, u32[]{:S(2)}) copy-start(f32[8,4000]{1,0:T(8,128)} %param.14) | copy-start | bytes 384004
  124.4 38.6 %copy-start.9 = (f32[8,3,320]{2,0,1:T(8,128)S(1)}, f32[8,3,320]{2,0,1:T(8,128)}, u32[]{:S(2)}) copy-start(f32[8,3,320]{2,0,1:T(8,128)} %param.17) | copy-start | bytes 92164
  124.4 7.7 %collective-permute-start.2 = (f32[2,2,30,512]{3,1,2,0:T(2,128)S(1)}, f32[2,2,30,512]{3,1,2,0:T(2,128)S(1)}, u32[]{:S(2)}, u32[]{:S(2)}) collective-permute-start(f32[2,2,30,512]{3,1,2,0:T(2,128)S(1)} %bitcast.168), channel_id=1, source_target_pairs={{0,4},{1,5},{2,6},{3,7},{4,0},{5,1},{6,2},{7,3},{8,12},{9,13},{10,... | collective-permute-start | bytes 737288 | tf_op jit(solution)/shard_map/ppermute | solution.py:88
  128.9 5.3 %collective-permute-start.7 = (f32[2,30,512]{2,0,1:T(2,128)S(1)}, f32[2,30,512]{2,0,1:T(2,128)S(1)}, u32[]{:S(2)}, u32[]{:S(2)}) collective-permute-start(f32[2,30,512]{2,0,1:T(2,128)S(1)} %bitcast.169), channel_id=1, source_target_pairs={{0,2},{1,3},{2,0},{3,1},{4,6},{5,7},{6,4},{7,5},{8,10},{9,11},{10,... | collective-permute-start | bytes 368648 | tf_op jit(solution)/shard_map/ppermute | solution.py:88
  132.1 31.7 %copy-start.7 = (f32[8,4000]{1,0:T(8,128)S(1)}, f32[8,4000]{1,0:T(8,128)}, u32[]{:S(2)}) copy-start(f32[8,4000]{1,0:T(8,128)} %param.15) | copy-start | bytes 384004
  132.6 3.8 %collective-permute-start.3 = (f32[2,30,512]{2,0,1:T(2,128)S(1)}, f32[2,30,512]{2,0,1:T(2,128)S(1)}, u32[]{:S(2)}, u32[]{:S(2)}) collective-permute-start(f32[2,30,512]{2,0,1:T(2,128)S(1)} %bitcast.170), channel_id=1, source_target_pairs={{0,8},{1,9},{2,10},{3,11},{4,12},{5,13},{6,14},{7,15},{8,0},{9,1},... | collective-permute-start | bytes 368648 | tf_op jit(solution)/shard_map/ppermute | solution.py:88
  134.4 4.7 %collective-permute-start.8 = (f32[30,512]{1,0:T(8,128)S(1)}, f32[30,512]{1,0:T(8,128)S(1)}, u32[]{:S(2)}, u32[]{:S(2)}) collective-permute-start(f32[30,512]{1,0:T(8,128)S(1)} %bitcast.171), channel_id=1, source_target_pairs={{0,4},{1,5},{2,6},{3,7},{4,0},{5,1},{6,2},{7,3},{8,12},{9,13},{10,... | collective-permute-start | bytes 184328 | tf_op jit(solution)/shard_map/ppermute | solution.py:88
  136.6 5.6 %collective-permute-start.4 = (f32[30,512]{1,0:T(8,128)S(1)}, f32[30,512]{1,0:T(8,128)S(1)}, u32[]{:S(2)}, u32[]{:S(2)}) collective-permute-start(f32[30,512]{1,0:T(8,128)S(1)} %bitcast.172), channel_id=1, source_target_pairs={{0,16},{1,17},{2,18},{3,19},{4,20},{5,21},{6,22},{7,23},{8,24},{9,... | collective-permute-start | bytes 184328 | tf_op jit(solution)/shard_map/ppermute | solution.py:88
  142.3 3.9 %collective-permute-start.9 = (f32[30,1024]{1,0:T(8,128)S(1)}, f32[30,1024]{1,0:T(8,128)S(1)}, u32[]{:S(2)}, u32[]{:S(2)}) collective-permute-start(f32[30,1024]{1,0:T(8,128)S(1)} %pad_maximum_fusion.5), channel_id=1, source_target_pairs={{0,32},{32,0},{64,96},{96,64},{128,160},{160,128},{192,224},{224,1... | collective-permute-start | bytes 368648 | tf_op jit(solution)/shard_map/ppermute | solution.py:55
  146.2 5.8 %collective-permute-start.10 = (f32[30,1024]{1,0:T(8,128)S(1)}, f32[30,1024]{1,0:T(8,128)S(1)}, u32[]{:S(2)}, u32[]{:S(2)}) collective-permute-start(f32[30,1024]{1,0:T(8,128)S(1)} %fusion.26), channel_id=1, source_target_pairs={{0,64},{32,96},{64,0},{96,32},{128,192},{160,224},{192,128},{224,1... | collective-permute-start | bytes 368648 | tf_op jit(solution)/shard_map/ppermute | solution.py:55
  152.0 9.1 %collective-permute-start.11 = (f32[30,1024]{1,0:T(8,128)S(1)}, f32[30,1024]{1,0:T(8,128)S(1)}, u32[]{:S(2)}, u32[]{:S(2)}) collective-permute-start(f32[30,1024]{1,0:T(8,128)S(1)} %add.145), channel_id=1, source_target_pairs={{0,128},{32,160},{64,192},{96,224},{128,0},{160,32},{192,64},{224,... | collective-permute-start | bytes 368648 | tf_op jit(solution)/shard_map/ppermute | solution.py:55
  192.5 4.8 %copy-start.4 = (f32[256,155]{0,1:T(8,128)}, f32[256,155]{0,1:T(8,128)S(1)}, u32[]{:S(2)}) copy-start(f32[256,155]{0,1:T(8,128)S(1)} %get-tuple-element.92) | copy-start | bytes 476164
  192.5 4.9 %copy-start.3 = (f32[256,155]{0,1:T(8,128)S(1)}, f32[256,155]{0,1:T(8,128)}, u32[]{:S(2)}) copy-start(f32[256,155]{0,1:T(8,128)} %get-tuple-element.94) | copy-start | bytes 476164
  198.4 14.0 %all-to-all-start.3 = ((f32[32,8,310]{2,1,0:T(8,128)}), f32[32,8,310]{2,1,0:T(8,128)S(1)}, u32[]{:S(2)}, u32[]{:S(2)}) async-start(f32[32,8,310]{2,1,0:T(8,128)} %bitcast.19), calls=%async_computation.3 | async-start | bytes 786432 | tf_op jit(solution)/shard_map/all_to_all | solution.py:92
  212.4 21.9 %all-to-all-start.2 = ((f32[32,30,155]{2,1,0:T(8,128)}), f32[32,30,155]{2,1,0:T(8,128)S(1)}, u32[]{:S(2)}, u32[]{:S(2)}) async-start(f32[32,30,155]{2,1,0:T(8,128)} %pad_maximum_fusion.1), calls=%async_computation.2 | async-start | bytes 2097152 | tf_op jit(solution)/shard_map/all_to_all | solution.py:92
  234.3 3.7 %copy-start.2 = (f32[30,1024]{1,0:T(8,128)S(1)}, f32[30,1024]{1,0:T(8,128)}, u32[]{:S(2)}) copy-start(f32[30,1024]{1,0:T(8,128)} %add.146) | copy-start | bytes 368644
Sparse Core Ops, SparseCore 0:
  11.1 60.0 all-gather.3
  161.9 63.1 all-gather.5

commit v8 on v6

--- a/solution.py
+++ b/solution.py
@@ -120,9 +120,11 @@
     mlp_found = jnp.einsum("kdf,rkf->dkr", mlp_grad, mlp_projected, precision=matmul_precision)
     found = jnp.concatenate([emb_found, mlp_found.reshape(rows, mats * rank)], axis=1)
     found = exchange_sum(found, "shard", shard_count)
-    every = lax.all_gather(found, WIDE, axis=0, tiled=True)
-    every = every.reshape(-1, mats + 1, rank).transpose(1, 0, 2)
-    gram = jnp.einsum("kdr,kds->krs", every, every, precision=matmul_precision)
+    every = lax.all_gather(found, WIDE, axis=0)
+    every = jnp.einsum("tdr,tds->rs", every, every, precision=matmul_precision)
+    gram = jnp.stack(
+        [every[k * rank : (k + 1) * rank, k * rank : (k + 1) * rank] for k in range(mats + 1)]
+    )
     targets = found.reshape(rows, mats + 1, rank).transpose(1, 0, 2)
     basis_new = newton_schulz(targets, gram)
     return (

time: 256 us -> 253 us (0.988)
  local copies, waits for them, and re-layouts: 18.6 us -> 13 us
  matrix products: 33.7 us -> 37 us
    reshape x1 -> x0, local copies, waits for them, and re-layouts: 5.62 us -> none  [local(): every = every.reshape(-1, mats + 1, rank).transpose(1, 0, 2)]
    dot_general x1, matrix products: 7.36 us -> 10.3 us  [local(): every = jnp.einsum('tdr,tds->rs', every, every, precision=matmul_precision)]
where the time goes in v8:
time: 253 us
  waiting for transfers between devices  157 us (62%)
  matrix products  37 us (15%)
  starting transfers between devices  23 us (9%)
  between operations  14.5 us (6%)
  local copies, waits for them, and re-layouts  13 us (5%)
  other arithmetic  8.05 us (3%)
    all_gather x1, waiting for transfers between devices, local(): gathered = lax.all_gather(pieces, WIDE, axis=0, tiled=True)  67.8 us
    all_gather x1, waiting for transfers between devices, local(): every = lax.all_gather(found, WIDE, axis=0)  44.6 us
    ppermute x9, waiting for transfers between devices, halving_step(): return (keep + lax.ppermute(send, axis, pairs), left)  32.4 us
    ppermute x9, starting transfers between devices, halving_step(): return (keep + lax.ppermute(send, axis, pairs), left)  12.6 us
    ppermute x3, waiting for transfers between devices, exchange_sum(): value = value + lax.ppermute(value, axis, pairs)  12.5 us
    dot_general x13, matrix products, matmul(): return jnp.einsum('...rs,...st->...rt', x, y, precision=matmul_precision)  11.6 us
    dot_general x1, matrix products, local(): every = jnp.einsum('tdr,tds->rs', every, every, precision=matmul_precision)  10.3 us
    ppermute x3, starting transfers between devices, exchange_sum(): value = value + lax.ppermute(value, axis, pairs)  10.2 us
  transfers between devices with their start and end apart: 14, of which 12 were waited for; matrix products, arithmetic and copies ran while one was open for 4% of the time, Pallas kernels for 0%

profile of v8, /device:TPU:1, one launch (start us, length us, event | category | flops | bytes accessed | tf_op | source)
XLA Modules:
  0.0 253.0 jit_solution(7751127891179148638)
XLA Ops:
  7.2 1.6 convolution_bitcast_fusion.3
  9.6 0.9 concatenate.19
  10.6 1.8 fusion.31
  12.4 2.0 copy-done.1
  14.4 1.8 fusion.7
  16.2 3.2 %collective-permute-start = (f32[2,2,2,2,8,4960]{5,4,3,2,1,0:T(8,128)}, f32[2,2,2,2,8,4960]{5,4,3,2,1,0:T(8,128)}, u32[]{:S(2)}, u32[]{:S(2)}) collective-permute-start(f32[2,2,2,2,8,4960]{5,4,3,2,1,0:T(8,128)} %fusion.7), channel_id=1, source_target_pairs={{0,1},{1,0},{2,3},{3,2},{4,5},{5,4},{6,7},{7,6},{8,9},{9,8},{10,11... | collective-permute-start | bytes 7618568 | tf_op jit(solution)/shard_map/ppermute | solution.py:88
  19.4 4.8 %collective-permute-done = f32[2,2,2,2,8,4960]{5,4,3,2,1,0:T(8,128)} collective-permute-done((f32[2,2,2,2,8,4960]{5,4,3,2,1,0:T(8,128)}, f32[2,2,2,2,8,4960]{5,4,3,2,1,0:T(8,128)}, u32[]{:S(2)}, u32[]{:S(2)}) %collective-permute-start) | collective-permute-done | bytes 2539552 | tf_op jit(solution)/shard_map/ppermute | solution.py:88
  24.2 2.7 %fusion.10 = f32[2,2,2,2,8,4960]{5,4,3,2,1,0:T(8,128)S(1)} fusion(f32[2,2,2,2,8,4960]{5,4,3,2,1,0:T(8,128)} %collective-permute-done, s32[]{:T(128)S(6)} %select_n.50, f32[2,2,2,2,2,8,4000]{6,5,4,3,2,1,0:T(8,128)} %bitcast.112, f32[2,2,2,2,2,8,960]{6,5,4,3,2,1,0:T(8,128)S(1)} %concatenate.19), kind=kLoop, calls=%fused_computation.17 | loop fusion | flops 1269760 | bytes 10158084 | tf_op jit(solution)/shard_map/add | solution.py:88
  27.4 0.9 dynamic-slice_bitcast_fusion
  28.3 0.9 collective-permute-start.1
  29.2 15.3 %collective-permute-done.5 = f32[2,2,2,8,2480]{4,3,2,1,0:T(8,128)} collective-permute-done((f32[2,2,2,8,2480]{4,3,2,1,0:T(8,128)}, f32[2,2,2,8,2480]{4,3,2,1,0:T(8,128)}, u32[]{:S(2)}, u32[]{:S(2)}) %collective-permute-start.5) | collective-permute-done | bytes 634912 | tf_op jit(solution)/shard_map/ppermute | solution.py:88
  44.5 1.2 bitcast_add_fusion
  45.7 1.3 collective-permute-start.6
  47.1 2.8 %collective-permute-start.2 = (f32[2,2,8,2480]{3,2,1,0:T(8,128)S(1)}, f32[2,2,8,2480]{3,2,1,0:T(8,128)S(1)}, u32[]{:S(2)}, u32[]{:S(2)}) collective-permute-start(f32[2,2,8,2480]{3,2,1,0:T(8,128)S(1)} %dynamic-slice_bitcast_fusion.3), channel_id=1, source_target_pairs={{0,4},{1,5},{2,6},{3,7},{4,0},{5,1},{6,2},{7,3},{8,12},{9,13},{10,... | collective-permute-start | bytes 952328 | tf_op jit(solution)/shard_map/ppermute | solution.py:88
  50.0 5.4 %collective-permute-done.6 = f32[2,2,8,2480]{3,2,1,0:T(8,128)S(1)} collective-permute-done((f32[2,2,8,2480]{3,2,1,0:T(8,128)S(1)}, f32[2,2,8,2480]{3,2,1,0:T(8,128)S(1)}, u32[]{:S(2)}, u32[]{:S(2)}) %collective-permute-start.6) | collective-permute-done | bytes 317472 | tf_op jit(solution)/shard_map/ppermute | solution.py:88
  55.5 1.0 collective-permute-done.2
  57.1 3.0 %collective-permute-done.7 = f32[2,8,2480]{2,1,0:T(8,128)S(1)} collective-permute-done((f32[2,8,2480]{2,1,0:T(8,128)S(1)}, f32[2,8,2480]{2,1,0:T(8,128)S(1)}, u32[]{:S(2)}, u32[]{:S(2)}) %collective-permute-start.7) | collective-permute-done | bytes 158752 | tf_op jit(solution)/shard_map/ppermute | solution.py:88
  60.1 2.3 collective-permute-start.8
  62.4 1.5 collective-permute-start.4
  63.9 1.0 collective-permute-done.8
  65.3 2.0 collective-permute-done.4
  67.4 0.8 add_divide_fusion
  68.2 0.8 concatenate.22
  69.3 67.8 %all-gather.5.cloned.1.call-done = f32[256,9920]{1,0:T(8,128)} async-done(((f32[8,9920]{1,0:T(8,128)}), f32[256,9920]{1,0:T(8,128)}) %all-gather.5.cloned.1.call-update) | async-done | bytes 10158096 | tf_op jit(solution)/shard_map/all_gather | solution.py:111
  137.0 1.9 fusion.27
  139.0 1.3 copy.62
  140.3 1.6 convolution_bitcast_fusion.5
  142.0 4.6 %fusion.11 = f32[30,256]{1,0:T(8,128)S(1)} fusion(f32[30,4000]{1,0:T(8,128)S(1)} %copy-done, f32[256,9920]{1,0:T(8,128)} %all-gather.5.cloned.1.call-done), kind=kOutput, calls=%fused_computation.22 | convolution fusion | flops 184320000 | bytes 4705024 | tf_op jit(solution)/shard_map/dv,rv->dr/dot_general | solution.py:119
  146.6 1.4 collective-permute-start.9
  148.0 3.5 %collective-permute-done.9 = f32[30,1024]{1,0:T(8,128)S(1)} collective-permute-done((f32[30,1024]{1,0:T(8,128)S(1)}, f32[30,1024]{1,0:T(8,128)S(1)}, u32[]{:S(2)}, u32[]{:S(2)}) %collective-permute-start.9) | collective-permute-done | bytes 122912 | tf_op jit(solution)/shard_map/ppermute | solution.py:55
  151.5 2.4 collective-permute-start.10
  153.9 5.9 %collective-permute-done.10 = f32[30,1024]{1,0:T(8,128)S(1)} collective-permute-done((f32[30,1024]{1,0:T(8,128)S(1)}, f32[30,1024]{1,0:T(8,128)S(1)}, u32[]{:S(2)}, u32[]{:S(2)}) %collective-permute-start.10) | collective-permute-done | bytes 122912 | tf_op jit(solution)/shard_map/ppermute | solution.py:55
  159.8 6.4 %collective-permute-start.11 = (f32[30,1024]{1,0:T(8,128)S(1)}, f32[30,1024]{1,0:T(8,128)S(1)}, u32[]{:S(2)}, u32[]{:S(2)}) collective-permute-start(f32[30,1024]{1,0:T(8,128)S(1)} %add.161), channel_id=1, source_target_pairs={{0,128},{32,160},{64,192},{96,224},{128,0},{160,32},{192,64},{224,... | collective-permute-start | bytes 368648 | tf_op jit(solution)/shard_map/ppermute | solution.py:55
  166.2 3.1 %collective-permute-done.11 = f32[30,1024]{1,0:T(8,128)S(1)} collective-permute-done((f32[30,1024]{1,0:T(8,128)S(1)}, f32[30,1024]{1,0:T(8,128)S(1)}, u32[]{:S(2)}, u32[]{:S(2)}) %collective-permute-start.11) | collective-permute-done | bytes 122912 | tf_op jit(solution)/shard_map/ppermute | solution.py:55
  171.8 1.2 convolution_bitcast_fusion.4
  173.0 4.2 %convolution_bitcast_fusion.1 = f32[30,4000]{1,0:T(8,128)} fusion(f32[30,256]{1,0:T(8,128)S(1)} %copy-done.5, f32[256,9920]{1,0:T(8,128)} %all-gather.5.cloned.1.call-done), kind=kOutput, calls=%fused_computation.9 | convolution fusion | flops 184320000 | bytes 4705024 | tf_op jit(solution)/shard_map/dot_general | solution.py:117
  177.2 44.6 %all-gather.7.cloned.1.call-done = f32[32,30,1024]{2,1,0:T(8,128)} async-done(((f32[1,30,1024]{2,1,0:T(8,128)}), f32[32,30,1024]{2,1,0:T(8,128)}) %all-gather.7.cloned.1.call-update) | async-done | bytes 3932176 | tf_op jit(solution)/shard_map/all_gather | solution.py:123
  221.9 10.3 %convolution_bitcast_fusion.2 = f32[1024,1024]{1,0:T(8,128)S(1)} fusion(f32[32,30,1024]{2,1,0:T(8,128)} %all-gather.7.cloned.1.call-done), kind=kOutput, calls=%fused_computation.18 | convolution fusion | flops 6039797760 | bytes 8126464 | tf_op jit(solution)/shard_map/tdr,tds->rs/dot_general | solution.py:124
  232.8 11.5 %while.13 = (s32[]{:T(128)}, f32[4,256,256]{2,1,0:T(8,128)S(1)}, f32[4,256,256]{1,2,0:T(8,128)S(1)}, f32[256,256]{1,0:T(8,128)S(1)}, s32[]{:T(128)}) while((s32[]{:T(128)}, f32[4,256,256]{2,1,0:T(8,128)S(1)}, f32[4,256,256]{1,2,0:T(8,128)S(1)}, f32[256,256]{1,0:T(8,128)S(1)}, s32[]{:T(128)}) %tuple.38), condition=%wide.region_2.3_spmd.clone, body=%wide.region_1.2_spmd.clone.sunk | while | flops 1611726848 | bytes 14417981 | solution.py:44
  232.9 0.8 fusion.72
  233.7 1.1 fusion.73
  235.6 1.1 convolution_bitcast_fusion.7
  236.7 0.8 fusion.72
  237.5 1.1 fusion.73
  239.4 1.1 convolution_bitcast_fusion.7
  240.5 0.8 fusion.72
  241.4 1.1 fusion.73
  243.2 1.1 convolution_bitcast_fusion.7
  (79 shorter events, 10.2 us)
Async XLA Ops:
  7.2 3.4 %copy-start = (f32[30,4000]{1,0:T(8,128)S(1)}, f32[30,4000]{1,0:T(8,128)}, u32[]{:S(2)}) copy-start(f32[30,4000]{1,0:T(8,128)} %param.10) | copy-start | bytes 1440004
  7.2 3.4 %copy-start.5 = (f32[30,256]{1,0:T(8,128)S(1)}, f32[30,256]{1,0:T(8,128)}, u32[]{:S(2)}) copy-start(f32[30,256]{1,0:T(8,128)} %param.12) | copy-start | bytes 92164
  7.2 129.8 %all-gather.5.cloned.1.call-start = ((), (), s32[]{:S(2)}) async-start(), calls=%async_computation | async-start | bytes 10543104 | tf_op jit(solution)/shard_map/all_gather | solution.py:111
  12.4 2.0 copy-start.1
  16.2 8.0 %collective-permute-start = (f32[2,2,2,2,8,4960]{5,4,3,2,1,0:T(8,128)}, f32[2,2,2,2,8,4960]{5,4,3,2,1,0:T(8,128)}, u32[]{:S(2)}, u32[]{:S(2)}) collective-permute-start(f32[2,2,2,2,8,4960]{5,4,3,2,1,0:T(8,128)} %fusion.7), channel_id=1, source_target_pairs={{0,1},{1,0},{2,3},{3,2},{4,5},{5,4},{6,7},{7,6},{8,9},{9,8},{10,11... | collective-permute-start | bytes 7618568 | tf_op jit(solution)/shard_map/ppermute | solution.py:88
  28.2 16.2 %collective-permute-start.5 = (f32[2,2,2,8,2480]{4,3,2,1,0:T(8,128)}, f32[2,2,2,8,2480]{4,3,2,1,0:T(8,128)}, u32[]{:S(2)}, u32[]{:S(2)}) collective-permute-start(f32[2,2,2,8,2480]{4,3,2,1,0:T(8,128)} %dynamic-slice_bitcast_fusion), channel_id=1, source_target_pairs={{0,8},{1,9},{2,10},{3,11},{4,12},{5,13},{6,14},{7,15},{8,0},{9,1},... | collective-permute-start | bytes 1904648 | tf_op jit(solution)/shard_map/ppermute | solution.py:88
  28.3 18.7 %collective-permute-start.1 = (f32[2,2,2,8,2480]{4,3,2,1,0:T(8,128)S(1)}, f32[2,2,2,8,2480]{4,3,2,1,0:T(8,128)S(1)}, u32[]{:S(2)}, u32[]{:S(2)}) collective-permute-start(f32[2,2,2,8,2480]{4,3,2,1,0:T(8,128)S(1)} %dynamic-slice_bitcast_fusion.1), channel_id=1, source_target_pairs={{0,2},{1,3},{2,0},{3,1},{4,6},{5,7},{6,4},{7,5},{8,10},{9,11},{10,... | collective-permute-start | bytes 1904648 | tf_op jit(solution)/shard_map/ppermute | solution.py:88
  45.6 19.5 %copy-start.8 = (f32[8,3,320]{2,0,1:T(8,128)S(1)}, f32[8,3,320]{2,0,1:T(8,128)}, u32[]{:S(2)}) copy-start(f32[8,3,320]{2,0,1:T(8,128)} %param.16) | copy-start | bytes 92164
  45.7 19.5 %copy-start.9 = (f32[8,3,320]{2,0,1:T(8,128)S(1)}, f32[8,3,320]{2,0,1:T(8,128)}, u32[]{:S(2)}) copy-start(f32[8,3,320]{2,0,1:T(8,128)} %param.17) | copy-start | bytes 92164
  45.7 21.7 %copy-start.6 = (f32[8,4000]{1,0:T(8,128)S(1)}, f32[8,4000]{1,0:T(8,128)}, u32[]{:S(2)}) copy-start(f32[8,4000]{1,0:T(8,128)} %param.14) | copy-start | bytes 384004
  45.7 21.7 %copy-start.7 = (f32[8,4000]{1,0:T(8,128)S(1)}, f32[8,4000]{1,0:T(8,128)}, u32[]{:S(2)}) copy-start(f32[8,4000]{1,0:T(8,128)} %param.15) | copy-start | bytes 384004
  45.7 9.6 %collective-permute-start.6 = (f32[2,2,8,2480]{3,2,1,0:T(8,128)S(1)}, f32[2,2,8,2480]{3,2,1,0:T(8,128)S(1)}, u32[]{:S(2)}, u32[]{:S(2)}) collective-permute-start(f32[2,2,8,2480]{3,2,1,0:T(8,128)S(1)} %dynamic-slice_bitcast_fusion.2), channel_id=1, source_target_pairs={{0,16},{1,17},{2,18},{3,19},{4,20},{5,21},{6,22},{7,23},{8,24},{9,... | collective-permute-start | bytes 952328 | tf_op jit(solution)/shard_map/ppermute | solution.py:88
  47.1 9.4 %collective-permute-start.2 = (f32[2,2,8,2480]{3,2,1,0:T(8,128)S(1)}, f32[2,2,8,2480]{3,2,1,0:T(8,128)S(1)}, u32[]{:S(2)}, u32[]{:S(2)}) collective-permute-start(f32[2,2,8,2480]{3,2,1,0:T(8,128)S(1)} %dynamic-slice_bitcast_fusion.3), channel_id=1, source_target_pairs={{0,4},{1,5},{2,6},{3,7},{4,0},{5,1},{6,2},{7,3},{8,12},{9,13},{10,... | collective-permute-start | bytes 952328 | tf_op jit(solution)/shard_map/ppermute | solution.py:88
  55.4 4.6 %collective-permute-start.7 = (f32[2,8,2480]{2,1,0:T(8,128)S(1)}, f32[2,8,2480]{2,1,0:T(8,128)S(1)}, u32[]{:S(2)}, u32[]{:S(2)}) collective-permute-start(f32[2,8,2480]{2,1,0:T(8,128)S(1)} %dynamic-slice_bitcast_fusion.4), channel_id=1, source_target_pairs={{0,2},{1,3},{2,0},{3,1},{4,6},{5,7},{6,4},{7,5},{8,10},{9,11},{10,... | collective-permute-start | bytes 476168 | tf_op jit(solution)/shard_map/ppermute | solution.py:88
  56.6 5.8 %collective-permute-start.3 = (f32[2,8,2480]{2,1,0:T(8,128)S(1)}, f32[2,8,2480]{2,1,0:T(8,128)S(1)}, u32[]{:S(2)}, u32[]{:S(2)}) collective-permute-start(f32[2,8,2480]{2,1,0:T(8,128)S(1)} %dynamic-slice_bitcast_fusion.5), channel_id=1, source_target_pairs={{0,8},{1,9},{2,10},{3,11},{4,12},{5,13},{6,14},{7,15},{8,0},{9,1},... | collective-permute-start | bytes 476168 | tf_op jit(solution)/shard_map/ppermute | solution.py:88
  60.1 4.9 %collective-permute-start.8 = (f32[8,2480]{1,0:T(8,128)S(1)}, f32[8,2480]{1,0:T(8,128)S(1)}, u32[]{:S(2)}, u32[]{:S(2)}) collective-permute-start(f32[8,2480]{1,0:T(8,128)S(1)} %dynamic-slice_bitcast_fusion.6), channel_id=1, source_target_pairs={{0,4},{1,5},{2,6},{3,7},{4,0},{5,1},{6,2},{7,3},{8,12},{9,13},{10,... | collective-permute-start | bytes 238088 | tf_op jit(solution)/shard_map/ppermute | solution.py:88
  62.4 4.9 %collective-permute-start.4 = (f32[8,2480]{1,0:T(8,128)S(1)}, f32[8,2480]{1,0:T(8,128)S(1)}, u32[]{:S(2)}, u32[]{:S(2)}) collective-permute-start(f32[8,2480]{1,0:T(8,128)S(1)} %dynamic-slice_bitcast_fusion.7), channel_id=1, source_target_pairs={{0,16},{1,17},{2,18},{3,19},{4,20},{5,21},{6,22},{7,23},{8,24},{9,... | collective-permute-start | bytes 238088 | tf_op jit(solution)/shard_map/ppermute | solution.py:88
  65.2 75.0 %copy-start.3 = (f32[3,30,320]{2,1,0:T(8,128)S(1)}, f32[3,30,320]{2,1,0:T(8,128)}, u32[]{:S(2)}) copy-start(f32[3,30,320]{2,1,0:T(8,128)} %param.11) | copy-start | bytes 345604
  69.0 152.8 %all-gather.7.cloned.1.call-start = ((), (), s32[]{:S(2)}) async-start(), calls=%async_computation.1 | async-start | bytes 4325376 | tf_op jit(solution)/shard_map/all_gather | solution.py:123
  142.0 29.8 %copy-start.4 = (f32[3,30,256]{2,1,0:T(8,128)S(1)}, f32[3,30,256]{2,1,0:T(8,128)}, u32[]{:S(2)}) copy-start(f32[3,30,256]{2,1,0:T(8,128)} %param.13) | copy-start | bytes 276484
  146.6 4.9 %collective-permute-start.9 = (f32[30,1024]{1,0:T(8,128)S(1)}, f32[30,1024]{1,0:T(8,128)S(1)}, u32[]{:S(2)}, u32[]{:S(2)}) collective-permute-start(f32[30,1024]{1,0:T(8,128)S(1)} %pad_maximum_fusion.2), channel_id=1, source_target_pairs={{0,32},{32,0},{64,96},{96,64},{128,160},{160,128},{192,224},{224,1... | collective-permute-start | bytes 368648 | tf_op jit(solution)/shard_map/ppermute | solution.py:55
  151.5 8.2 %collective-permute-start.10 = (f32[30,1024]{1,0:T(8,128)S(1)}, f32[30,1024]{1,0:T(8,128)S(1)}, u32[]{:S(2)}, u32[]{:S(2)}) collective-permute-start(f32[30,1024]{1,0:T(8,128)S(1)} %fusion.22), channel_id=1, source_target_pairs={{0,64},{32,96},{64,0},{96,32},{128,192},{160,224},{192,128},{224,1... | collective-permute-start | bytes 368648 | tf_op jit(solution)/shard_map/ppermute | solution.py:55
  159.8 9.5 %collective-permute-start.11 = (f32[30,1024]{1,0:T(8,128)S(1)}, f32[30,1024]{1,0:T(8,128)S(1)}, u32[]{:S(2)}, u32[]{:S(2)}) collective-permute-start(f32[30,1024]{1,0:T(8,128)S(1)} %add.161), channel_id=1, source_target_pairs={{0,128},{32,160},{64,192},{96,224},{128,0},{160,32},{192,64},{224,... | collective-permute-start | bytes 368648 | tf_op jit(solution)/shard_map/ppermute | solution.py:55
  170.2 7.0 %copy-start.2 = (f32[30,1024]{1,0:T(8,128)S(1)}, f32[30,1024]{1,0:T(8,128)}, u32[]{:S(2)}) copy-start(f32[30,1024]{1,0:T(8,128)} %add.162) | copy-start | bytes 368644
Sparse Core Ops, SparseCore 0:
  69.1 67.8 all-gather.4
  170.1 51.6 all-gather.6

commit v9 on v8

--- a/solution.py
+++ b/solution.py
@@ -100,20 +100,15 @@
     mlp_share = share[:, long_side : long_side + mats * cols].reshape(-1, mats, cols)
     emb_first_new, emb_second_new, emb_direction = adam_moments(emb_first, emb_second, emb_share)
     mlp_first_new, mlp_second_new, mlp_direction = adam_moments(mlp_first, mlp_second, mlp_share)
-    pieces = jnp.concatenate(
-        [
-            emb_direction,
-            mlp_direction.reshape(-1, mats * cols),
-            share,
-        ],
-        axis=1,
+    projected = lax.all_gather(share, WIDE, axis=0, tiled=True)
+    directions = jnp.concatenate(
+        [emb_direction, mlp_direction.reshape(-1, mats * cols)], axis=1
     )
-    gathered = lax.all_gather(pieces, WIDE, axis=0, tiled=True)
-    width = long_side + mats * cols
-    emb_piece = gathered[:, :long_side]
-    mlp_piece = gathered[:, long_side:width].reshape(rank, mats, cols)
-    emb_projected = gathered[:, width : width + long_side]
-    mlp_projected = gathered[:, width + long_side :].reshape(rank, mats, cols)
+    directions = lax.all_gather(directions, WIDE, axis=0, tiled=True)
+    emb_piece = directions[:, :long_side]
+    mlp_piece = directions[:, long_side:].reshape(rank, mats, cols)
+    emb_projected = projected[:, :long_side]
+    mlp_projected = projected[:, long_side:].reshape(rank, mats, cols)
     emb_total = jnp.dot(emb_basis, emb_piece, precision=matmul_precision)
     mlp_total = jnp.einsum("kdr,rkf->kdf", mlp_basis, mlp_piece, precision=matmul_precision)
     emb_found = jnp.einsum("dv,rv->dr", emb_grad, emb_projected, precision=matmul_precision)

time: 253 us -> 265 us (1.047)
  waiting for transfers between devices: 157 us -> 170 us
    all_gather x1 -> x2, waiting for transfers between devices: 67.8 us -> 79.5 us  [the longest x1 56.2 us: local(): projected = lax.all_gather(share, WIDE, axis=0, tiled=True)]
  transfers between devices with their start and end apart: 14 -> 15, of which waited for: 12 -> 13; matrix products, arithmetic and copies ran while one was open for 4% -> 7% of each run, Pallas kernels for 0% -> 0%
where the time goes in v9:
time: 265 us
  waiting for transfers between devices  170 us (64%)
  matrix products  35 us (13%)
  starting transfers between devices  22.8 us (9%)
  between operations  14.2 us (5%)
  local copies, waits for them, and re-layouts  12.4 us (5%)
  other arithmetic  9.58 us (4%)
    all_gather x1, waiting for transfers between devices, local(): projected = lax.all_gather(share, WIDE, axis=0, tiled=True)  56.2 us
    all_gather x1, waiting for transfers between devices, local(): every = lax.all_gather(found, WIDE, axis=0)  45.6 us
    ppermute x9, waiting for transfers between devices, halving_step(): return (keep + lax.ppermute(send, axis, pairs), left)  32.6 us
    all_gather x1, waiting for transfers between devices, local(): directions = lax.all_gather(directions, WIDE, axis=0, tiled=True)  23.3 us
    ppermute x3, waiting for transfers between devices, exchange_sum(): value = value + lax.ppermute(value, axis, pairs)  12.6 us
    ppermute x9, starting transfers between devices, halving_step(): return (keep + lax.ppermute(send, axis, pairs), left)  12.4 us
    dot_general x13, matrix products, matmul(): return jnp.einsum('...rs,...st->...rt', x, y, precision=matmul_precision)  11.4 us
    dot_general x1, matrix products, local(): every = jnp.einsum('tdr,tds->rs', every, every, precision=matmul_precision)  10.3 us
  transfers between devices with their start and end apart: 15, of which 13 were waited for; matrix products, arithmetic and copies ran while one was open for 7% of the time, Pallas kernels for 0%

profile of v9, /device:TPU:1, one launch (start us, length us, event | category | flops | bytes accessed | tf_op | source)
XLA Modules:
  0.0 264.5 jit_solution(17572298452342759057)
XLA Ops:
  7.2 1.6 convolution_bitcast_fusion.3
  8.9 0.8 copy.58
  9.6 0.9 concatenate.18
  10.6 1.8 fusion.31
  12.4 1.9 copy-done.1
  14.4 1.8 fusion.7
  16.2 3.2 %collective-permute-start = (f32[2,2,2,2,8,4960]{5,4,3,2,1,0:T(8,128)}, f32[2,2,2,2,8,4960]{5,4,3,2,1,0:T(8,128)}, u32[]{:S(2)}, u32[]{:S(2)}) collective-permute-start(f32[2,2,2,2,8,4960]{5,4,3,2,1,0:T(8,128)} %fusion.7), channel_id=1, source_target_pairs={{0,1},{1,0},{2,3},{3,2},{4,5},{5,4},{6,7},{7,6},{8,9},{9,8},{10,11... | collective-permute-start | bytes 7618568 | tf_op jit(solution)/shard_map/ppermute | solution.py:88
  19.4 4.8 %collective-permute-done = f32[2,2,2,2,8,4960]{5,4,3,2,1,0:T(8,128)} collective-permute-done((f32[2,2,2,2,8,4960]{5,4,3,2,1,0:T(8,128)}, f32[2,2,2,2,8,4960]{5,4,3,2,1,0:T(8,128)}, u32[]{:S(2)}, u32[]{:S(2)}) %collective-permute-start) | collective-permute-done | bytes 2539552 | tf_op jit(solution)/shard_map/ppermute | solution.py:88
  24.2 2.7 %fusion.10 = f32[2,2,2,2,8,4960]{5,4,3,2,1,0:T(8,128)S(1)} fusion(f32[2,2,2,2,8,4960]{5,4,3,2,1,0:T(8,128)} %collective-permute-done, s32[]{:T(128)S(6)} %select_n.50, f32[2,2,2,2,2,8,4000]{6,5,4,3,2,1,0:T(8,128)} %bitcast.112, f32[2,2,2,2,2,8,960]{6,5,4,3,2,1,0:T(8,128)S(1)} %concatenate.18), kind=kLoop, calls=%fused_computation.17 | loop fusion | flops 1269760 | bytes 10158084 | tf_op jit(solution)/shard_map/add | solution.py:88
  27.4 0.9 dynamic-slice_bitcast_fusion.1
  28.3 0.9 collective-permute-start.5
  29.2 15.3 %collective-permute-done.1 = f32[2,2,2,8,2480]{4,3,2,1,0:T(8,128)} collective-permute-done((f32[2,2,2,8,2480]{4,3,2,1,0:T(8,128)}, f32[2,2,2,8,2480]{4,3,2,1,0:T(8,128)}, u32[]{:S(2)}, u32[]{:S(2)}) %collective-permute-start.1) | collective-permute-done | bytes 634912 | tf_op jit(solution)/shard_map/ppermute | solution.py:88
  44.5 1.2 bitcast_add_fusion.1
  45.7 1.1 collective-permute-start.2
  47.0 3.0 %collective-permute-start.6 = (f32[2,2,8,2480]{3,2,1,0:T(8,128)S(1)}, f32[2,2,8,2480]{3,2,1,0:T(8,128)S(1)}, u32[]{:S(2)}, u32[]{:S(2)}) collective-permute-start(f32[2,2,8,2480]{3,2,1,0:T(8,128)S(1)} %dynamic-slice_bitcast_fusion.2), channel_id=1, source_target_pairs={{0,16},{1,17},{2,18},{3,19},{4,20},{5,21},{6,22},{7,23},{8,24},{9,... | collective-permute-start | bytes 952328 | tf_op jit(solution)/shard_map/ppermute | solution.py:88
  50.0 5.4 %collective-permute-done.2 = f32[2,2,8,2480]{3,2,1,0:T(8,128)S(1)} collective-permute-done((f32[2,2,8,2480]{3,2,1,0:T(8,128)S(1)}, f32[2,2,8,2480]{3,2,1,0:T(8,128)S(1)}, u32[]{:S(2)}, u32[]{:S(2)}) %collective-permute-start.2) | collective-permute-done | bytes 317472 | tf_op jit(solution)/shard_map/ppermute | solution.py:88
  55.5 0.8 collective-permute-done.6
  56.8 3.3 %collective-permute-done.3 = f32[2,8,2480]{2,1,0:T(8,128)S(1)} collective-permute-done((f32[2,8,2480]{2,1,0:T(8,128)S(1)}, f32[2,8,2480]{2,1,0:T(8,128)S(1)}, u32[]{:S(2)}, u32[]{:S(2)}) %collective-permute-start.3) | collective-permute-done | bytes 158752 | tf_op jit(solution)/shard_map/ppermute | solution.py:88
  60.2 1.9 collective-permute-start.4
  62.2 1.8 collective-permute-start.8
  63.9 1.1 collective-permute-done.4
  65.1 2.0 collective-permute-done.8
  67.1 0.8 pad_maximum_fusion.1
  68.3 0.8 add_divide_fusion
  70.1 56.2 %all-gather.8.cloned.1.call-done = f32[256,4960]{1,0:T(8,128)} async-done(((f32[8,4960]{1,0:T(8,128)}), f32[256,4960]{1,0:T(8,128)}) %all-gather.8.cloned.1.call-update) | async-done | bytes 5079056 | tf_op jit(solution)/shard_map/all_gather | solution.py:103
  126.3 1.6 slice.64
  128.7 4.1 %fusion.11 = f32[30,256]{1,0:T(8,128)S(1)} fusion(f32[30,4000]{1,0:T(8,128)S(1)} %copy-done, f32[256,4960]{1,0:T(8,128)} %all-gather.8.cloned.1.call-done), kind=kOutput, calls=%fused_computation.22 | convolution fusion | flops 184320000 | bytes 4705024 | tf_op jit(solution)/shard_map/dv,rv->dr/dot_general | solution.py:114
  132.8 1.4 collective-permute-start.9
  134.2 3.5 %collective-permute-done.9 = f32[30,1024]{1,0:T(8,128)S(1)} collective-permute-done((f32[30,1024]{1,0:T(8,128)S(1)}, f32[30,1024]{1,0:T(8,128)S(1)}, u32[]{:S(2)}, u32[]{:S(2)}) %collective-permute-start.9) | collective-permute-done | bytes 122912 | tf_op jit(solution)/shard_map/ppermute | solution.py:55
  137.7 2.3 collective-permute-start.10
  140.1 6.0 %collective-permute-done.10 = f32[30,1024]{1,0:T(8,128)S(1)} collective-permute-done((f32[30,1024]{1,0:T(8,128)S(1)}, f32[30,1024]{1,0:T(8,128)S(1)}, u32[]{:S(2)}, u32[]{:S(2)}) %collective-permute-start.10) | collective-permute-done | bytes 122912 | tf_op jit(solution)/shard_map/ppermute | solution.py:55
  146.1 6.3 %collective-permute-start.11 = (f32[30,1024]{1,0:T(8,128)S(1)}, f32[30,1024]{1,0:T(8,128)S(1)}, u32[]{:S(2)}, u32[]{:S(2)}) collective-permute-start(f32[30,1024]{1,0:T(8,128)S(1)} %add.161), channel_id=1, source_target_pairs={{0,128},{32,160},{64,192},{96,224},{128,0},{160,32},{192,64},{224,... | collective-permute-start | bytes 368648 | tf_op jit(solution)/shard_map/ppermute | solution.py:55
  152.4 3.1 %collective-permute-done.11 = f32[30,1024]{1,0:T(8,128)S(1)} collective-permute-done((f32[30,1024]{1,0:T(8,128)S(1)}, f32[30,1024]{1,0:T(8,128)S(1)}, u32[]{:S(2)}, u32[]{:S(2)}) %collective-permute-start.11) | collective-permute-done | bytes 122912 | tf_op jit(solution)/shard_map/ppermute | solution.py:55
  157.6 23.3 %all-gather.6.cloned.1.call-done = f32[256,4960]{1,0:T(8,128)} async-done(((f32[8,4960]{1,0:T(8,128)}), f32[256,4960]{1,0:T(8,128)}) %all-gather.6.cloned.1.call-update) | async-done | bytes 5079056 | tf_op jit(solution)/shard_map/all_gather | solution.py:107
  181.0 1.6 slice.62
  182.9 1.2 convolution_bitcast_fusion.4
  184.0 4.2 %convolution_bitcast_fusion.1 = f32[30,4000]{1,0:T(8,128)} fusion(f32[30,256]{1,0:T(8,128)S(1)} %copy-done.5, f32[256,4960]{1,0:T(8,128)} %all-gather.6.cloned.1.call-done), kind=kOutput, calls=%fused_computation.9 | convolution fusion | flops 184320000 | bytes 4705024 | tf_op jit(solution)/shard_map/dot_general | solution.py:112
  188.3 45.6 %all-gather.10.cloned.1.call-done = f32[32,30,1024]{2,1,0:T(8,128)} async-done(((f32[1,30,1024]{2,1,0:T(8,128)}), f32[32,30,1024]{2,1,0:T(8,128)}) %all-gather.10.cloned.1.call-update) | async-done | bytes 3932176 | tf_op jit(solution)/shard_map/all_gather | solution.py:118
  233.9 10.3 %convolution_bitcast_fusion.2 = f32[1024,1024]{1,0:T(8,128)S(1)} fusion(f32[32,30,1024]{2,1,0:T(8,128)} %all-gather.10.cloned.1.call-done), kind=kOutput, calls=%fused_computation.18 | convolution fusion | flops 6039797760 | bytes 8126464 | tf_op jit(solution)/shard_map/tdr,tds->rs/dot_general | solution.py:119
  244.8 11.3 %while.13 = (s32[]{:T(128)}, f32[4,256,256]{2,1,0:T(8,128)S(1)}, f32[4,256,256]{1,2,0:T(8,128)S(1)}, f32[256,256]{1,0:T(8,128)S(1)}, s32[]{:T(128)}) while((s32[]{:T(128)}, f32[4,256,256]{2,1,0:T(8,128)S(1)}, f32[4,256,256]{1,2,0:T(8,128)S(1)}, f32[256,256]{1,0:T(8,128)S(1)}, s32[]{:T(128)}) %tuple.37), condition=%wide.region_2.3_spmd.clone, body=%wide.region_1.2_spmd.clone.sunk | while | flops 1611726848 | bytes 14417981 | solution.py:44
  244.9 0.8 fusion.72
  245.6 1.1 fusion.73
  247.5 1.1 convolution_bitcast_fusion.7
  248.7 0.8 fusion.72
  249.4 1.1 fusion.73
  251.3 1.1 convolution_bitcast_fusion.7
  253.2 1.1 fusion.73
  255.0 1.1 convolution_bitcast_fusion.7
  (84 shorter events, 11.6 us)
Async XLA Ops:
  7.2 3.4 %copy-start = (f32[30,4000]{1,0:T(8,128)S(1)}, f32[30,4000]{1,0:T(8,128)}, u32[]{:S(2)}) copy-start(f32[30,4000]{1,0:T(8,128)} %param.10) | copy-start | bytes 1440004
  7.2 3.4 %copy-start.5 = (f32[30,256]{1,0:T(8,128)S(1)}, f32[30,256]{1,0:T(8,128)}, u32[]{:S(2)}) copy-start(f32[30,256]{1,0:T(8,128)} %param.12) | copy-start | bytes 92164
  7.2 119.1 %all-gather.8.cloned.1.call-start = ((), (), s32[]{:S(2)}) async-start(), calls=%async_computation.1 | async-start | bytes 5271552 | tf_op jit(solution)/shard_map/all_gather | solution.py:103
  12.4 2.0 copy-start.1
  16.2 8.0 %collective-permute-start = (f32[2,2,2,2,8,4960]{5,4,3,2,1,0:T(8,128)}, f32[2,2,2,2,8,4960]{5,4,3,2,1,0:T(8,128)}, u32[]{:S(2)}, u32[]{:S(2)}) collective-permute-start(f32[2,2,2,2,8,4960]{5,4,3,2,1,0:T(8,128)} %fusion.7), channel_id=1, source_target_pairs={{0,1},{1,0},{2,3},{3,2},{4,5},{5,4},{6,7},{7,6},{8,9},{9,8},{10,11... | collective-permute-start | bytes 7618568 | tf_op jit(solution)/shard_map/ppermute | solution.py:88
  28.3 16.2 %collective-permute-start.1 = (f32[2,2,2,8,2480]{4,3,2,1,0:T(8,128)}, f32[2,2,2,8,2480]{4,3,2,1,0:T(8,128)}, u32[]{:S(2)}, u32[]{:S(2)}) collective-permute-start(f32[2,2,2,8,2480]{4,3,2,1,0:T(8,128)} %dynamic-slice_bitcast_fusion.1), channel_id=1, source_target_pairs={{0,2},{1,3},{2,0},{3,1},{4,6},{5,7},{6,4},{7,5},{8,10},{9,11},{10,... | collective-permute-start | bytes 1904648 | tf_op jit(solution)/shard_map/ppermute | solution.py:88
  28.3 18.6 %collective-permute-start.5 = (f32[2,2,2,8,2480]{4,3,2,1,0:T(8,128)S(1)}, f32[2,2,2,8,2480]{4,3,2,1,0:T(8,128)S(1)}, u32[]{:S(2)}, u32[]{:S(2)}) collective-permute-start(f32[2,2,2,8,2480]{4,3,2,1,0:T(8,128)S(1)} %dynamic-slice_bitcast_fusion), channel_id=1, source_target_pairs={{0,8},{1,9},{2,10},{3,11},{4,12},{5,13},{6,14},{7,15},{8,0},{9,1},... | collective-permute-start | bytes 1904648 | tf_op jit(solution)/shard_map/ppermute | solution.py:88
  45.7 22.4 %copy-start.8 = (f32[8,3,320]{2,0,1:T(8,128)S(1)}, f32[8,3,320]{2,0,1:T(8,128)}, u32[]{:S(2)}) copy-start(f32[8,3,320]{2,0,1:T(8,128)} %param.16) | copy-start | bytes 92164
  45.7 22.4 %copy-start.9 = (f32[8,3,320]{2,0,1:T(8,128)S(1)}, f32[8,3,320]{2,0,1:T(8,128)}, u32[]{:S(2)}) copy-start(f32[8,3,320]{2,0,1:T(8,128)} %param.17) | copy-start | bytes 92164
  45.7 22.6 %copy-start.6 = (f32[8,4000]{1,0:T(8,128)S(1)}, f32[8,4000]{1,0:T(8,128)}, u32[]{:S(2)}) copy-start(f32[8,4000]{1,0:T(8,128)} %param.14) | copy-start | bytes 384004
  45.7 22.6 %copy-start.7 = (f32[8,4000]{1,0:T(8,128)S(1)}, f32[8,4000]{1,0:T(8,128)}, u32[]{:S(2)}) copy-start(f32[8,4000]{1,0:T(8,128)} %param.15) | copy-start | bytes 384004
  45.7 9.6 %collective-permute-start.2 = (f32[2,2,8,2480]{3,2,1,0:T(8,128)S(1)}, f32[2,2,8,2480]{3,2,1,0:T(8,128)S(1)}, u32[]{:S(2)}, u32[]{:S(2)}) collective-permute-start(f32[2,2,8,2480]{3,2,1,0:T(8,128)S(1)} %dynamic-slice_bitcast_fusion.3), channel_id=1, source_target_pairs={{0,4},{1,5},{2,6},{3,7},{4,0},{5,1},{6,2},{7,3},{8,12},{9,13},{10,... | collective-permute-start | bytes 952328 | tf_op jit(solution)/shard_map/ppermute | solution.py:88
  47.0 9.4 %collective-permute-start.6 = (f32[2,2,8,2480]{3,2,1,0:T(8,128)S(1)}, f32[2,2,8,2480]{3,2,1,0:T(8,128)S(1)}, u32[]{:S(2)}, u32[]{:S(2)}) collective-permute-start(f32[2,2,8,2480]{3,2,1,0:T(8,128)S(1)} %dynamic-slice_bitcast_fusion.2), channel_id=1, source_target_pairs={{0,16},{1,17},{2,18},{3,19},{4,20},{5,21},{6,22},{7,23},{8,24},{9,... | collective-permute-start | bytes 952328 | tf_op jit(solution)/shard_map/ppermute | solution.py:88
  55.4 4.7 %collective-permute-start.3 = (f32[2,8,2480]{2,1,0:T(8,128)S(1)}, f32[2,8,2480]{2,1,0:T(8,128)S(1)}, u32[]{:S(2)}, u32[]{:S(2)}) collective-permute-start(f32[2,8,2480]{2,1,0:T(8,128)S(1)} %dynamic-slice_bitcast_fusion.5), channel_id=1, source_target_pairs={{0,8},{1,9},{2,10},{3,11},{4,12},{5,13},{6,14},{7,15},{8,0},{9,1},... | collective-permute-start | bytes 476168 | tf_op jit(solution)/shard_map/ppermute | solution.py:88
  56.4 71.7 %copy-start.3 = (f32[3,30,320]{2,1,0:T(8,128)S(1)}, f32[3,30,320]{2,1,0:T(8,128)}, u32[]{:S(2)}) copy-start(f32[3,30,320]{2,1,0:T(8,128)} %param.11) | copy-start | bytes 345604
  56.4 5.7 %collective-permute-start.7 = (f32[2,8,2480]{2,1,0:T(8,128)S(1)}, f32[2,8,2480]{2,1,0:T(8,128)S(1)}, u32[]{:S(2)}, u32[]{:S(2)}) collective-permute-start(f32[2,8,2480]{2,1,0:T(8,128)S(1)} %dynamic-slice_bitcast_fusion.4), channel_id=1, source_target_pairs={{0,2},{1,3},{2,0},{3,1},{4,6},{5,7},{6,4},{7,5},{8,10},{9,11},{10,... | collective-permute-start | bytes 476168 | tf_op jit(solution)/shard_map/ppermute | solution.py:88
  60.2 4.9 %collective-permute-start.4 = (f32[8,2480]{1,0:T(8,128)S(1)}, f32[8,2480]{1,0:T(8,128)S(1)}, u32[]{:S(2)}, u32[]{:S(2)}) collective-permute-start(f32[8,2480]{1,0:T(8,128)S(1)} %dynamic-slice_bitcast_fusion.7), channel_id=1, source_target_pairs={{0,16},{1,17},{2,18},{3,19},{4,20},{5,21},{6,22},{7,23},{8,24},{9,... | collective-permute-start | bytes 238088 | tf_op jit(solution)/shard_map/ppermute | solution.py:88
  62.2 4.9 %collective-permute-start.8 = (f32[8,2480]{1,0:T(8,128)S(1)}, f32[8,2480]{1,0:T(8,128)S(1)}, u32[]{:S(2)}, u32[]{:S(2)}) collective-permute-start(f32[8,2480]{1,0:T(8,128)S(1)} %dynamic-slice_bitcast_fusion.6), channel_id=1, source_target_pairs={{0,4},{1,5},{2,6},{3,7},{4,0},{5,1},{6,2},{7,3},{8,12},{9,13},{10,... | collective-permute-start | bytes 238088 | tf_op jit(solution)/shard_map/ppermute | solution.py:88
  67.8 113.1 %all-gather.6.cloned.1.call-start = ((), (), s32[]{:S(2)}) async-start(), calls=%async_computation | async-start | bytes 5271552 | tf_op jit(solution)/shard_map/all_gather | solution.py:107
  69.8 164.1 %all-gather.10.cloned.1.call-start = ((), (), s32[]{:S(2)}) async-start(), calls=%async_computation.2 | async-start | bytes 4325376 | tf_op jit(solution)/shard_map/all_gather | solution.py:118
  132.8 50.1 %copy-start.4 = (f32[3,30,256]{2,1,0:T(8,128)S(1)}, f32[3,30,256]{2,1,0:T(8,128)}, u32[]{:S(2)}) copy-start(f32[3,30,256]{2,1,0:T(8,128)} %param.13) | copy-start | bytes 276484
  132.8 4.9 %collective-permute-start.9 = (f32[30,1024]{1,0:T(8,128)S(1)}, f32[30,1024]{1,0:T(8,128)S(1)}, u32[]{:S(2)}, u32[]{:S(2)}) collective-permute-start(f32[30,1024]{1,0:T(8,128)S(1)} %pad_maximum_fusion.3), channel_id=1, source_target_pairs={{0,32},{32,0},{64,96},{96,64},{128,160},{160,128},{192,224},{224,1... | collective-permute-start | bytes 368648 | tf_op jit(solution)/shard_map/ppermute | solution.py:55
  137.7 8.3 %collective-permute-start.10 = (f32[30,1024]{1,0:T(8,128)S(1)}, f32[30,1024]{1,0:T(8,128)S(1)}, u32[]{:S(2)}, u32[]{:S(2)}) collective-permute-start(f32[30,1024]{1,0:T(8,128)S(1)} %fusion.23), channel_id=1, source_target_pairs={{0,64},{32,96},{64,0},{96,32},{128,192},{160,224},{192,128},{224,1... | collective-permute-start | bytes 368648 | tf_op jit(solution)/shard_map/ppermute | solution.py:55
  146.1 9.4 %collective-permute-start.11 = (f32[30,1024]{1,0:T(8,128)S(1)}, f32[30,1024]{1,0:T(8,128)S(1)}, u32[]{:S(2)}, u32[]{:S(2)}) collective-permute-start(f32[30,1024]{1,0:T(8,128)S(1)} %add.161), channel_id=1, source_target_pairs={{0,128},{32,160},{64,192},{96,224},{128,0},{160,32},{192,64},{224,... | collective-permute-start | bytes 368648 | tf_op jit(solution)/shard_map/ppermute | solution.py:55
  182.5 5.7 %copy-start.2 = (f32[30,1024]{1,0:T(8,128)S(1)}, f32[30,1024]{1,0:T(8,128)}, u32[]{:S(2)}) copy-start(f32[30,1024]{1,0:T(8,128)} %add.162) | copy-start | bytes 368644
Sparse Core Ops, SparseCore 0:
  68.0 58.2 all-gather.7
  129.5 51.4 all-gather.5
  183.5 50.3 all-gather.9

commit v10 on v8

--- a/solution.py
+++ b/solution.py
@@ -34,14 +34,19 @@
     squares = jnp.trace(gram, axis1=-2, axis2=-1)
     scale = 1.0 / (jnp.sqrt(squares) + norm_eps)
     gram_term = gram * (scale * scale)[..., None, None]
-    eye = jnp.broadcast_to(jnp.eye(gram.shape[-1], dtype=gram.dtype), gram.shape)
+    eye = jnp.eye(gram.shape[-1], dtype=gram.dtype)
+
+    def factor_of(gram_term):
+        return coef_a * eye + coef_b * gram_term + coef_c * matmul(gram_term, gram_term)
 
     def sweep(_, carry):
-        gram_term, total = carry
-        factor = coef_a * eye + coef_b * gram_term + coef_c * matmul(gram_term, gram_term)
-        return (matmul(factor, matmul(gram_term, factor)), matmul(total, factor))
+        gram_term, total, factor = carry
+        gram_term = matmul(factor, matmul(gram_term, factor))
+        factor = factor_of(gram_term)
+        return (gram_term, matmul(total, factor), factor)
 
-    _, total = lax.fori_loop(0, NS_STEPS, sweep, (gram_term, eye))
+    factor = factor_of(gram_term)
+    _, total, _ = lax.fori_loop(1, NS_STEPS, sweep, (gram_term, factor, factor))
     current = target * scale[..., None, None]
     return matmul(current, total)
 

time: 253 us -> 259 us (1.024)
  local copies, waits for them, and re-layouts: 13 us -> 19.1 us
    unnamed x24 -> x27, local copies, waits for them, and re-layouts: 3.3 us -> 7.39 us
    dot_general x13 -> x10, matrix products: 11.6 us -> 10.8 us  [matmul(): return jnp.einsum('...rs,...st->...rt', x, y, precision=matmul_precision)]
  transfers between devices with their start and end apart: 14 -> 14, of which waited for: 12 -> 12; matrix products, arithmetic and copies ran while one was open for 4% -> 3% of each run, Pallas kernels for 0% -> 0%
where the time goes in v10:
time: 259 us; the launch traced here: 258 us
  waiting for transfers between devices  157 us (61%)
  matrix products  36.2 us (14%)
  starting transfers between devices  23 us (9%)
  local copies, waits for them, and re-layouts  19.1 us (7%)
  between operations  14.4 us (6%)
  other arithmetic  8.01 us (3%)
    all_gather x1, waiting for transfers between devices, local(): gathered = lax.all_gather(pieces, WIDE, axis=0, tiled=True)  67.8 us
    all_gather x1, waiting for transfers between devices, local(): every = lax.all_gather(found, WIDE, axis=0)  44.8 us
    ppermute x9, waiting for transfers between devices, halving_step(): return (keep + lax.ppermute(send, axis, pairs), left)  32.4 us
    ppermute x9, starting transfers between devices, halving_step(): return (keep + lax.ppermute(send, axis, pairs), left)  12.6 us
    ppermute x3, waiting for transfers between devices, exchange_sum(): value = value + lax.ppermute(value, axis, pairs)  12.5 us
    dot_general x10, matrix products, matmul(): return jnp.einsum('...rs,...st->...rt', x, y, precision=matmul_precision)  10.8 us
    dot_general x1, matrix products, local(): every = jnp.einsum('tdr,tds->rs', every, every, precision=matmul_precision)  10.3 us
    ppermute x3, starting transfers between devices, exchange_sum(): value = value + lax.ppermute(value, axis, pairs)  10.2 us
  transfers between devices with their start and end apart: 14, of which 12 were waited for; matrix products, arithmetic and copies ran while one was open for 3% of the time, Pallas kernels for 0%

profile of v10, /device:TPU:1, one launch (start us, length us, event | category | flops | bytes accessed | tf_op | source)
XLA Modules:
  0.0 258.3 jit_solution(3337412341489411261)
XLA Ops:
  7.2 1.6 convolution_bitcast_fusion.3
  8.9 0.8 copy.76
  9.6 0.9 concatenate.19
  10.6 1.8 fusion.32
  12.4 2.0 copy-done.1
  14.4 1.8 fusion.8
  16.2 3.2 %collective-permute-start = (f32[2,2,2,2,8,4960]{5,4,3,2,1,0:T(8,128)}, f32[2,2,2,2,8,4960]{5,4,3,2,1,0:T(8,128)}, u32[]{:S(2)}, u32[]{:S(2)}) collective-permute-start(f32[2,2,2,2,8,4960]{5,4,3,2,1,0:T(8,128)} %fusion.8), channel_id=1, source_target_pairs={{0,1},{1,0},{2,3},{3,2},{4,5},{5,4},{6,7},{7,6},{8,9},{9,8},{10,11... | collective-permute-start | bytes 7618568 | tf_op jit(solution)/shard_map/ppermute | solution.py:93
  19.4 4.8 %collective-permute-done = f32[2,2,2,2,8,4960]{5,4,3,2,1,0:T(8,128)} collective-permute-done((f32[2,2,2,2,8,4960]{5,4,3,2,1,0:T(8,128)}, f32[2,2,2,2,8,4960]{5,4,3,2,1,0:T(8,128)}, u32[]{:S(2)}, u32[]{:S(2)}) %collective-permute-start) | collective-permute-done | bytes 2539552 | tf_op jit(solution)/shard_map/ppermute | solution.py:93
  24.2 2.7 %fusion.11 = f32[2,2,2,2,8,4960]{5,4,3,2,1,0:T(8,128)S(1)} fusion(f32[2,2,2,2,8,4960]{5,4,3,2,1,0:T(8,128)} %collective-permute-done, s32[]{:T(128)S(6)} %select_n.50, f32[2,2,2,2,2,8,4000]{6,5,4,3,2,1,0:T(8,128)} %bitcast.119, f32[2,2,2,2,2,8,960]{6,5,4,3,2,1,0:T(8,128)S(1)} %concatenate.19), kind=kLoop, calls=%fused_computation.18 | loop fusion | flops 1269760 | bytes 10158084 | tf_op jit(solution)/shard_map/add | solution.py:93
  27.4 0.9 dynamic-slice_bitcast_fusion
  28.3 0.9 collective-permute-start.1
  29.2 15.3 %collective-permute-done.5 = f32[2,2,2,8,2480]{4,3,2,1,0:T(8,128)} collective-permute-done((f32[2,2,2,8,2480]{4,3,2,1,0:T(8,128)}, f32[2,2,2,8,2480]{4,3,2,1,0:T(8,128)}, u32[]{:S(2)}, u32[]{:S(2)}) %collective-permute-start.5) | collective-permute-done | bytes 634912 | tf_op jit(solution)/shard_map/ppermute | solution.py:93
  44.5 1.2 bitcast_add_fusion
  45.7 1.3 collective-permute-start.6
  47.1 2.8 %collective-permute-start.2 = (f32[2,2,8,2480]{3,2,1,0:T(8,128)S(1)}, f32[2,2,8,2480]{3,2,1,0:T(8,128)S(1)}, u32[]{:S(2)}, u32[]{:S(2)}) collective-permute-start(f32[2,2,8,2480]{3,2,1,0:T(8,128)S(1)} %dynamic-slice_bitcast_fusion.3), channel_id=1, source_target_pairs={{0,4},{1,5},{2,6},{3,7},{4,0},{5,1},{6,2},{7,3},{8,12},{9,13},{10,... | collective-permute-start | bytes 952328 | tf_op jit(solution)/shard_map/ppermute | solution.py:93
  50.0 5.4 %collective-permute-done.6 = f32[2,2,8,2480]{3,2,1,0:T(8,128)S(1)} collective-permute-done((f32[2,2,8,2480]{3,2,1,0:T(8,128)S(1)}, f32[2,2,8,2480]{3,2,1,0:T(8,128)S(1)}, u32[]{:S(2)}, u32[]{:S(2)}) %collective-permute-start.6) | collective-permute-done | bytes 317472 | tf_op jit(solution)/shard_map/ppermute | solution.py:93
  55.5 1.0 collective-permute-done.2
  57.1 3.0 %collective-permute-done.7 = f32[2,8,2480]{2,1,0:T(8,128)S(1)} collective-permute-done((f32[2,8,2480]{2,1,0:T(8,128)S(1)}, f32[2,8,2480]{2,1,0:T(8,128)S(1)}, u32[]{:S(2)}, u32[]{:S(2)}) %collective-permute-start.7) | collective-permute-done | bytes 158752 | tf_op jit(solution)/shard_map/ppermute | solution.py:93
  60.1 2.3 collective-permute-start.8
  62.5 1.5 collective-permute-start.4
  63.9 1.0 collective-permute-done.8
  65.3 2.0 collective-permute-done.4
  67.4 0.8 add_divide_fusion
  68.2 0.8 concatenate.22
  69.3 67.8 %all-gather.5.cloned.1.call-done = f32[256,9920]{1,0:T(8,128)} async-done(((f32[8,9920]{1,0:T(8,128)}), f32[256,9920]{1,0:T(8,128)}) %all-gather.5.cloned.1.call-update) | async-done | bytes 10158096 | tf_op jit(solution)/shard_map/all_gather | solution.py:116
  137.0 1.9 fusion.28
  139.0 1.3 copy.80
  140.3 1.6 convolution_bitcast_fusion.5
  142.0 4.6 %fusion.13 = f32[30,256]{1,0:T(8,128)S(1)} fusion(f32[30,4000]{1,0:T(8,128)S(1)} %copy-done, f32[256,9920]{1,0:T(8,128)} %all-gather.5.cloned.1.call-done), kind=kOutput, calls=%fused_computation.25 | convolution fusion | flops 184320000 | bytes 4705024 | tf_op jit(solution)/shard_map/dv,rv->dr/dot_general | solution.py:124
  146.6 1.4 collective-permute-start.9
  148.0 3.5 %collective-permute-done.9 = f32[30,1024]{1,0:T(8,128)S(1)} collective-permute-done((f32[30,1024]{1,0:T(8,128)S(1)}, f32[30,1024]{1,0:T(8,128)S(1)}, u32[]{:S(2)}, u32[]{:S(2)}) %collective-permute-start.9) | collective-permute-done | bytes 122912 | tf_op jit(solution)/shard_map/ppermute | solution.py:60
  151.5 2.4 collective-permute-start.10
  153.9 5.9 %collective-permute-done.10 = f32[30,1024]{1,0:T(8,128)S(1)} collective-permute-done((f32[30,1024]{1,0:T(8,128)S(1)}, f32[30,1024]{1,0:T(8,128)S(1)}, u32[]{:S(2)}, u32[]{:S(2)}) %collective-permute-start.10) | collective-permute-done | bytes 122912 | tf_op jit(solution)/shard_map/ppermute | solution.py:60
  159.8 6.4 %collective-permute-start.11 = (f32[30,1024]{1,0:T(8,128)S(1)}, f32[30,1024]{1,0:T(8,128)S(1)}, u32[]{:S(2)}, u32[]{:S(2)}) collective-permute-start(f32[30,1024]{1,0:T(8,128)S(1)} %add.177), channel_id=1, source_target_pairs={{0,128},{32,160},{64,192},{96,224},{128,0},{160,32},{192,64},{224,... | collective-permute-start | bytes 368648 | tf_op jit(solution)/shard_map/ppermute | solution.py:60
  166.2 3.1 %collective-permute-done.11 = f32[30,1024]{1,0:T(8,128)S(1)} collective-permute-done((f32[30,1024]{1,0:T(8,128)S(1)}, f32[30,1024]{1,0:T(8,128)S(1)}, u32[]{:S(2)}, u32[]{:S(2)}) %collective-permute-start.11) | collective-permute-done | bytes 122912 | tf_op jit(solution)/shard_map/ppermute | solution.py:60
  171.7 1.2 convolution_bitcast_fusion.4
  172.8 4.2 %convolution_bitcast_fusion.1 = f32[30,4000]{1,0:T(8,128)} fusion(f32[30,256]{1,0:T(8,128)S(1)} %copy-done.5, f32[256,9920]{1,0:T(8,128)} %all-gather.5.cloned.1.call-done), kind=kOutput, calls=%fused_computation.10 | convolution fusion | flops 184320000 | bytes 4705024 | tf_op jit(solution)/shard_map/dot_general | solution.py:122
  177.1 44.8 %all-gather.7.cloned.1.call-done = f32[32,30,1024]{2,1,0:T(8,128)} async-done(((f32[1,30,1024]{2,1,0:T(8,128)}), f32[32,30,1024]{2,1,0:T(8,128)}) %all-gather.7.cloned.1.call-update) | async-done | bytes 3932176 | tf_op jit(solution)/shard_map/all_gather | solution.py:128
  221.9 10.3 %convolution_bitcast_fusion.2 = f32[1024,1024]{1,0:T(8,128)S(1)} fusion(f32[32,30,1024]{2,1,0:T(8,128)} %all-gather.7.cloned.1.call-done), kind=kOutput, calls=%fused_computation.19 | convolution fusion | flops 6039797760 | bytes 8126464 | tf_op jit(solution)/shard_map/tdr,tds->rs/dot_general | solution.py:129
  233.1 1.7 fusion.12
  234.8 2.5 copy.86
  237.3 1.2 copy.118
  238.6 9.8 %while.15 = (s32[]{:T(128)}, f32[4,256,256]{1,2,0:T(8,128)S(1)}, f32[4,256,256]{1,2,0:T(8,128)}, f32[4,256,256]{1,2,0:T(8,128)S(1)}, s32[]{:T(128)}) while((s32[]{:T(128)}, f32[4,256,256]{1,2,0:T(8,128)S(1)}, f32[4,256,256]{1,2,0:T(8,128)}, f32[4,256,256]{1,2,0:T(8,128)S(1)}, s32[]{:T(128)}) %tuple.42), condition=%wide.region_2.3_spmd.clone, body=%wide.region_1.2_spmd.clone.sunk | while | flops 1611792384 | bytes 15204413 | solution.py:49
  238.6 1.2 copy.130
  241.8 1.7 convolution_bitcast_fusion.7
  243.5 1.2 copy.130
  246.7 1.7 convolution_bitcast_fusion.7
  248.4 1.8 fusion.18
  (75 shorter events, 10.7 us)
Async XLA Ops:
  7.2 3.4 %copy-start = (f32[30,4000]{1,0:T(8,128)S(1)}, f32[30,4000]{1,0:T(8,128)}, u32[]{:S(2)}) copy-start(f32[30,4000]{1,0:T(8,128)} %param.10) | copy-start | bytes 1440004
  7.2 3.4 %copy-start.5 = (f32[30,256]{1,0:T(8,128)S(1)}, f32[30,256]{1,0:T(8,128)}, u32[]{:S(2)}) copy-start(f32[30,256]{1,0:T(8,128)} %param.12) | copy-start | bytes 92164
  7.2 129.9 %all-gather.5.cloned.1.call-start = ((), (), s32[]{:S(2)}) async-start(), calls=%async_computation | async-start | bytes 10543104 | tf_op jit(solution)/shard_map/all_gather | solution.py:116
  12.4 2.0 copy-start.1
  16.2 8.0 %collective-permute-start = (f32[2,2,2,2,8,4960]{5,4,3,2,1,0:T(8,128)}, f32[2,2,2,2,8,4960]{5,4,3,2,1,0:T(8,128)}, u32[]{:S(2)}, u32[]{:S(2)}) collective-permute-start(f32[2,2,2,2,8,4960]{5,4,3,2,1,0:T(8,128)} %fusion.8), channel_id=1, source_target_pairs={{0,1},{1,0},{2,3},{3,2},{4,5},{5,4},{6,7},{7,6},{8,9},{9,8},{10,11... | collective-permute-start | bytes 7618568 | tf_op jit(solution)/shard_map/ppermute | solution.py:93
  28.2 16.2 %collective-permute-start.5 = (f32[2,2,2,8,2480]{4,3,2,1,0:T(8,128)}, f32[2,2,2,8,2480]{4,3,2,1,0:T(8,128)}, u32[]{:S(2)}, u32[]{:S(2)}) collective-permute-start(f32[2,2,2,8,2480]{4,3,2,1,0:T(8,128)} %dynamic-slice_bitcast_fusion), channel_id=1, source_target_pairs={{0,8},{1,9},{2,10},{3,11},{4,12},{5,13},{6,14},{7,15},{8,0},{9,1},... | collective-permute-start | bytes 1904648 | tf_op jit(solution)/shard_map/ppermute | solution.py:93
  28.3 18.7 %collective-permute-start.1 = (f32[2,2,2,8,2480]{4,3,2,1,0:T(8,128)S(1)}, f32[2,2,2,8,2480]{4,3,2,1,0:T(8,128)S(1)}, u32[]{:S(2)}, u32[]{:S(2)}) collective-permute-start(f32[2,2,2,8,2480]{4,3,2,1,0:T(8,128)S(1)} %dynamic-slice_bitcast_fusion.1), channel_id=1, source_target_pairs={{0,2},{1,3},{2,0},{3,1},{4,6},{5,7},{6,4},{7,5},{8,10},{9,11},{10,... | collective-permute-start | bytes 1904648 | tf_op jit(solution)/shard_map/ppermute | solution.py:93
  45.6 19.5 %copy-start.8 = (f32[8,3,320]{2,0,1:T(8,128)S(1)}, f32[8,3,320]{2,0,1:T(8,128)}, u32[]{:S(2)}) copy-start(f32[8,3,320]{2,0,1:T(8,128)} %param.16) | copy-start | bytes 92164
  45.7 19.5 %copy-start.9 = (f32[8,3,320]{2,0,1:T(8,128)S(1)}, f32[8,3,320]{2,0,1:T(8,128)}, u32[]{:S(2)}) copy-start(f32[8,3,320]{2,0,1:T(8,128)} %param.17) | copy-start | bytes 92164
  45.7 21.7 %copy-start.6 = (f32[8,4000]{1,0:T(8,128)S(1)}, f32[8,4000]{1,0:T(8,128)}, u32[]{:S(2)}) copy-start(f32[8,4000]{1,0:T(8,128)} %param.14) | copy-start | bytes 384004
  45.7 21.7 %copy-start.7 = (f32[8,4000]{1,0:T(8,128)S(1)}, f32[8,4000]{1,0:T(8,128)}, u32[]{:S(2)}) copy-start(f32[8,4000]{1,0:T(8,128)} %param.15) | copy-start | bytes 384004
  45.7 9.6 %collective-permute-start.6 = (f32[2,2,8,2480]{3,2,1,0:T(8,128)S(1)}, f32[2,2,8,2480]{3,2,1,0:T(8,128)S(1)}, u32[]{:S(2)}, u32[]{:S(2)}) collective-permute-start(f32[2,2,8,2480]{3,2,1,0:T(8,128)S(1)} %dynamic-slice_bitcast_fusion.2), channel_id=1, source_target_pairs={{0,16},{1,17},{2,18},{3,19},{4,20},{5,21},{6,22},{7,23},{8,24},{9,... | collective-permute-start | bytes 952328 | tf_op jit(solution)/shard_map/ppermute | solution.py:93
  47.1 9.4 %collective-permute-start.2 = (f32[2,2,8,2480]{3,2,1,0:T(8,128)S(1)}, f32[2,2,8,2480]{3,2,1,0:T(8,128)S(1)}, u32[]{:S(2)}, u32[]{:S(2)}) collective-permute-start(f32[2,2,8,2480]{3,2,1,0:T(8,128)S(1)} %dynamic-slice_bitcast_fusion.3), channel_id=1, source_target_pairs={{0,4},{1,5},{2,6},{3,7},{4,0},{5,1},{6,2},{7,3},{8,12},{9,13},{10,... | collective-permute-start | bytes 952328 | tf_op jit(solution)/shard_map/ppermute | solution.py:93
  55.4 4.6 %collective-permute-start.7 = (f32[2,8,2480]{2,1,0:T(8,128)S(1)}, f32[2,8,2480]{2,1,0:T(8,128)S(1)}, u32[]{:S(2)}, u32[]{:S(2)}) collective-permute-start(f32[2,8,2480]{2,1,0:T(8,128)S(1)} %dynamic-slice_bitcast_fusion.4), channel_id=1, source_target_pairs={{0,2},{1,3},{2,0},{3,1},{4,6},{5,7},{6,4},{7,5},{8,10},{9,11},{10,... | collective-permute-start | bytes 476168 | tf_op jit(solution)/shard_map/ppermute | solution.py:93
  56.6 5.8 %collective-permute-start.3 = (f32[2,8,2480]{2,1,0:T(8,128)S(1)}, f32[2,8,2480]{2,1,0:T(8,128)S(1)}, u32[]{:S(2)}, u32[]{:S(2)}) collective-permute-start(f32[2,8,2480]{2,1,0:T(8,128)S(1)} %dynamic-slice_bitcast_fusion.5), channel_id=1, source_target_pairs={{0,8},{1,9},{2,10},{3,11},{4,12},{5,13},{6,14},{7,15},{8,0},{9,1},... | collective-permute-start | bytes 476168 | tf_op jit(solution)/shard_map/ppermute | solution.py:93
  60.1 4.9 %collective-permute-start.8 = (f32[8,2480]{1,0:T(8,128)S(1)}, f32[8,2480]{1,0:T(8,128)S(1)}, u32[]{:S(2)}, u32[]{:S(2)}) collective-permute-start(f32[8,2480]{1,0:T(8,128)S(1)} %dynamic-slice_bitcast_fusion.6), channel_id=1, source_target_pairs={{0,4},{1,5},{2,6},{3,7},{4,0},{5,1},{6,2},{7,3},{8,12},{9,13},{10,... | collective-permute-start | bytes 238088 | tf_op jit(solution)/shard_map/ppermute | solution.py:93
  62.5 4.9 %collective-permute-start.4 = (f32[8,2480]{1,0:T(8,128)S(1)}, f32[8,2480]{1,0:T(8,128)S(1)}, u32[]{:S(2)}, u32[]{:S(2)}) collective-permute-start(f32[8,2480]{1,0:T(8,128)S(1)} %dynamic-slice_bitcast_fusion.7), channel_id=1, source_target_pairs={{0,16},{1,17},{2,18},{3,19},{4,20},{5,21},{6,22},{7,23},{8,24},{9,... | collective-permute-start | bytes 238088 | tf_op jit(solution)/shard_map/ppermute | solution.py:93
  65.2 75.0 %copy-start.3 = (f32[3,30,320]{2,1,0:T(8,128)S(1)}, f32[3,30,320]{2,1,0:T(8,128)}, u32[]{:S(2)}) copy-start(f32[3,30,320]{2,1,0:T(8,128)} %param.11) | copy-start | bytes 345604
  69.0 152.8 %all-gather.7.cloned.1.call-start = ((), (), s32[]{:S(2)}) async-start(), calls=%async_computation.1 | async-start | bytes 4325376 | tf_op jit(solution)/shard_map/all_gather | solution.py:128
  142.0 29.7 %copy-start.4 = (f32[3,30,256]{2,1,0:T(8,128)S(1)}, f32[3,30,256]{2,1,0:T(8,128)}, u32[]{:S(2)}) copy-start(f32[3,30,256]{2,1,0:T(8,128)} %param.13) | copy-start | bytes 276484
  146.6 4.9 %collective-permute-start.9 = (f32[30,1024]{1,0:T(8,128)S(1)}, f32[30,1024]{1,0:T(8,128)S(1)}, u32[]{:S(2)}, u32[]{:S(2)}) collective-permute-start(f32[30,1024]{1,0:T(8,128)S(1)} %pad_maximum_fusion.2), channel_id=1, source_target_pairs={{0,32},{32,0},{64,96},{96,64},{128,160},{160,128},{192,224},{224,1... | collective-permute-start | bytes 368648 | tf_op jit(solution)/shard_map/ppermute | solution.py:60
  151.5 8.2 %collective-permute-start.10 = (f32[30,1024]{1,0:T(8,128)S(1)}, f32[30,1024]{1,0:T(8,128)S(1)}, u32[]{:S(2)}, u32[]{:S(2)}) collective-permute-start(f32[30,1024]{1,0:T(8,128)S(1)} %fusion.23), channel_id=1, source_target_pairs={{0,64},{32,96},{64,0},{96,32},{128,192},{160,224},{192,128},{224,1... | collective-permute-start | bytes 368648 | tf_op jit(solution)/shard_map/ppermute | solution.py:60
  159.8 9.5 %collective-permute-start.11 = (f32[30,1024]{1,0:T(8,128)S(1)}, f32[30,1024]{1,0:T(8,128)S(1)}, u32[]{:S(2)}, u32[]{:S(2)}) collective-permute-start(f32[30,1024]{1,0:T(8,128)S(1)} %add.177), channel_id=1, source_target_pairs={{0,128},{32,160},{64,192},{96,224},{128,0},{160,32},{192,64},{224,... | collective-permute-start | bytes 368648 | tf_op jit(solution)/shard_map/ppermute | solution.py:60
  170.1 7.0 %copy-start.2 = (f32[30,1024]{1,0:T(8,128)S(1)}, f32[30,1024]{1,0:T(8,128)}, u32[]{:S(2)}) copy-start(f32[30,1024]{1,0:T(8,128)} %add.178) | copy-start | bytes 368644
Sparse Core Ops, SparseCore 0:
  69.2 67.8 all-gather.4
  170.1 51.6 all-gather.6

commit v11 on v8

--- a/solution.py
+++ b/solution.py
@@ -34,14 +34,13 @@
     squares = jnp.trace(gram, axis1=-2, axis2=-1)
     scale = 1.0 / (jnp.sqrt(squares) + norm_eps)
     gram_term = gram * (scale * scale)[..., None, None]
-    eye = jnp.broadcast_to(jnp.eye(gram.shape[-1], dtype=gram.dtype), gram.shape)
-
-    def sweep(_, carry):
-        gram_term, total = carry
+    eye = jnp.eye(gram.shape[-1], dtype=gram.dtype)
+    total = None
+    for sweep_index in range(NS_STEPS):
         factor = coef_a * eye + coef_b * gram_term + coef_c * matmul(gram_term, gram_term)
-        return (matmul(factor, matmul(gram_term, factor)), matmul(total, factor))
-
-    _, total = lax.fori_loop(0, NS_STEPS, sweep, (gram_term, eye))
+        if sweep_index + 1 < NS_STEPS:
+            gram_term = matmul(factor, matmul(gram_term, factor))
+        total = factor if total is None else matmul(total, factor)
     current = target * scale[..., None, None]
     return matmul(current, total)
 

time: 253 us -> 248 us (0.980)
  matrix products: 37 us -> 32.5 us
    dot_general x13 -> x10, matrix products: 11.6 us -> 7.11 us  [matmul(): return jnp.einsum('...rs,...st->...rt', x, y, precision=matmul_precision)]
where the time goes in v11:
time: 248 us
  waiting for transfers between devices  157 us (63%)
  matrix products  32.5 us (13%)
  starting transfers between devices  23 us (9%)
  between operations  14.5 us (6%)
  local copies, waits for them, and re-layouts  12.6 us (5%)
  other arithmetic  7.79 us (3%)
    all_gather x1, waiting for transfers between devices, local(): gathered = lax.all_gather(pieces, WIDE, axis=0, tiled=True)  67.8 us
    all_gather x1, waiting for transfers between devices, local(): every = lax.all_gather(found, WIDE, axis=0)  44.8 us
    ppermute x9, waiting for transfers between devices, halving_step(): return (keep + lax.ppermute(send, axis, pairs), left)  32.4 us
    ppermute x9, starting transfers between devices, halving_step(): return (keep + lax.ppermute(send, axis, pairs), left)  12.6 us
    ppermute x3, waiting for transfers between devices, exchange_sum(): value = value + lax.ppermute(value, axis, pairs)  12.5 us
    dot_general x1, matrix products, local(): every = jnp.einsum('tdr,tds->rs', every, every, precision=matmul_precision)  10.4 us
    ppermute x3, starting transfers between devices, exchange_sum(): value = value + lax.ppermute(value, axis, pairs)  10.2 us
    dot_general x10, matrix products, matmul(): return jnp.einsum('...rs,...st->...rt', x, y, precision=matmul_precision)  7.11 us
  transfers between devices with their start and end apart: 14, of which 12 were waited for; matrix products, arithmetic and copies ran while one was open for 4% of the time, Pallas kernels for 0%

profile of v11, /device:TPU:1, one launch (start us, length us, event | category | flops | bytes accessed | tf_op | source)
XLA Modules:
  0.0 247.9 jit_solution(9102320212348652262)
XLA Ops:
  7.2 1.6 convolution_bitcast_fusion.2
  8.9 0.8 copy.42
  9.6 0.9 concatenate.19
  10.6 1.8 fusion.34
  12.4 2.0 copy-done.1
  14.4 1.8 fusion.4
  16.2 3.2 %collective-permute-start = (f32[2,2,2,2,8,4960]{5,4,3,2,1,0:T(8,128)}, f32[2,2,2,2,8,4960]{5,4,3,2,1,0:T(8,128)}, u32[]{:S(2)}, u32[]{:S(2)}) collective-permute-start(f32[2,2,2,2,8,4960]{5,4,3,2,1,0:T(8,128)} %fusion.4), channel_id=1, source_target_pairs={{0,1},{1,0},{2,3},{3,2},{4,5},{5,4},{6,7},{7,6},{8,9},{9,8},{10,11... | collective-permute-start | bytes 7618568 | tf_op jit(solution)/shard_map/ppermute | solution.py:87
  19.4 4.8 %collective-permute-done = f32[2,2,2,2,8,4960]{5,4,3,2,1,0:T(8,128)} collective-permute-done((f32[2,2,2,2,8,4960]{5,4,3,2,1,0:T(8,128)}, f32[2,2,2,2,8,4960]{5,4,3,2,1,0:T(8,128)}, u32[]{:S(2)}, u32[]{:S(2)}) %collective-permute-start) | collective-permute-done | bytes 2539552 | tf_op jit(solution)/shard_map/ppermute | solution.py:87
  24.2 2.7 %fusion.7 = f32[2,2,2,2,8,4960]{5,4,3,2,1,0:T(8,128)S(1)} fusion(f32[2,2,2,2,8,4960]{5,4,3,2,1,0:T(8,128)} %collective-permute-done, s32[]{:T(128)S(6)} %select_n.50, f32[2,2,2,2,2,8,4000]{6,5,4,3,2,1,0:T(8,128)} %bitcast.99, f32[2,2,2,2,2,8,960]{6,5,4,3,2,1,0:T(8,128)S(1)} %concatenate.19), kind=kLoop, calls=%fused_computation.12 | loop fusion | flops 1269760 | bytes 10158084 | tf_op jit(solution)/shard_map/add | solution.py:87
  27.4 0.9 dynamic-slice_bitcast_fusion
  28.3 0.9 collective-permute-start.1
  29.2 15.3 %collective-permute-done.5 = f32[2,2,2,8,2480]{4,3,2,1,0:T(8,128)} collective-permute-done((f32[2,2,2,8,2480]{4,3,2,1,0:T(8,128)}, f32[2,2,2,8,2480]{4,3,2,1,0:T(8,128)}, u32[]{:S(2)}, u32[]{:S(2)}) %collective-permute-start.5) | collective-permute-done | bytes 634912 | tf_op jit(solution)/shard_map/ppermute | solution.py:87
  44.5 1.2 bitcast_add_fusion
  45.7 1.3 collective-permute-start.6
  47.1 2.8 %collective-permute-start.2 = (f32[2,2,8,2480]{3,2,1,0:T(8,128)S(1)}, f32[2,2,8,2480]{3,2,1,0:T(8,128)S(1)}, u32[]{:S(2)}, u32[]{:S(2)}) collective-permute-start(f32[2,2,8,2480]{3,2,1,0:T(8,128)S(1)} %dynamic-slice_bitcast_fusion.3), channel_id=1, source_target_pairs={{0,4},{1,5},{2,6},{3,7},{4,0},{5,1},{6,2},{7,3},{8,12},{9,13},{10,... | collective-permute-start | bytes 952328 | tf_op jit(solution)/shard_map/ppermute | solution.py:87
  50.0 5.4 %collective-permute-done.6 = f32[2,2,8,2480]{3,2,1,0:T(8,128)S(1)} collective-permute-done((f32[2,2,8,2480]{3,2,1,0:T(8,128)S(1)}, f32[2,2,8,2480]{3,2,1,0:T(8,128)S(1)}, u32[]{:S(2)}, u32[]{:S(2)}) %collective-permute-start.6) | collective-permute-done | bytes 317472 | tf_op jit(solution)/shard_map/ppermute | solution.py:87
  55.5 1.0 collective-permute-done.2
  57.0 3.0 %collective-permute-done.7 = f32[2,8,2480]{2,1,0:T(8,128)S(1)} collective-permute-done((f32[2,8,2480]{2,1,0:T(8,128)S(1)}, f32[2,8,2480]{2,1,0:T(8,128)S(1)}, u32[]{:S(2)}, u32[]{:S(2)}) %collective-permute-start.7) | collective-permute-done | bytes 158752 | tf_op jit(solution)/shard_map/ppermute | solution.py:87
  60.1 2.3 collective-permute-start.8
  62.4 1.5 collective-permute-start.4
  63.9 1.0 collective-permute-done.8
  65.3 2.0 collective-permute-done.4
  67.4 0.8 add_divide_fusion
  68.2 0.8 concatenate.22
  69.3 67.8 %all-gather.5.cloned.1.call-done = f32[256,9920]{1,0:T(8,128)} async-done(((f32[8,9920]{1,0:T(8,128)}), f32[256,9920]{1,0:T(8,128)}) %all-gather.5.cloned.1.call-update) | async-done | bytes 10158096 | tf_op jit(solution)/shard_map/all_gather | solution.py:110
  137.0 2.0 fusion.32
  139.0 1.3 copy.46
  140.3 1.6 convolution_bitcast_fusion.4
  142.0 4.6 %fusion.11 = f32[30,256]{1,0:T(8,128)S(1)} fusion(f32[30,4000]{1,0:T(8,128)S(1)} %copy-done, f32[256,9920]{1,0:T(8,128)} %all-gather.5.cloned.1.call-done), kind=kOutput, calls=%fused_computation.23 | convolution fusion | flops 184320000 | bytes 4705024 | tf_op jit(solution)/shard_map/dv,rv->dr/dot_general | solution.py:118
  146.6 1.4 collective-permute-start.9
  148.0 3.5 %collective-permute-done.9 = f32[30,1024]{1,0:T(8,128)S(1)} collective-permute-done((f32[30,1024]{1,0:T(8,128)S(1)}, f32[30,1024]{1,0:T(8,128)S(1)}, u32[]{:S(2)}, u32[]{:S(2)}) %collective-permute-start.9) | collective-permute-done | bytes 122912 | tf_op jit(solution)/shard_map/ppermute | solution.py:54
  151.5 2.3 collective-permute-start.10
  153.9 5.9 %collective-permute-done.10 = f32[30,1024]{1,0:T(8,128)S(1)} collective-permute-done((f32[30,1024]{1,0:T(8,128)S(1)}, f32[30,1024]{1,0:T(8,128)S(1)}, u32[]{:S(2)}, u32[]{:S(2)}) %collective-permute-start.10) | collective-permute-done | bytes 122912 | tf_op jit(solution)/shard_map/ppermute | solution.py:54
  159.8 6.4 %collective-permute-start.11 = (f32[30,1024]{1,0:T(8,128)S(1)}, f32[30,1024]{1,0:T(8,128)S(1)}, u32[]{:S(2)}, u32[]{:S(2)}) collective-permute-start(f32[30,1024]{1,0:T(8,128)S(1)} %add.185), channel_id=1, source_target_pairs={{0,128},{32,160},{64,192},{96,224},{128,0},{160,32},{192,64},{224,... | collective-permute-start | bytes 368648 | tf_op jit(solution)/shard_map/ppermute | solution.py:54
  166.2 3.1 %collective-permute-done.11 = f32[30,1024]{1,0:T(8,128)S(1)} collective-permute-done((f32[30,1024]{1,0:T(8,128)S(1)}, f32[30,1024]{1,0:T(8,128)S(1)}, u32[]{:S(2)}, u32[]{:S(2)}) %collective-permute-start.11) | collective-permute-done | bytes 122912 | tf_op jit(solution)/shard_map/ppermute | solution.py:54
  169.3 0.7 add.186
  171.7 1.2 convolution_bitcast_fusion.3
  172.8 4.2 %convolution_bitcast_fusion = f32[30,4000]{1,0:T(8,128)} fusion(f32[30,256]{1,0:T(8,128)S(1)} %copy-done.5, f32[256,9920]{1,0:T(8,128)} %all-gather.5.cloned.1.call-done), kind=kOutput, calls=%fused_computation.4 | convolution fusion | flops 184320000 | bytes 4705024 | tf_op jit(solution)/shard_map/dot_general | solution.py:116
  177.1 44.8 %all-gather.7.cloned.1.call-done = f32[32,30,1024]{2,1,0:T(8,128)} async-done(((f32[1,30,1024]{2,1,0:T(8,128)}), f32[32,30,1024]{2,1,0:T(8,128)}) %all-gather.7.cloned.1.call-update) | async-done | bytes 3932176 | tf_op jit(solution)/shard_map/all_gather | solution.py:122
  221.9 10.4 %convolution_bitcast_fusion.1 = f32[1024,1024]{1,0:T(8,128)S(1)} fusion(f32[32,30,1024]{2,1,0:T(8,128)} %all-gather.7.cloned.1.call-done), kind=kOutput, calls=%fused_computation.13 | convolution fusion | flops 6039797760 | bytes 8126464 | tf_op jit(solution)/shard_map/tdr,tds->rs/dot_general | solution.py:123
  232.6 0.9 fusion.10
  233.5 0.7 fusion.15
  234.9 0.8 fusion.9
  235.7 0.7 fusion.37
  236.4 0.7 fusion.36
  237.1 0.7 fusion.38
  237.8 0.8 fusion.8
  238.6 0.7 fusion.39
  (66 shorter events, 6.6 us)
Async XLA Ops:
  7.2 3.4 %copy-start = (f32[30,4000]{1,0:T(8,128)S(1)}, f32[30,4000]{1,0:T(8,128)}, u32[]{:S(2)}) copy-start(f32[30,4000]{1,0:T(8,128)} %param.8) | copy-start | bytes 1440004
  7.2 3.4 %copy-start.5 = (f32[30,256]{1,0:T(8,128)S(1)}, f32[30,256]{1,0:T(8,128)}, u32[]{:S(2)}) copy-start(f32[30,256]{1,0:T(8,128)} %param.10) | copy-start | bytes 92164
  7.2 129.8 %all-gather.5.cloned.1.call-start = ((), (), s32[]{:S(2)}) async-start(), calls=%async_computation | async-start | bytes 10543104 | tf_op jit(solution)/shard_map/all_gather | solution.py:110
  12.4 2.0 copy-start.1
  16.2 8.0 %collective-permute-start = (f32[2,2,2,2,8,4960]{5,4,3,2,1,0:T(8,128)}, f32[2,2,2,2,8,4960]{5,4,3,2,1,0:T(8,128)}, u32[]{:S(2)}, u32[]{:S(2)}) collective-permute-start(f32[2,2,2,2,8,4960]{5,4,3,2,1,0:T(8,128)} %fusion.4), channel_id=1, source_target_pairs={{0,1},{1,0},{2,3},{3,2},{4,5},{5,4},{6,7},{7,6},{8,9},{9,8},{10,11... | collective-permute-start | bytes 7618568 | tf_op jit(solution)/shard_map/ppermute | solution.py:87
  28.2 16.2 %collective-permute-start.5 = (f32[2,2,2,8,2480]{4,3,2,1,0:T(8,128)}, f32[2,2,2,8,2480]{4,3,2,1,0:T(8,128)}, u32[]{:S(2)}, u32[]{:S(2)}) collective-permute-start(f32[2,2,2,8,2480]{4,3,2,1,0:T(8,128)} %dynamic-slice_bitcast_fusion), channel_id=1, source_target_pairs={{0,8},{1,9},{2,10},{3,11},{4,12},{5,13},{6,14},{7,15},{8,0},{9,1},... | collective-permute-start | bytes 1904648 | tf_op jit(solution)/shard_map/ppermute | solution.py:87
  28.3 18.7 %collective-permute-start.1 = (f32[2,2,2,8,2480]{4,3,2,1,0:T(8,128)S(1)}, f32[2,2,2,8,2480]{4,3,2,1,0:T(8,128)S(1)}, u32[]{:S(2)}, u32[]{:S(2)}) collective-permute-start(f32[2,2,2,8,2480]{4,3,2,1,0:T(8,128)S(1)} %dynamic-slice_bitcast_fusion.1), channel_id=1, source_target_pairs={{0,2},{1,3},{2,0},{3,1},{4,6},{5,7},{6,4},{7,5},{8,10},{9,11},{10,... | collective-permute-start | bytes 1904648 | tf_op jit(solution)/shard_map/ppermute | solution.py:87
  45.6 19.5 %copy-start.8 = (f32[8,3,320]{2,0,1:T(8,128)S(1)}, f32[8,3,320]{2,0,1:T(8,128)}, u32[]{:S(2)}) copy-start(f32[8,3,320]{2,0,1:T(8,128)} %param.14) | copy-start | bytes 92164
  45.7 19.5 %copy-start.9 = (f32[8,3,320]{2,0,1:T(8,128)S(1)}, f32[8,3,320]{2,0,1:T(8,128)}, u32[]{:S(2)}) copy-start(f32[8,3,320]{2,0,1:T(8,128)} %param.15) | copy-start | bytes 92164
  45.7 21.7 %copy-start.6 = (f32[8,4000]{1,0:T(8,128)S(1)}, f32[8,4000]{1,0:T(8,128)}, u32[]{:S(2)}) copy-start(f32[8,4000]{1,0:T(8,128)} %param.12) | copy-start | bytes 384004
  45.7 21.7 %copy-start.7 = (f32[8,4000]{1,0:T(8,128)S(1)}, f32[8,4000]{1,0:T(8,128)}, u32[]{:S(2)}) copy-start(f32[8,4000]{1,0:T(8,128)} %param.13) | copy-start | bytes 384004
  45.7 9.6 %collective-permute-start.6 = (f32[2,2,8,2480]{3,2,1,0:T(8,128)S(1)}, f32[2,2,8,2480]{3,2,1,0:T(8,128)S(1)}, u32[]{:S(2)}, u32[]{:S(2)}) collective-permute-start(f32[2,2,8,2480]{3,2,1,0:T(8,128)S(1)} %dynamic-slice_bitcast_fusion.2), channel_id=1, source_target_pairs={{0,16},{1,17},{2,18},{3,19},{4,20},{5,21},{6,22},{7,23},{8,24},{9,... | collective-permute-start | bytes 952328 | tf_op jit(solution)/shard_map/ppermute | solution.py:87
  47.1 9.4 %collective-permute-start.2 = (f32[2,2,8,2480]{3,2,1,0:T(8,128)S(1)}, f32[2,2,8,2480]{3,2,1,0:T(8,128)S(1)}, u32[]{:S(2)}, u32[]{:S(2)}) collective-permute-start(f32[2,2,8,2480]{3,2,1,0:T(8,128)S(1)} %dynamic-slice_bitcast_fusion.3), channel_id=1, source_target_pairs={{0,4},{1,5},{2,6},{3,7},{4,0},{5,1},{6,2},{7,3},{8,12},{9,13},{10,... | collective-permute-start | bytes 952328 | tf_op jit(solution)/shard_map/ppermute | solution.py:87
  55.4 4.6 %collective-permute-start.7 = (f32[2,8,2480]{2,1,0:T(8,128)S(1)}, f32[2,8,2480]{2,1,0:T(8,128)S(1)}, u32[]{:S(2)}, u32[]{:S(2)}) collective-permute-start(f32[2,8,2480]{2,1,0:T(8,128)S(1)} %dynamic-slice_bitcast_fusion.4), channel_id=1, source_target_pairs={{0,2},{1,3},{2,0},{3,1},{4,6},{5,7},{6,4},{7,5},{8,10},{9,11},{10,... | collective-permute-start | bytes 476168 | tf_op jit(solution)/shard_map/ppermute | solution.py:87
  56.6 5.8 %collective-permute-start.3 = (f32[2,8,2480]{2,1,0:T(8,128)S(1)}, f32[2,8,2480]{2,1,0:T(8,128)S(1)}, u32[]{:S(2)}, u32[]{:S(2)}) collective-permute-start(f32[2,8,2480]{2,1,0:T(8,128)S(1)} %dynamic-slice_bitcast_fusion.5), channel_id=1, source_target_pairs={{0,8},{1,9},{2,10},{3,11},{4,12},{5,13},{6,14},{7,15},{8,0},{9,1},... | collective-permute-start | bytes 476168 | tf_op jit(solution)/shard_map/ppermute | solution.py:87
  60.1 4.9 %collective-permute-start.8 = (f32[8,2480]{1,0:T(8,128)S(1)}, f32[8,2480]{1,0:T(8,128)S(1)}, u32[]{:S(2)}, u32[]{:S(2)}) collective-permute-start(f32[8,2480]{1,0:T(8,128)S(1)} %dynamic-slice_bitcast_fusion.6), channel_id=1, source_target_pairs={{0,4},{1,5},{2,6},{3,7},{4,0},{5,1},{6,2},{7,3},{8,12},{9,13},{10,... | collective-permute-start | bytes 238088 | tf_op jit(solution)/shard_map/ppermute | solution.py:87
  62.4 4.9 %collective-permute-start.4 = (f32[8,2480]{1,0:T(8,128)S(1)}, f32[8,2480]{1,0:T(8,128)S(1)}, u32[]{:S(2)}, u32[]{:S(2)}) collective-permute-start(f32[8,2480]{1,0:T(8,128)S(1)} %dynamic-slice_bitcast_fusion.7), channel_id=1, source_target_pairs={{0,16},{1,17},{2,18},{3,19},{4,20},{5,21},{6,22},{7,23},{8,24},{9,... | collective-permute-start | bytes 238088 | tf_op jit(solution)/shard_map/ppermute | solution.py:87
  65.2 75.1 %copy-start.3 = (f32[3,30,320]{2,1,0:T(8,128)S(1)}, f32[3,30,320]{2,1,0:T(8,128)}, u32[]{:S(2)}) copy-start(f32[3,30,320]{2,1,0:T(8,128)} %param.9) | copy-start | bytes 345604
  69.0 152.8 %all-gather.7.cloned.1.call-start = ((), (), s32[]{:S(2)}) async-start(), calls=%async_computation.1 | async-start | bytes 4325376 | tf_op jit(solution)/shard_map/all_gather | solution.py:122
  142.0 29.7 %copy-start.4 = (f32[3,30,256]{2,1,0:T(8,128)S(1)}, f32[3,30,256]{2,1,0:T(8,128)}, u32[]{:S(2)}) copy-start(f32[3,30,256]{2,1,0:T(8,128)} %param.11) | copy-start | bytes 276484
  146.6 4.9 %collective-permute-start.9 = (f32[30,1024]{1,0:T(8,128)S(1)}, f32[30,1024]{1,0:T(8,128)S(1)}, u32[]{:S(2)}, u32[]{:S(2)}) collective-permute-start(f32[30,1024]{1,0:T(8,128)S(1)} %pad_maximum_fusion.4), channel_id=1, source_target_pairs={{0,32},{32,0},{64,96},{96,64},{128,160},{160,128},{192,224},{224,1... | collective-permute-start | bytes 368648 | tf_op jit(solution)/shard_map/ppermute | solution.py:54
  151.5 8.2 %collective-permute-start.10 = (f32[30,1024]{1,0:T(8,128)S(1)}, f32[30,1024]{1,0:T(8,128)S(1)}, u32[]{:S(2)}, u32[]{:S(2)}) collective-permute-start(f32[30,1024]{1,0:T(8,128)S(1)} %fusion.27), channel_id=1, source_target_pairs={{0,64},{32,96},{64,0},{96,32},{128,192},{160,224},{192,128},{224,1... | collective-permute-start | bytes 368648 | tf_op jit(solution)/shard_map/ppermute | solution.py:54
  159.8 9.5 %collective-permute-start.11 = (f32[30,1024]{1,0:T(8,128)S(1)}, f32[30,1024]{1,0:T(8,128)S(1)}, u32[]{:S(2)}, u32[]{:S(2)}) collective-permute-start(f32[30,1024]{1,0:T(8,128)S(1)} %add.185), channel_id=1, source_target_pairs={{0,128},{32,160},{64,192},{96,224},{128,0},{160,32},{192,64},{224,... | collective-permute-start | bytes 368648 | tf_op jit(solution)/shard_map/ppermute | solution.py:54
  170.0 7.0 %copy-start.2 = (f32[30,1024]{1,0:T(8,128)S(1)}, f32[30,1024]{1,0:T(8,128)}, u32[]{:S(2)}) copy-start(f32[30,1024]{1,0:T(8,128)} %add.186) | copy-start | bytes 368644
Sparse Core Ops, SparseCore 0:
  69.1 67.8 all-gather.4
  170.1 51.6 all-gather.6
